TPU v7x, 256 devices: a whole 4x4x8 slice. The times are simulated.
256 devices in a mesh: ctx: 32 (over x, z), head: 8 (over y, core).
Axes of the slice: x: 4, y: 4, z: 8, core: 2. Of those that a mesh axis runs over, the one named last changes fastest.
Arguments:
- features: bfloat16 [8192, 16384], P('ctx', 'head'), may hold values from -6 to 6
- log_decay: float32 [256, 8192], P('head', 'ctx'), may hold values from -2 to 0, as said below
- step_size: float32 [256, 8192], P('head', 'ctx'), may hold values from 0.0002 to 0.002
- b_matrix: bfloat16 [8192, 2048], P('ctx', 'head'), may hold values from -6 to 6
- c_matrix: bfloat16 [8192, 2048], P('ctx', 'head'), may hold values from -6 to 6
- skip_gain: float32 [256], P('head'), may hold values from 0.5 to 1.5
Outputs:
- mixed: bfloat16 [8192, 16384], P('ctx', 'head')
Inputs may be any that keep to these rules, and one draw needn't show every extreme that they name: `log_decay`: every entry is negative.
All inputs are finite; a program needn't handle non-finite values.
Results may differ from a plain program's by a relative error of at most 0.0013.
Values sent between devices are 32-bit elements; how exact they have to be, the bound alone decides.
No kernel may reach another device: no remote copies, remote signals or barrier semaphores. Data moves between devices by JAX's collectives and lax.ppermute only.
A program may use at most 320 MiB of HBM per device.

v0:
```python
import jax
import jax.numpy as jnp
from jax import lax
from jax.sharding import PartitionSpec as P

N = 256
SPAN = 128


def carried_in(x, axis, combine, identity, reverse):
    length, place = (lax.axis_size(axis), lax.axis_index(axis))
    everything = jax.tree.map(lambda part: lax.all_gather(part, axis), x)
    start = jax.tree.map(
        lambda part, zero: jnp.broadcast_to(jnp.asarray(zero, part.dtype), part.shape), x, identity
    )

    def step(k, before):
        at = length - 1 - k if reverse else k
        reached = at > place if reverse else at < place
        new = combine(before, jax.tree.map(lambda part: part[at], everything))
        return jax.tree.map(lambda a, b: jnp.where(reached, a, b), new, before)

    return lax.fori_loop(0, length, step, start)


def from_root(block, axis, source):
    block = jnp.where(lax.axis_index(axis) == source, block, jnp.zeros_like(block))
    return lax.psum(block, axis)


def chain(earlier, later_pair):
    return (
        earlier[0] + later_pair[0],
        jnp.exp(later_pair[0])[:, None, None] * earlier[1] + later_pair[1],
    )


def on_device(features, log_decay, step_size, b_matrix, c_matrix, skip_gain):
    head_count = log_decay.shape[0]
    tok_rows = features.shape[0]
    head_width = features.shape[1] // head_count
    state_size = N
    group_count = b_matrix.shape[1] // state_size
    per_group = head_count // group_count
    span_count = tok_rows // SPAN
    half_count = span_count // 2
    cumulative = jnp.cumsum(log_decay.reshape(head_count, span_count, SPAN), axis=2)
    step_rows = step_size.reshape(head_count, span_count, SPAN)
    inputs = features.reshape(span_count, SPAN, head_count, head_width)
    grouped_inputs = features.reshape(span_count, SPAN, group_count, per_group, head_width)
    b_spans = b_matrix.reshape(span_count, SPAN, group_count, state_size)
    c_spans = c_matrix.reshape(span_count, SPAN, group_count, state_size)
    scores = jnp.einsum("ktgn,ksgn->gkts", c_spans, b_spans, preferred_element_type=jnp.float32)
    causal = jnp.arange(SPAN)[:, None] >= jnp.arange(SPAN)[None, :]
    cum_grouped = cumulative.reshape(group_count, per_group, span_count, SPAN)
    step_grouped = step_rows.reshape(group_count, per_group, span_count, SPAN)
    decay_gaps = jnp.where(causal, cum_grouped[..., :, None] - cum_grouped[..., None, :], -jnp.inf)
    weights = (scores[:, None] * jnp.exp(decay_gaps) * step_grouped[:, :, :, None, :]).astype(
        jnp.bfloat16
    )
    diagonal_part = jnp.einsum(
        "gqkts,ksgqp->ktgqp", weights, grouped_inputs, preferred_element_type=jnp.float32
    )
    diagonal_part = diagonal_part.reshape(span_count, SPAN, head_count, head_width)
    span_ends = cumulative[:, :, -1]
    coeffs = jnp.exp(span_ends[:, :, None] - cumulative) * step_rows
    weighted = (inputs * jnp.transpose(coeffs, (1, 2, 0))[:, :, :, None]).astype(jnp.bfloat16)
    weighted = weighted.reshape(span_count, SPAN, group_count, per_group, head_width)
    span_states = jnp.einsum(
        "ksgn,ksgqp->kgqpn", b_spans, weighted, preferred_element_type=jnp.float32
    )
    span_states = span_states.reshape(span_count, head_count, head_width, state_size)
    totals = jnp.transpose(span_ends).reshape(2, half_count, head_count)
    grouped = span_states.reshape(2, half_count, head_count, head_width, state_size)

    def advance(running, element):
        return (jnp.exp(element[0])[:, :, None, None] * running + element[1], running)

    start = jnp.zeros((2, head_count, head_width, state_size), jnp.float32)
    block_states, prefix = lax.scan(
        advance, start, (jnp.swapaxes(totals, 0, 1), jnp.swapaxes(grouped, 0, 1))
    )
    shifted = jnp.concatenate([jnp.zeros((2, 1, head_count), jnp.float32), totals[:, :-1]], axis=1)
    before = jnp.cumsum(shifted, axis=1)
    block_decay = jnp.sum(totals, axis=1)
    front_pair = (block_decay[0], block_states[0])
    back_pair = (block_decay[1], block_states[1])
    neutral = (
        jnp.zeros((head_count,), jnp.float32),
        jnp.zeros((head_count, head_width, state_size), jnp.float32),
    )
    enter_front = carried_in(front_pair, "ctx", chain, neutral, False)
    through_front = chain(enter_front, front_pair)[1]
    middle = from_root(through_front, "ctx", lax.axis_size("ctx") - 1)
    behind = carried_in(back_pair, "ctx", chain, neutral, True)
    enter_back = jnp.exp(behind[0])[:, None, None] * middle + behind[1]
    entering = jnp.stack([enter_front[1], enter_back])
    span_enter = jnp.exp(before)[:, :, :, None, None] * entering[:, None] + jnp.swapaxes(
        prefix, 0, 1
    )
    state_bf = span_enter.astype(jnp.bfloat16)
    state_part = jnp.einsum(
        "ktgn,kgqpn->ktgqp", c_spans, state_bf, preferred_element_type=jnp.float32
    )
    state_part = state_part.reshape(span_count, SPAN, head_count, head_width)
    state_part = state_part * jnp.transpose(jnp.exp(cumulative), (1, 2, 0))[:, :, :, None]
    output_rows = (
        diagonal_part + state_part + skip_gain[None, None, :, None] * inputs.astype(jnp.float32)
    )
    return output_rows.reshape(tok_rows, head_count * head_width).astype(jnp.bfloat16)


def solution(mesh):
    placed = (
        P("ctx", "head"),
        P("head", "ctx"),
        P("head", "ctx"),
        P("ctx", "head"),
        P("ctx", "head"),
        P("head"),
    )
    return jax.shard_map(
        on_device, mesh=mesh, in_specs=placed, out_specs=P("ctx", "head"), check_vma=False
    )
```

profile of v0, /device:TPU:8, one launch (start us, length us, event | category | flops | bytes accessed | tf_op | source)
XLA Modules:
  0.0 1049.9 jit_solution(3869095595849692370)
XLA Ops:
  12.6 2.5 fusion.26
  17.0 3.6 fusion.20
  20.6 3.0 copy.27
  23.7 43.5 %all-gather = f32[32,1,32]{2,1,0:T(1,128)S(1)} all-gather(f32[1,1,32]{2,1,0:T(1,128)S(1)} %get-tuple-element.343), channel_id=1, replica_groups=mesh['ctx'=32,'head'=8] {'ctx'}, dimensions={0}, use_global_device_ids=true | all-gather | bytes 4224 | tf_op jit(solution)/shard_map/all_gather | solution.py:12
  67.2 38.4 %all-gather.1 = f32[32,1,32]{2,1,0:T(1,128)S(1)} all-gather(f32[1,1,32]{2,1,0:T(1,128)S(1)} %get-tuple-element.342), channel_id=1, replica_groups=mesh['ctx'=32,'head'=8] {'ctx'}, dimensions={0}, use_global_device_ids=true | all-gather | bytes 4224 | tf_op jit(solution)/shard_map/all_gather | solution.py:12
  105.6 344.3 %all-gather.5.cloned.1.call-done = f32[32,32,64,256]{3,2,1,0:T(8,128)} async-done(((f32[1,32,64,256]{3,2,1,0:T(8,128)}), f32[32,32,64,256]{3,2,1,0:T(8,128)}) %all-gather.5.cloned.1.call-update) | async-done | bytes 67108880 | tf_op jit(solution)/shard_map/all_gather | solution.py:12
  449.9 127.7 %while.37 = (s32[]{:T(128)}, f32[32,64,256]{2,1,0:T(8,128)}, s32[]{:T(128)}, f32[32,32]{1,0:T(8,128)S(1)}, f32[32,32,64,256]{3,2,1,0:T(8,128)}, /*index=5*/s32[]{:T(128)}, s32[]{:T(128)}) while((s32[]{:T(128)}, f32[32,64,256]{2,1,0:T(8,128)}, s32[]{:T(128)}, f32[32,32]{1,0:T(8,128)S(1)}, f32[32,32,64,256]{3,2,1,0:T(8,128)}, ...), condition=%wide.region_2.3_spmd.clone, body=%wide.region_1.2_spmd.clone.sunk | while | flops 2097156 | bytes 6291945 | solution.py:23
  449.9 3.2 fusion.37
  453.2 3.9 fusion.37
  457.1 3.9 fusion.37
  461.0 4.6 fusion.37
  465.6 4.3 fusion.37
  469.9 3.9 fusion.37
  473.8 3.9 fusion.37
  477.8 4.0 fusion.37
  481.7 3.9 fusion.37
  485.7 3.9 fusion.37
  489.6 3.9 fusion.37
  493.5 3.9 fusion.37
  497.4 4.0 fusion.37
  501.4 3.9 fusion.37
  505.4 3.9 fusion.37
  509.3 3.9 fusion.37
  513.2 3.9 fusion.37
  517.1 4.0 fusion.37
  521.1 3.9 fusion.37
  525.0 3.9 fusion.37
  528.9 3.9 fusion.37
  532.9 3.9 fusion.37
  536.7 3.9 fusion.37
  540.7 3.9 fusion.37
  544.6 3.9 fusion.37
  548.5 3.9 fusion.37
  552.4 3.9 fusion.37
  556.2 4.1 fusion.37
  560.3 5.1 fusion.37
  565.5 4.3 fusion.37
  569.8 3.9 fusion.37
  573.6 4.0 fusion.37
  577.6 4.9 convert_bitcast_fusion
  582.5 298.2 %all-gather.7.cloned.1.call-done = f32[32,32,64,256]{3,2,1,0:T(8,128)} async-done(((f32[1,32,64,256]{3,2,1,0:T(8,128)}), f32[32,32,64,256]{3,2,1,0:T(8,128)}) %all-gather.7.cloned.1.call-update) | async-done | bytes 67108880 | tf_op jit(solution)/shard_map/all_gather | solution.py:12
  880.7 69.6 %while.38 = (s32[]{:T(128)}, f32[32]{0:T(128)S(1)}, f32[32,64,256]{2,1,0:T(8,128)S(1)}, s32[]{:T(128)}, f32[32,32]{1,0:T(8,128)S(1)}, /*index=5*/f32[32,32,64,25...) while((s32[]{:T(128)}, f32[32]{0:T(128)S(1)}, f32[32,64,256]{2,1,0:T(8,128)S(1)}, ...), condition=%wide.region_4.5_spmd.clone, body=%wide.region_3.4_spmd.clone.sunk | while | flops 2097256 | bytes 6292273 | solution.py:23
  882.9 2.1 fusion.38
  885.0 2.1 fusion.38
  887.2 2.1 fusion.38
  889.3 2.1 fusion.38
  891.5 2.3 fusion.38
  893.8 2.1 fusion.38
  896.0 2.1 fusion.38
  898.1 2.1 fusion.38
  902.5 2.1 fusion.38
  906.8 2.1 fusion.38
  909.0 2.1 fusion.38
  911.2 2.1 fusion.38
  913.4 2.1 fusion.38
  915.6 2.1 fusion.38
  917.7 2.2 fusion.38
  922.1 2.1 fusion.38
  930.8 2.1 fusion.38
  937.3 2.1 fusion.38
  941.6 2.1 fusion.38
  943.8 2.1 fusion.38
  948.1 2.1 fusion.38
  950.3 85.2 %all-reduce.2.cloned.1.call-done = f32[32,64,256]{2,1,0:T(8,128)} async-done(((f32[32,64,256]{2,1,0:T(8,128)}), f32[32,64,256]{2,1,0:T(8,128)}) %all-reduce.2.cloned.1.call-update) | async-done | bytes 2097168 | tf_op jit(solution)/shard_map/psum | solution.py:28
  (124 shorter events, 39.9 us)
Async XLA Ops:
  6.5 5.3 copy-start
  6.5 443.4 %all-gather.5.cloned.1.call-start = ((), (), s32[]{:S(2)}) async-start(), calls=%async_computation | async-start | bytes 69206016 | tf_op jit(solution)/shard_map/all_gather | solution.py:12
  10.8 1.8 copy-start.3
  12.6 3.3 copy-start.1
  15.8 0.9 copy-start.6
  15.8 0.9 copy-start.5
  15.9 864.8 %all-gather.7.cloned.1.call-start = ((), (), s32[]{:S(2)}) async-start(), calls=%async_computation.1 | async-start | bytes 69206016 | tf_op jit(solution)/shard_map/all_gather | solution.py:12
  16.6 1018.8 %all-reduce.2.cloned.1.call-start = ((), (), s32[]{:S(2)}) async-start(), calls=%async_computation.2 | async-start | bytes 4194304 | tf_op jit(solution)/shard_map/psum | solution.py:28
  20.6 3.0 copy-start.7
  1035.5 2.0 copy-start.4
  1039.8 1.6 copy-start.2
Sparse Core Ops, SparseCore 0:
  16.0 433.8 all-gather.4
  452.5 428.1 all-gather.6
  884.2 151.2 all-reduce.1
where the time goes:
time: 1050 us
  waiting for transfers between devices  728 us (69%)
  other arithmetic  206 us (20%)
  blocking collectives  81.9 us (8%)
  local copies, waits for them, and re-layouts  14.1 us (1%)
  between operations  13.3 us (1%)
    all_gather x2, waiting for transfers between devices, carried_in(): everything = jax.tree.map(lambda part: lax.all_gather(part, axis), x)  642 us
    select_n x64, other arithmetic, step(): return jax.tree.map(lambda a, b: jnp.where(reached, a, b), new, before)  195 us
    psum x1, waiting for transfers between devices, from_root(): return lax.psum(block, axis)  85.2 us
    all_gather x2, blocking collectives, carried_in(): everything = jax.tree.map(lambda part: lax.all_gather(part, axis), x)  81.9 us
  transfers between devices with their start and end apart: 3, of which 3 were waited for; matrix products, arithmetic and copies ran while one was open for 20% of the time, Pallas kernels for 0%

commit v1 on v0

v1 whole, which is shorter than its diff:
```python
import jax
import jax.numpy as jnp
import numpy as np
from jax import lax
from jax.sharding import PartitionSpec as P

N = 256
SPAN = 128


def chain_mixing(chain_decay, devices, halves):
    links = halves * devices
    q = np.arange(links)
    between = (q[None, None, :] > q[None, :, None]) & (q[None, None, :] < q[:, None, None])
    gap = jnp.sum(jnp.where(between[None], chain_decay[:, None, None, :], 0.0), axis=-1)
    lower = q[:, None] > q[None, :]
    mixing = jnp.where(lower[None], jnp.exp(gap), 0.0)
    place = np.stack([np.arange(devices), links - 1 - np.arange(devices)], axis=1)
    return mixing[:, place[:, :, None, None], place[None, None, :, :]]


def on_device(features, log_decay, step_size, b_matrix, c_matrix, skip_gain):
    head_count = log_decay.shape[0]
    tok_rows = features.shape[0]
    head_width = features.shape[1] // head_count
    state_size = N
    group_count = b_matrix.shape[1] // state_size
    per_group = head_count // group_count
    halves = tok_rows // SPAN
    assert halves == 2
    devices = lax.axis_size("ctx")
    per_chunk = head_count // devices
    flat = head_width * state_size

    cumulative = jnp.cumsum(log_decay.reshape(head_count, halves, SPAN), axis=2)
    totals = cumulative[:, :, -1]
    got_totals = lax.all_to_all(totals, "ctx", 0, 0, tiled=True)

    step_rows = step_size.reshape(head_count, halves, SPAN)
    grouped_inputs = features.reshape(halves, SPAN, group_count, per_group, head_width)
    b_spans = b_matrix.reshape(halves, SPAN, group_count, state_size)
    c_spans = c_matrix.reshape(halves, SPAN, group_count, state_size)

    coeffs = jnp.exp(totals[:, :, None] - cumulative) * step_rows
    coeffs = jnp.transpose(coeffs.reshape(group_count, per_group, halves, SPAN), (2, 3, 0, 1))
    weighted = (grouped_inputs * coeffs[..., None]).astype(jnp.bfloat16)
    span_states = jnp.einsum(
        "ksgn,ksgqp->gqkpn", b_spans, weighted, preferred_element_type=jnp.float32
    ).reshape(head_count, halves, flat)

    got = lax.all_to_all(span_states, "ctx", 0, 0, tiled=True)
    got = got.reshape(devices, per_chunk, halves, flat)

    chain_decay = got_totals.reshape(devices, per_chunk, halves)
    chain_decay = jnp.concatenate(
        [jnp.transpose(chain_decay[:, :, 0]), jnp.transpose(chain_decay[::-1, :, 1])], axis=1
    )
    mixing = chain_mixing(chain_decay, devices, halves)
    j = np.arange(devices)
    own = np.zeros((devices, halves, devices, halves), bool)
    own[j, 1, j, 0] = True
    own_gain = jnp.sum(jnp.where(own[None], mixing, 0.0), axis=(2, 3, 4))
    solved = jnp.einsum(
        "cjkJL,JcLf->jckf", jnp.where(own[None], 0.0, mixing), got,
        precision=lax.Precision.HIGHEST, preferred_element_type=jnp.float32,
    ).reshape(devices * per_chunk, halves, flat)
    back = lax.all_to_all(solved, "ctx", 0, 0, tiled=True)
    gain = lax.all_to_all(jnp.transpose(own_gain), "ctx", 0, 0, tiled=True).reshape(head_count)
    entering = jnp.stack(
        [back[:, 0], back[:, 1] + gain[:, None] * span_states[:, 0]], axis=1
    )
    state_bf = entering.astype(jnp.bfloat16).reshape(
        group_count, per_group, halves, head_width, state_size
    )

    scores = jnp.einsum("ktgn,ksgn->gkts", c_spans, b_spans, preferred_element_type=jnp.float32)
    causal = jnp.arange(SPAN)[:, None] >= jnp.arange(SPAN)[None, :]
    cum_grouped = cumulative.reshape(group_count, per_group, halves, SPAN)
    step_grouped = step_rows.reshape(group_count, per_group, halves, SPAN)
    decay_gaps = jnp.where(causal, cum_grouped[..., :, None] - cum_grouped[..., None, :], -jnp.inf)
    weights = (scores[:, None] * jnp.exp(decay_gaps) * step_grouped[:, :, :, None, :]).astype(
        jnp.bfloat16
    )
    diagonal_part = jnp.einsum(
        "gqkts,ksgqp->ktgqp", weights, grouped_inputs, preferred_element_type=jnp.float32
    )
    state_part = jnp.einsum(
        "ktgn,gqkpn->ktgqp", c_spans, state_bf, preferred_element_type=jnp.float32
    )
    decay_in = jnp.transpose(jnp.exp(cum_grouped), (2, 3, 0, 1))[..., None]
    skip = skip_gain.reshape(group_count, per_group)[None, None, :, :, None]
    output_rows = (
        diagonal_part + state_part * decay_in + skip * grouped_inputs.astype(jnp.float32)
    )
    return output_rows.reshape(tok_rows, head_count * head_width).astype(jnp.bfloat16)


def solution(mesh):
    placed = (
        P("ctx", "head"),
        P("head", "ctx"),
        P("head", "ctx"),
        P("ctx", "head"),
        P("ctx", "head"),
        P("head"),
    )
    return jax.shard_map(
        on_device, mesh=mesh, in_specs=placed, out_specs=P("ctx", "head"), check_vma=False
    )
```

time: 1050 us -> 289 us (0.28)
  waiting for transfers between devices: 728 us -> 150 us
  other arithmetic: 206 us -> 19.4 us
  blocking collectives: 81.9 us -> 0 us
  local copies, waits for them, and re-layouts: 14.1 us -> 67.1 us
  starting transfers between devices: 0.08 us -> 36.6 us
  between operations: 13.3 us -> 0.35 us
    all_gather x2 -> x0, waiting for transfers between devices: 642 us -> none  [carried_in(): everything = jax.tree.map(lambda part: lax.all_gather(part, axis), x)]
    select_n x64 -> x2, other arithmetic: 195 us -> 0.02 us  [the longest x1 0.01 us: chain_mixing(): mixing = jnp.where(lower[None], jnp.exp(gap), 0.0)]
    all_to_all x0 -> x4, waiting for transfers between devices: none -> 150 us  [the longest x1 85.4 us: on_device(): back = lax.all_to_all(solved, 'ctx', 0, 0, tiled=True)]
    psum x1 -> x0, waiting for transfers between devices: 85.2 us -> none  [from_root(): return lax.psum(block, axis)]
    all_gather x2 -> x0, blocking collectives: 81.9 us -> none  [carried_in(): everything = jax.tree.map(lambda part: lax.all_gather(part, axis), x)]
    all_to_all x0 -> x4, starting transfers between devices: none -> 36.6 us  [the longest x1 11.3 us: on_device(): got_totals = lax.all_to_all(totals, 'ctx', 0, 0, tiled=True)]
    gather x0 -> x1, local copies, waits for them, and re-layouts: none -> 26.7 us  [chain_mixing(): return mixing[:, place[:, :, None, None], place[None, None, :, :]]]
    reshape x1 -> x5, local copies, waits for them, and re-layouts: 0.8 us -> 19.1 us  [the longest x2 12.3 us: on_device(): span_states = jnp.einsum('ksgn,ksgqp->gqkpn', b_spans, weighted, preferre...]
  transfers between devices with their start and end apart: 3 -> 4, of which waited for: 3 -> 2; matrix products, arithmetic and copies ran while one was open for 20% -> 26% of each run, Pallas kernels for 0% -> 0%
where the time goes in v1:
time: 289 us; the launch traced here: 288 us
  waiting for transfers between devices  150 us (52%)
  local copies, waits for them, and re-layouts  67.1 us (23%)
  starting transfers between devices  36.6 us (13%)
  other arithmetic  19.4 us (7%)
  matrix products  15.4 us (5%)
    all_to_all x1, waiting for transfers between devices, on_device(): back = lax.all_to_all(solved, 'ctx', 0, 0, tiled=True)  85.4 us
    all_to_all x1, waiting for transfers between devices, on_device(): got = lax.all_to_all(span_states, 'ctx', 0, 0, tiled=True)  64.2 us
    gather x1, local copies, waits for them, and re-layouts, chain_mixing(): return mixing[:, place[:, :, None, None], place[None, None, :, :]]  26.7 us
    slice x1, other arithmetic, on_device(): back[:, 0]  15.6 us
    reshape x2, local copies, waits for them, and re-layouts, on_device(): span_states = jnp.einsum('ksgn,ksgqp->gqkpn', b_spans, weighted, preferre...  12.3 us
    all_to_all x1, starting transfers between devices, on_device(): got_totals = lax.all_to_all(totals, 'ctx', 0, 0, tiled=True)  11.3 us
    all_to_all x1, starting transfers between devices, on_device(): back = lax.all_to_all(solved, 'ctx', 0, 0, tiled=True)  10.1 us
    all_to_all x1, starting transfers between devices, on_device(): got = lax.all_to_all(span_states, 'ctx', 0, 0, tiled=True)  10.1 us
  transfers between devices with their start and end apart: 4, of which 2 were waited for; matrix products, arithmetic and copies ran while one was open for 26% of the time, Pallas kernels for 0%

profile of v1, /device:TPU:8, one launch (start us, length us, event | category | flops | bytes accessed | tf_op | source)
XLA Modules:
  0.0 288.3 jit_solution(11145454750974745485)
XLA Ops:
  0.0 0.0 copy-start
  0.0 0.8 copy_bitcast_fusion.1
  0.8 0.6 reduce_window_sum.13
  1.4 0.2 slice_reduce_fusion.1
  1.5 0.9 copy.88
  2.5 11.3 %all-to-all-start.1 = ((f32[32,1,2]{2,1,0:T(1,128)}), f32[32,1,2]{2,1,0:T(1,128)S(1)}, u32[]{:S(2)}, u32[]{:S(2)}) async-start(f32[32,1,2]{2,1,0:T(1,128)} %bitcast.13), calls=%async_computation.1 | async-start | bytes 32768 | tf_op jit(solution)/shard_map/all_to_all | solution.py:37
  13.8 0.8 reshape.179
  14.6 0.6 fusion.25
  15.2 0.0 copy-done.7
  15.2 1.5 copy.69
  16.7 0.3 reshape.178
  17.0 0.0 copy-start.2
  17.0 1.1 multiply_convert_fusion.2
  18.1 0.0 copy-done
  18.1 2.6 convolution_bitcast_fusion.1
  20.7 0.0 copy-done.2
  20.7 5.0 %reshape.180 = f32[32,2,16384]{2,0,1:T(8,128)} reshape(f32[1,32,2,64,256]{4,3,1,2,0:T(8,128)} %convolution_bitcast_fusion.1) | data formatting | bytes 8388608 | tf_op jit(solution)/shard_map/reshape | solution.py:49
  25.7 7.4 %copy.74 = f32[32,2,16384]{2,1,0:T(2,128)} copy(f32[32,2,16384]{2,0,1:T(8,128)} %reshape.180) | data formatting | bytes 8388608 | tf_op jit(solution)/shard_map/reshape | solution.py:49
  33.1 0.0 all-to-all-done.1
  33.1 10.1 %all-to-all-start = ((f32[32,2,16384]{2,1,0:T(2,128)}), f32[32,2,16384]{2,1,0:T(2,128)}, u32[]{:S(2)}, u32[]{:S(2)}) async-start(f32[32,2,16384]{2,1,0:T(2,128)} %copy.74), calls=%async_computation | async-start | bytes 8388608 | tf_op jit(solution)/shard_map/all_to_all | solution.py:51
  43.1 0.0 copy-done.11
  43.1 0.0 copy-done.12
  43.1 0.0 copy-start.6
  43.2 0.0 copy-start.13
  43.2 0.1 broadcast_or_fusion
  43.3 0.5 reshape.189
  43.8 0.3 slice_reduce_fusion
  44.1 0.3 reverse_reduce_fusion
  44.4 0.1 maximum_bitcast_fusion
  44.5 0.0 copy-done.6
  44.5 0.6 select_reduce_fusion
  45.1 0.0 copy-done.13
  45.1 0.0 copy-start.14
  45.2 26.7 %gather_fusion = f32[4096]{0:T(1024)S(1)} fusion(f32[64,64]{1,0:T(8,128)S(1)} %exponential_select_fusion, s32[4096]{0:T(1024)S(1)} %reshape.189), kind=kCustom, calls=%fused_computation | custom fusion | bytes 65536 | tf_op jit(solution)/shard_map/gather | solution.py:19
  71.9 0.0 copy-done.14
  71.9 1.0 reshape.205
  72.9 0.5 copy.77
  73.4 1.0 reshape.208
  74.4 0.3 reduce_sum.19
  74.7 0.7 copy.79
  75.4 64.2 %all-to-all-done = f32[32,2,16384]{2,1,0:T(2,128)} async-done(((f32[32,2,16384]{2,1,0:T(2,128)}), f32[32,2,16384]{2,1,0:T(2,128)}, u32[]{:S(2)}, u32[]{:S(2)}) %all-to-all-start) | async-done | bytes 4194336 | tf_op jit(solution)/shard_map/all_to_all | solution.py:51
  139.6 5.1 %all-to-all-start.3 = ((f32[32,1,1]{2,1,0:T(1,128)}), f32[32,1,1]{2,1,0:T(1,128)S(1)}, u32[]{:S(2)}, u32[]{:S(2)}) async-start(f32[32,1,1]{2,1,0:T(1,128)} %copy.79), calls=%async_computation.3 | async-start | bytes 32768 | tf_op jit(solution)/shard_map/all_to_all | solution.py:68
  144.7 8.5 %convolution_bitcast_fusion = f32[32,2,16384]{2,0,1:T(8,128)S(1)} fusion(f32[32,2,32,2]{2,0,3,1:T(8,128)S(1)} %copy.77, f32[32,2,16384]{2,1,0:T(2,128)} %all-to-all-done), kind=kOutput, calls=%fused_computation.1 | convolution fusion | flops 805306368 | bytes 8404992 | tf_op jit(solution)/shard_map/cjkJL,JcLf->jckf/dot_general | solution.py:63
  153.2 5.2 %copy.78 = f32[32,2,16384]{2,1,0:T(2,128)} copy(f32[32,2,16384]{2,0,1:T(8,128)S(1)} %convolution_bitcast_fusion) | data formatting | bytes 8388608 | tf_op jit(solution)/shard_map/reshape | solution.py:66
  158.4 0.0 all-to-all-done.3
  158.4 10.1 %all-to-all-start.2 = ((f32[32,2,16384]{2,1,0:T(2,128)}), f32[32,2,16384]{2,1,0:T(2,128)}, u32[]{:S(2)}, u32[]{:S(2)}) async-start(f32[32,2,16384]{2,1,0:T(2,128)} %copy.78), calls=%async_computation.2 | async-start | bytes 8388608 | tf_op jit(solution)/shard_map/all_to_all | solution.py:67
  168.5 0.0 copy-done.1
  168.5 3.2 %reshape.213 = f32[2,128,1,32,64]{4,3,1,0,2:T(8,128)} reshape(bf16[256,2048]{1,0:T(8,128)(2,1)S(1)} %copy-done.1) | data formatting | bytes 3145728 | tf_op jit(solution)/shard_map/convert_element_type | solution.py:46
  171.8 3.9 %copy.82 = f32[2,128,1,32,64]{1,4,3,0,2:T(8,128)S(1)} copy(f32[2,128,1,32,64]{4,3,1,0,2:T(8,128)} %reshape.213) | data formatting | bytes 4194304 | tf_op jit(solution)/shard_map/convert_element_type | solution.py:46
  175.7 0.2 fusion.28
  175.9 3.3 %fusion.2 = f32[2,32,128,64]{2,3,1,0:T(8,128)} fusion(f32[32,2,128]{2,0,1:T(8,128)S(1)} %copy_bitcast_fusion, f32[32,2,128]{2,0,1:T(8,128)S(1)} %copy-done.8, f32[2,128,128]{2,1,0:T(8,128)S(1)} %fusion.28, pred[128,128]{1,0:T(8,128)(4,1)S(1)} %iota_compare_fusion, bf16[2,128,32,64]{1,0,3,2:T(2,128)(2,1)S(1)} %copy-done.3), kind=kOutput, calls=%fused_computation.6 | convolution fusion | flops 139460608 | bytes 3358720 | tf_op jit(solution)/shard_map/gqkts,ksgqp->ktgqp/dot_general | solution.py:84
  179.2 0.3 reduce.7
  179.6 85.4 %all-to-all-done.2 = f32[32,2,16384]{2,1,0:T(2,128)} async-done(((f32[32,2,16384]{2,1,0:T(2,128)}), f32[32,2,16384]{2,1,0:T(2,128)}, u32[]{:S(2)}, u32[]{:S(2)}) %all-to-all-start.2) | async-done | bytes 4194336 | tf_op jit(solution)/shard_map/all_to_all | solution.py:67
  264.9 15.6 %fusion.4 = (bf16[32,16384]{1,0:T(8,128)(2,1)S(1)}, bf16[32,16384]{1,0:T(8,128)(2,1)S(1)}) fusion(f32[32,2,16384]{2,1,0:T(2,128)} %all-to-all-done.2, f32[32,2,16384]{2,1,0:T(2,128)} %copy.74, f32[32]{0:T(128)S(1)} %reduce.7), kind=kLoop, calls=%fused_computation.10 | loop fusion | flops 2097152 | bytes 8388736 | tf_op jit(solution)/shard_map/slice | solution.py:70
  280.6 0.0 copy-start.4
  280.6 0.0 copy-start.9
  280.6 0.0 copy-start.15
  280.6 0.2 copy.95
  280.8 0.2 copy.96
  281.1 1.1 copy-done.4
  282.2 0.0 copy-done.15
  282.2 0.8 fusion.11
  282.9 3.0 %copy.91 = bf16[2,128,1,32,64]{4,3,1,0,2:T(8,128)(2,1)S(1)} copy(bf16[2,128,1,32,64]{1,4,3,0,2:T(8,128)(2,1)S(1)} %fusion.11) | data formatting | bytes 2097152 | tf_op jit(solution)/shard_map/convert_element_type | solution.py:95
  285.9 2.4 reshape.214
  (18 shorter events, 0.1 us)
Async XLA Ops:
  0.0 18.1 %copy-start = (bf16[256,256]{1,0:T(8,128)(2,1)S(1)}, bf16[256,256]{1,0:T(8,128)(2,1)}, u32[]{:S(2)}) copy-start(bf16[256,256]{1,0:T(8,128)(2,1)} %param.17) | copy-start | bytes 393220
  1.4 13.8 %copy-start.7 = (f32[32,2,128]{2,0,1:T(8,128)}, f32[32,2,128]{2,0,1:T(8,128)S(1)}, u32[]{:S(2)}) copy-start(f32[32,2,128]{2,0,1:T(8,128)S(1)} %reduce_window_sum.13) | copy-start | bytes 98308
  2.5 30.6 %all-to-all-start.1 = ((f32[32,1,2]{2,1,0:T(1,128)}), f32[32,1,2]{2,1,0:T(1,128)S(1)}, u32[]{:S(2)}, u32[]{:S(2)}) async-start(f32[32,1,2]{2,1,0:T(1,128)} %bitcast.13), calls=%async_computation.1 | async-start | bytes 32768 | tf_op jit(solution)/shard_map/all_to_all | solution.py:37
  17.0 3.7 %copy-start.2 = (bf16[2,128,32,64]{1,0,3,2:T(2,128)(2,1)}, bf16[2,128,32,64]{1,0,3,2:T(2,128)(2,1)S(1)}, u32[]{:S(2)}) copy-start(bf16[2,128,32,64]{1,0,3,2:T(2,128)(2,1)S(1)} %reshape.178) | copy-start | bytes 3145732
  33.1 10.1 %copy-start.11 = (s32[32,2]{1,0:T(8,128)S(1)}, s32[32,2]{1,0:T(8,128)}, u32[]{:S(2)}) copy-start(s32[32,2]{1,0:T(8,128)} %constant.48) | copy-start | bytes 772
  33.1 10.1 %copy-start.12 = (s32[32,2]{1,0:T(8,128)S(1)}, s32[32,2]{1,0:T(8,128)}, u32[]{:S(2)}) copy-start(s32[32,2]{1,0:T(8,128)} %constant.50) | copy-start | bytes 772
  33.1 106.6 %all-to-all-start = ((f32[32,2,16384]{2,1,0:T(2,128)}), f32[32,2,16384]{2,1,0:T(2,128)}, u32[]{:S(2)}, u32[]{:S(2)}) async-start(f32[32,2,16384]{2,1,0:T(2,128)} %copy.74), calls=%async_computation | async-start | bytes 8388608 | tf_op jit(solution)/shard_map/all_to_all | solution.py:51
  43.1 1.4 copy-start.6
  43.2 2.0 copy-start.13
  45.1 26.7 %copy-start.14 = (pred[4096]{0:T(1024)(128)(4,1)S(1)}, pred[4096]{0:T(1024)(128)(4,1)}, u32[]{:S(2)}) copy-start(pred[4096]{0:T(1024)(128)(4,1)} %constant.52) | copy-start | bytes 12292
  139.6 18.8 %all-to-all-start.3 = ((f32[32,1,1]{2,1,0:T(1,128)}), f32[32,1,1]{2,1,0:T(1,128)S(1)}, u32[]{:S(2)}, u32[]{:S(2)}) async-start(f32[32,1,1]{2,1,0:T(1,128)} %copy.79), calls=%async_computation.3 | async-start | bytes 32768 | tf_op jit(solution)/shard_map/all_to_all | solution.py:68
  158.4 10.1 %copy-start.1 = (bf16[256,2048]{1,0:T(8,128)(2,1)S(1)}, bf16[256,2048]{1,0:T(8,128)(2,1)}, u32[]{:S(2)}) copy-start(bf16[256,2048]{1,0:T(8,128)(2,1)} %param.14) | copy-start | bytes 3145732
  158.4 106.5 %all-to-all-start.2 = ((f32[32,2,16384]{2,1,0:T(2,128)}), f32[32,2,16384]{2,1,0:T(2,128)}, u32[]{:S(2)}, u32[]{:S(2)}) async-start(f32[32,2,16384]{2,1,0:T(2,128)} %copy.78), calls=%async_computation.2 | async-start | bytes 8388608 | tf_op jit(solution)/shard_map/all_to_all | solution.py:67
  171.8 3.9 %copy-start.10 = (f32[32,256]{1,0:T(8,128)S(1)}, f32[32,256]{1,0:T(8,128)}, u32[]{:S(2)}) copy-start(f32[32,256]{1,0:T(8,128)} %param.16) | copy-start | bytes 98308
  171.8 3.9 %copy-start.5 = (bf16[256,256]{1,0:T(8,128)(2,1)S(1)}, bf16[256,256]{1,0:T(8,128)(2,1)}, u32[]{:S(2)}) copy-start(bf16[256,256]{1,0:T(8,128)(2,1)} %param.18) | copy-start | bytes 393220
  171.8 4.1 %copy-start.3 = (bf16[2,128,32,64]{1,0,3,2:T(2,128)(2,1)S(1)}, bf16[2,128,32,64]{1,0,3,2:T(2,128)(2,1)}, u32[]{:S(2)}) copy-start(bf16[2,128,32,64]{1,0,3,2:T(2,128)(2,1)} %copy-done.2) | copy-start | bytes 3145732
  171.8 4.1 %copy-start.8 = (f32[32,2,128]{2,0,1:T(8,128)S(1)}, f32[32,2,128]{2,0,1:T(8,128)}, u32[]{:S(2)}) copy-start(f32[32,2,128]{2,0,1:T(8,128)} %copy-done.7) | copy-start | bytes 98308
  280.6 1.6 copy-start.4
  280.6 1.6 copy-start.9
  280.6 1.6 copy-start.15

commit v2 on v1

--- a/solution.py
+++ b/solution.py
@@ -8,15 +8,14 @@
 SPAN = 128
 
 
-def chain_mixing(chain_decay, devices, halves):
-    links = halves * devices
-    q = np.arange(links)
-    between = (q[None, None, :] > q[None, :, None]) & (q[None, None, :] < q[:, None, None])
-    gap = jnp.sum(jnp.where(between[None], chain_decay[:, None, None, :], 0.0), axis=-1)
-    lower = q[:, None] > q[None, :]
+def chain_mixing(decay, devices, halves):
+    j = np.arange(devices)
+    pos = np.stack([j, halves * devices - 1 - j], axis=1).reshape(-1)
+    between = (pos[None, :, None] < pos[None, None, :]) & (pos[None, None, :] < pos[:, None, None])
+    gap = jnp.sum(jnp.where(between[None], decay[:, None, None, :], 0.0), axis=-1)
+    lower = pos[None, :] < pos[:, None]
     mixing = jnp.where(lower[None], jnp.exp(gap), 0.0)
-    place = np.stack([np.arange(devices), links - 1 - np.arange(devices)], axis=1)
-    return mixing[:, place[:, :, None, None], place[None, None, :, :]]
+    return mixing.reshape(-1, devices, halves, devices, halves)
 
 
 def on_device(features, log_decay, step_size, b_matrix, c_matrix, skip_gain):
@@ -32,9 +31,10 @@
     per_chunk = head_count // devices
     flat = head_width * state_size
 
+    rows = halves * head_width
+    extra = 8
     cumulative = jnp.cumsum(log_decay.reshape(head_count, halves, SPAN), axis=2)
     totals = cumulative[:, :, -1]
-    got_totals = lax.all_to_all(totals, "ctx", 0, 0, tiled=True)
 
     step_rows = step_size.reshape(head_count, halves, SPAN)
     grouped_inputs = features.reshape(halves, SPAN, group_count, per_group, head_width)
@@ -46,28 +46,41 @@
     weighted = (grouped_inputs * coeffs[..., None]).astype(jnp.bfloat16)
     span_states = jnp.einsum(
         "ksgn,ksgqp->gqkpn", b_spans, weighted, preferred_element_type=jnp.float32
-    ).reshape(head_count, halves, flat)
+    ).reshape(head_count, rows, state_size)
+    tail = jnp.concatenate(
+        [totals, jnp.zeros((head_count, extra - halves), jnp.float32)], axis=1
+    )
+    payload = jnp.concatenate(
+        [span_states, jnp.broadcast_to(tail[:, :, None], (head_count, extra, state_size))], axis=1
+    )
+    got = lax.all_to_all(payload, "ctx", 0, 0, tiled=True)
+    got_states = got[:, :rows].reshape(devices, per_chunk, halves, head_width, state_size)
+    got_decay = got[:, rows:rows + halves, 0].reshape(devices, per_chunk, halves)
 
-    got = lax.all_to_all(span_states, "ctx", 0, 0, tiled=True)
-    got = got.reshape(devices, per_chunk, halves, flat)
-
-    chain_decay = got_totals.reshape(devices, per_chunk, halves)
-    chain_decay = jnp.concatenate(
-        [jnp.transpose(chain_decay[:, :, 0]), jnp.transpose(chain_decay[::-1, :, 1])], axis=1
+    mixing = chain_mixing(
+        jnp.transpose(got_decay, (1, 0, 2)).reshape(per_chunk, devices * halves), devices, halves
     )
-    mixing = chain_mixing(chain_decay, devices, halves)
     j = np.arange(devices)
     own = np.zeros((devices, halves, devices, halves), bool)
     own[j, 1, j, 0] = True
-    own_gain = jnp.sum(jnp.where(own[None], mixing, 0.0), axis=(2, 3, 4))
+    own_gain = jnp.sum(jnp.where(own[None], mixing, 0.0), axis=(3, 4))[:, :, 1]
     solved = jnp.einsum(
-        "cjkJL,JcLf->jckf", jnp.where(own[None], 0.0, mixing), got,
+        "cjkJL,JcLpn->jckpn", jnp.where(own[None], 0.0, mixing), got_states,
         precision=lax.Precision.HIGHEST, preferred_element_type=jnp.float32,
-    ).reshape(devices * per_chunk, halves, flat)
-    back = lax.all_to_all(solved, "ctx", 0, 0, tiled=True)
-    gain = lax.all_to_all(jnp.transpose(own_gain), "ctx", 0, 0, tiled=True).reshape(head_count)
-    entering = jnp.stack(
-        [back[:, 0], back[:, 1] + gain[:, None] * span_states[:, 0]], axis=1
+    ).reshape(devices * per_chunk, rows, state_size)
+    gain_rows = jnp.broadcast_to(
+        jnp.transpose(own_gain).reshape(devices * per_chunk, 1, 1),
+        (devices * per_chunk, extra, state_size),
+    )
+    back = lax.all_to_all(jnp.concatenate([solved, gain_rows], axis=1), "ctx", 0, 0, tiled=True)
+    half_rows = head_width
+    gain = back[:, rows:rows + 1, :1]
+    entering = jnp.concatenate(
+        [
+            back[:, :half_rows],
+            back[:, half_rows:rows] + gain * span_states[:, :half_rows],
+        ],
+        axis=1,
     )
     state_bf = entering.astype(jnp.bfloat16).reshape(
         group_count, per_group, halves, head_width, state_size

time: 289 us -> 265 us (0.917)
  blocking collectives: 0 us -> 114 us
  waiting for transfers between devices: 150 us -> 91.3 us
  local copies, waits for them, and re-layouts: 67.1 us -> 31.9 us
  starting transfers between devices: 36.6 us -> 5.2 us
  other arithmetic: 19.4 us -> 10.5 us
  matrix products: 15.4 us -> 11.5 us
    all_to_all x0 -> x1, blocking collectives: none -> 114 us  [on_device(): got = lax.all_to_all(payload, 'ctx', 0, 0, tiled=True)]
    all_to_all x4 -> x1, waiting for transfers between devices: 150 us -> 91.3 us  [on_device(): lax.all_to_all(jnp.concatenate([solved, gain_rows], axis=1), 'ctx', 0, 0,...]
    all_to_all x4 -> x1, starting transfers between devices: 36.6 us -> 5.2 us  [on_device(): lax.all_to_all(jnp.concatenate([solved, gain_rows], axis=1), 'ctx', 0, 0,...]
    gather x1 -> x0, local copies, waits for them, and re-layouts: 26.7 us -> none  [chain_mixing(): return mixing[:, place[:, :, None, None], place[None, None, :, :]]]
    reshape x3 -> x0, local copies, waits for them, and re-layouts: 17.5 us -> none  [the longest x2 12.3 us: on_device(): span_states = jnp.einsum('ksgn,ksgqp->gqkpn', b_spans, weighted, preferre...]
    slice x1 -> x0, other arithmetic: 15.6 us -> none  [on_device(): back[:, 0]]
    concatenate x1 -> x3, other arithmetic: 0.13 us -> 5.36 us  [the longest x1 4.72 us: on_device(): jnp.concatenate([solved, gain_rows], axis=1)]
    slice x1 -> x6, local copies, waits for them, and re-layouts: 0.32 us -> 5.44 us  [the longest x2 2.2 us: on_device(): got[:, :rows].reshape(devices, per_chunk, halves, head_width, state_size)]
  transfers between devices with their start and end apart: 4 -> 1, of which waited for: 2 -> 1; matrix products, arithmetic and copies ran while one was open for 26% -> 4% of each run, Pallas kernels for 0% -> 0%
where the time goes in v2:
time: 265 us; the launch traced here: 264 us
  blocking collectives  114 us (43%)
  waiting for transfers between devices  91.3 us (34%)
  local copies, waits for them, and re-layouts  31.9 us (12%)
  matrix products  11.5 us (4%)
  other arithmetic  10.5 us (4%)
  starting transfers between devices  5.2 us (2%)
    all_to_all x1, blocking collectives, on_device(): got = lax.all_to_all(payload, 'ctx', 0, 0, tiled=True)  114 us
    all_to_all x1, waiting for transfers between devices, on_device(): lax.all_to_all(jnp.concatenate([solved, gain_rows], axis=1), 'ctx', 0, 0,...  91.3 us
    convert_element_type x2, local copies, waits for them, and re-layouts, on_device(): weighted = (grouped_inputs * coeffs[..., None]).astype(jnp.bfloat16)  7.03 us
    dot_general x1, matrix products, on_device(): jnp.einsum('cjkJL,JcLpn->jckpn', jnp.where(own[None], 0.0, mixing), got_s...  6.44 us
    convert_element_type x2, local copies, waits for them, and re-layouts, on_device(): output_rows.reshape(tok_rows, head_count * head_width).astype(jnp.bfloat16)  5.39 us
  transfers between devices with their start and end apart: 1, of which 1 were waited for; matrix products, arithmetic and copies ran while one was open for 4% of the time, Pallas kernels for 0%

profile of v2, /device:TPU:8, one launch (start us, length us, event | category | flops | bytes accessed | tf_op | source)
XLA Modules:
  0.0 264.1 jit_solution(10545384249660082848)
XLA Ops:
  0.0 0.0 copy-start
  0.0 0.8 copy_bitcast_fusion.1
  0.8 0.6 reduce_window_sum.13
  1.4 0.2 slice_reduce_fusion.1
  1.5 0.8 reshape.156
  2.3 0.1 copy.77
  2.4 0.1 fusion.27
  2.5 1.5 copy.52
  4.0 0.3 reshape.155
  4.3 1.1 multiply_convert_fusion.2
  5.4 0.0 copy-done
  5.4 0.7 convolution_bitcast_fusion
  6.1 0.5 copy.57
  6.6 0.0 copy-start.1
  6.6 0.1 broadcast_in_dim.53
  6.7 0.4 pad_maximum_fusion
  7.1 1.5 copy-done.1
  8.6 0.0 copy-start.6
  8.6 0.0 copy-start.8
  8.7 0.0 copy-start.9
  8.7 113.5 %all_to_all.10 = f32[32,136,256]{2,1,0:T(8,128)S(1)} all-to-all(f32[32,136,256]{2,1,0:T(8,128)S(1)} %pad_maximum_fusion), channel_id=1, replica_groups=mesh['ctx'=32,'head'=8] {'ctx'}, dimensions={0} | all-to-all | bytes 8912896 | tf_op jit(solution)/shard_map/all_to_all | solution.py:56
  122.2 0.0 copy-start.2
  122.2 2.0 copy-done.2
  124.2 0.1 slice_reduce_fusion
  124.3 0.1 broadcast_in_dim.55
  124.4 0.0 copy-done.6
  124.5 0.6 select_reduce_fusion
  125.1 0.0 copy-done.8
  125.1 0.0 copy-done.9
  125.1 0.1 fusion.28
  125.2 1.1 reshape.160
  126.3 0.5 copy.60
  126.8 0.0 slice-start
  126.8 2.2 slice-done
  129.0 6.4 %fusion.2 = f32[32,1,2,64,256]{4,0,2,3,1:T(8,128)S(1)} fusion(f32[32,2,64,256,1]{3,2,1,0,4:T(8,128)S(1)} %bitcast.88, f32[32,2,32,2]{2,0,3,1:T(8,128)S(1)} %copy.60), kind=kOutput, calls=%fused_computation.5 | convolution fusion | flops 805306368 | bytes 8404992 | tf_op jit(solution)/shard_map/cjkJL,JcLpn->jckpn/dot_general | solution.py:67
  135.4 4.4 %copy.61 = f32[32,1,2,64,256]{4,3,2,0,1:T(8,128)} copy(f32[32,1,2,64,256]{4,0,2,3,1:T(8,128)S(1)} %fusion.2) | data formatting | bytes 8388608 | tf_op jit(solution)/shard_map/cjkJL,JcLpn->jckpn/transpose | solution.py:67
  139.8 0.1 reduce_sum.22
  139.9 0.2 slice_reduce_fusion.3
  140.1 0.1 broadcast_in_dim.60
  140.2 4.7 %pad_maximum_fusion.1 = f32[32,136,256]{2,1,0:T(8,128)} fusion(f32[32,8,256]{2,1,0:T(8,128)S(1)} %broadcast_in_dim.60, f32[32,128,256]{2,1,0:T(8,128)} %bitcast.89), kind=kLoop, calls=%fused_computation.1 | loop fusion | flops 1114112 | bytes 8912896 | tf_op jit(solution)/shard_map/concatenate | solution.py:75
  144.9 0.0 copy-start.3
  144.9 5.2 %all-to-all-start.1 = ((f32[32,136,256]{2,1,0:T(8,128)}), f32[32,136,256]{2,1,0:T(8,128)}, u32[]{:S(2)}, u32[]{:S(2)}) async-start(f32[32,136,256]{2,1,0:T(8,128)} %pad_maximum_fusion.1), calls=%async_computation.1 | async-start | bytes 8912896 | tf_op jit(solution)/shard_map/all_to_all | solution.py:75
  150.1 0.0 copy-done.3
  150.1 3.2 %reshape.188 = f32[2,128,1,32,64]{4,3,1,0,2:T(8,128)} reshape(bf16[256,2048]{1,0:T(8,128)(2,1)S(1)} %copy-done.3) | data formatting | bytes 3145728 | tf_op jit(solution)/shard_map/convert_element_type | solution.py:46
  153.3 0.0 copy-start.7
  153.3 0.0 copy-start.5
  153.3 3.8 %copy.64 = f32[2,128,1,32,64]{1,4,3,0,2:T(8,128)S(1)} copy(f32[2,128,1,32,64]{4,3,1,0,2:T(8,128)} %reshape.188) | data formatting | bytes 4194304 | tf_op jit(solution)/shard_map/convert_element_type | solution.py:46
  157.2 0.0 copy-done.7
  157.2 0.0 copy-done.5
  157.2 0.2 fusion.30
  157.4 3.4 %fusion.5 = f32[2,32,128,64]{2,3,1,0:T(8,128)} fusion(f32[32,2,128]{2,0,1:T(8,128)S(1)} %copy_bitcast_fusion, f32[32,2,128]{2,0,1:T(8,128)S(1)} %reduce_window_sum.13, f32[2,128,128]{2,1,0:T(8,128)S(1)} %fusion.30, pred[128,128]{1,0:T(8,128)(4,1)S(1)} %iota_compare_fusion, bf16[2,128,32,64]{1,0,3,2:T(2,128)(2,1)S(1)} %reshape.155), kind=kOutput, calls=%fused_computation.7 | convolution fusion | flops 139460608 | bytes 3358720 | tf_op jit(solution)/shard_map/gqkts,ksgqp->ktgqp/dot_general | solution.py:97
  160.8 91.3 %all-to-all-done.1 = f32[32,136,256]{2,1,0:T(8,128)} async-done(((f32[32,136,256]{2,1,0:T(8,128)}), f32[32,136,256]{2,1,0:T(8,128)}, u32[]{:S(2)}, u32[]{:S(2)}) %all-to-all-start.1) | async-done | bytes 4456480 | tf_op jit(solution)/shard_map/all_to_all | solution.py:75
  252.0 1.2 slice_reduce_fusion.2
  253.2 1.7 slice.52
  255.0 0.0 copy-start.4
  255.0 0.0 copy-start.10
  255.0 2.6 fusion.7
  257.6 0.2 pad_maximum_fusion.2
  257.9 0.0 copy-done.4
  257.9 0.0 copy-done.10
  257.9 0.8 fusion.10
  258.7 3.0 %copy.75 = bf16[2,128,1,32,64]{4,3,1,0,2:T(8,128)(2,1)S(1)} copy(bf16[2,128,1,32,64]{1,4,3,0,2:T(8,128)(2,1)S(1)} %fusion.10) | data formatting | bytes 2097152 | tf_op jit(solution)/shard_map/convert_element_type | solution.py:108
  261.7 2.4 reshape.189
  (4 shorter events, 0.1 us)
Async XLA Ops:
  0.0 5.4 %copy-start = (bf16[256,256]{1,0:T(8,128)(2,1)S(1)}, bf16[256,256]{1,0:T(8,128)(2,1)}, u32[]{:S(2)}) copy-start(bf16[256,256]{1,0:T(8,128)(2,1)} %param.13) | copy-start | bytes 393220
  6.6 2.1 copy-start.1
  8.6 115.8 %copy-start.6 = (pred[1,64,64,64]{3,2,1,0:T(32,128)(4,1)S(1)}, pred[1,64,64,64]{3,2,1,0:T(32,128)(4,1)}, u32[]{:S(2)}) copy-start(pred[1,64,64,64]{3,2,1,0:T(32,128)(4,1)} %constant.14.clone) | copy-start | bytes 786436
  8.6 116.4 %copy-start.8 = (pred[64,64]{1,0:T(32,128)(4,1)S(1)}, pred[64,64]{1,0:T(32,128)(4,1)}, u32[]{:S(2)}) copy-start(pred[64,64]{1,0:T(32,128)(4,1)} %constant.20) | copy-start | bytes 12292
  8.7 116.4 %copy-start.9 = (pred[64,64]{1,0:T(32,128)(4,1)S(1)}, pred[64,64]{1,0:T(32,128)(4,1)}, u32[]{:S(2)}) copy-start(pred[64,64]{1,0:T(32,128)(4,1)} %constant.22) | copy-start | bytes 12292
  122.2 2.0 copy-start.2
  126.8 2.2 slice-start
  144.9 5.2 %copy-start.3 = (bf16[256,2048]{1,0:T(8,128)(2,1)S(1)}, bf16[256,2048]{1,0:T(8,128)(2,1)}, u32[]{:S(2)}) copy-start(bf16[256,2048]{1,0:T(8,128)(2,1)} %param.10) | copy-start | bytes 3145732
  144.9 107.1 %all-to-all-start.1 = ((f32[32,136,256]{2,1,0:T(8,128)}), f32[32,136,256]{2,1,0:T(8,128)}, u32[]{:S(2)}, u32[]{:S(2)}) async-start(f32[32,136,256]{2,1,0:T(8,128)} %pad_maximum_fusion.1), calls=%async_computation.1 | async-start | bytes 8912896 | tf_op jit(solution)/shard_map/all_to_all | solution.py:75
  153.3 3.8 %copy-start.7 = (f32[32,256]{1,0:T(8,128)S(1)}, f32[32,256]{1,0:T(8,128)}, u32[]{:S(2)}) copy-start(f32[32,256]{1,0:T(8,128)} %param.12) | copy-start | bytes 98308
  153.3 3.9 %copy-start.5 = (bf16[256,256]{1,0:T(8,128)(2,1)S(1)}, bf16[256,256]{1,0:T(8,128)(2,1)}, u32[]{:S(2)}) copy-start(bf16[256,256]{1,0:T(8,128)(2,1)} %param.14) | copy-start | bytes 393220
  255.0 2.9 %copy-start.4 = (f32[2,32,128,64]{2,3,1,0:T(8,128)S(1)}, f32[2,32,128,64]{2,3,1,0:T(8,128)}, u32[]{:S(2)}) copy-start(f32[2,32,128,64]{2,3,1,0:T(8,128)} %fusion.5) | copy-start | bytes 6291460
  255.0 2.9 %copy-start.10 = (f32[32]{0:T(128)S(1)}, f32[32]{0:T(128)}, u32[]{:S(2)}) copy-start(f32[32]{0:T(128)} %param.15) | copy-start | bytes 388

commit v3 on v2

--- a/solution.py
+++ b/solution.py
@@ -6,6 +6,7 @@
 
 N = 256
 SPAN = 128
+PIECES = 2
 
 
 def chain_mixing(decay, devices, halves):
@@ -50,38 +51,43 @@
     tail = jnp.concatenate(
         [totals, jnp.zeros((head_count, extra - halves), jnp.float32)], axis=1
     )
-    payload = jnp.concatenate(
-        [span_states, jnp.broadcast_to(tail[:, :, None], (head_count, extra, state_size))], axis=1
-    )
-    got = lax.all_to_all(payload, "ctx", 0, 0, tiled=True)
-    got_states = got[:, :rows].reshape(devices, per_chunk, halves, head_width, state_size)
-    got_decay = got[:, rows:rows + halves, 0].reshape(devices, per_chunk, halves)
-
-    mixing = chain_mixing(
-        jnp.transpose(got_decay, (1, 0, 2)).reshape(per_chunk, devices * halves), devices, halves
-    )
+    tail = jnp.broadcast_to(tail[:, :, None], (head_count, extra, state_size))
+    grid = span_states.reshape(head_count, halves, head_width, state_size)
+    width = head_width // PIECES
     j = np.arange(devices)
     own = np.zeros((devices, halves, devices, halves), bool)
     own[j, 1, j, 0] = True
-    own_gain = jnp.sum(jnp.where(own[None], mixing, 0.0), axis=(3, 4))[:, :, 1]
-    solved = jnp.einsum(
-        "cjkJL,JcLpn->jckpn", jnp.where(own[None], 0.0, mixing), got_states,
-        precision=lax.Precision.HIGHEST, preferred_element_type=jnp.float32,
-    ).reshape(devices * per_chunk, rows, state_size)
-    gain_rows = jnp.broadcast_to(
-        jnp.transpose(own_gain).reshape(devices * per_chunk, 1, 1),
-        (devices * per_chunk, extra, state_size),
-    )
-    back = lax.all_to_all(jnp.concatenate([solved, gain_rows], axis=1), "ctx", 0, 0, tiled=True)
-    half_rows = head_width
-    gain = back[:, rows:rows + 1, :1]
-    entering = jnp.concatenate(
-        [
-            back[:, :half_rows],
-            back[:, half_rows:rows] + gain * span_states[:, :half_rows],
-        ],
-        axis=1,
-    )
+    parts = []
+    for piece in range(PIECES):
+        chunk = grid[:, :, piece * width:(piece + 1) * width].reshape(head_count, halves * width, state_size)
+        if piece == 0:
+            chunk = jnp.concatenate([chunk, tail], axis=1)
+        got = lax.all_to_all(chunk, "ctx", 0, 0, tiled=True)
+        got_states = got[:, :halves * width].reshape(devices, per_chunk, halves, width, state_size)
+        if piece == 0:
+            got_decay = got[:, halves * width:halves * width + halves, 0]
+            got_decay = got_decay.reshape(devices, per_chunk, halves)
+            mixing = chain_mixing(
+                jnp.transpose(got_decay, (1, 0, 2)).reshape(per_chunk, devices * halves),
+                devices, halves,
+            )
+            own_gain = jnp.sum(jnp.where(own[None], mixing, 0.0), axis=(3, 4))[:, :, 1]
+            others = jnp.where(own[None], 0.0, mixing)
+        solved = jnp.einsum(
+            "cjkJL,JcLpn->jckpn", others, got_states,
+            precision=lax.Precision.HIGHEST, preferred_element_type=jnp.float32,
+        ).reshape(devices * per_chunk, halves * width, state_size)
+        gain_rows = jnp.broadcast_to(
+            jnp.transpose(own_gain).reshape(devices * per_chunk, 1, 1),
+            (devices * per_chunk, extra, state_size),
+        )
+        back = lax.all_to_all(jnp.concatenate([solved, gain_rows], axis=1), "ctx", 0, 0, tiled=True)
+        gain = back[:, halves * width:halves * width + 1, :1]
+        back = back[:, :halves * width].reshape(head_count, halves, width, state_size)
+        parts.append(
+            jnp.stack([back[:, 0], back[:, 1] + gain * grid[:, 0, piece * width:(piece + 1) * width]], axis=1)
+        )
+    entering = jnp.concatenate(parts, axis=2)
     state_bf = entering.astype(jnp.bfloat16).reshape(
         group_count, per_group, halves, head_width, state_size
     )

time: 265 us -> 282 us (1.064)
  blocking collectives: 114 us -> 62.9 us
  waiting for transfers between devices: 91.3 us -> 133 us
  starting transfers between devices: 5.2 us -> 20.8 us
  local copies, waits for them, and re-layouts: 31.9 us -> 37.1 us
  matrix products: 11.5 us -> 16.5 us
    all_to_all x0 -> x2, waiting for transfers between devices: none -> 94 us  [on_device(): got = lax.all_to_all(chunk, 'ctx', 0, 0, tiled=True)]
    all_to_all x1, waiting for transfers between devices: 91.3 us -> 38.8 us  [on_device(): lax.all_to_all(jnp.concatenate([solved, gain_rows], axis=1), 'ctx', 0, 0,...]
    all_to_all x1, blocking collectives: 114 us -> 62.9 us  [on_device(): lax.all_to_all(jnp.concatenate([solved, gain_rows], axis=1), 'ctx', 0, 0,...]
    all_to_all x0 -> x2, starting transfers between devices: none -> 16.4 us  [on_device(): got = lax.all_to_all(chunk, 'ctx', 0, 0, tiled=True)]
    slice x5 -> x9, local copies, waits for them, and re-layouts: 5.26 us -> 8.26 us  [the longest x3 5.48 us: on_device(): grid[:, :, piece * width:(piece + 1) * width]]
    dot_general x1 -> x2, matrix products: 6.44 us -> 8.09 us  [on_device(): jnp.einsum('cjkJL,JcLpn->jckpn', others, got_states, precision=lax.Precis...]
  transfers between devices with their start and end apart: 1 -> 3, of which waited for: 1 -> 3; matrix products, arithmetic and copies ran while one was open for 4% -> 10% of each run, Pallas kernels for 0% -> 0%
where the time goes in v3:
time: 282 us; the launch traced here: 281 us
  waiting for transfers between devices  133 us (47%)
  blocking collectives  62.9 us (22%)
  local copies, waits for them, and re-layouts  37.1 us (13%)
  starting transfers between devices  20.8 us (7%)
  matrix products  16.5 us (6%)
  other arithmetic  10.4 us (4%)
    all_to_all x2, waiting for transfers between devices, on_device(): got = lax.all_to_all(chunk, 'ctx', 0, 0, tiled=True)  94 us
    all_to_all x1, blocking collectives, on_device(): lax.all_to_all(jnp.concatenate([solved, gain_rows], axis=1), 'ctx', 0, 0,...  62.9 us
    all_to_all x1, waiting for transfers between devices, on_device(): lax.all_to_all(jnp.concatenate([solved, gain_rows], axis=1), 'ctx', 0, 0,...  38.8 us
    all_to_all x2, starting transfers between devices, on_device(): got = lax.all_to_all(chunk, 'ctx', 0, 0, tiled=True)  16.4 us
    dot_general x2, matrix products, on_device(): jnp.einsum('cjkJL,JcLpn->jckpn', others, got_states, precision=lax.Precis...  8.09 us
    convert_element_type x2, local copies, waits for them, and re-layouts, on_device(): weighted = (grouped_inputs * coeffs[..., None]).astype(jnp.bfloat16)  8.08 us
  transfers between devices with their start and end apart: 3, of which 3 were waited for; matrix products, arithmetic and copies ran while one was open for 10% of the time, Pallas kernels for 0%

profile of v3, /device:TPU:8, one launch (start us, length us, event | category | flops | bytes accessed | tf_op | source)
XLA Modules:
  0.0 280.7 jit_solution(4796856212691498563)
XLA Ops:
  0.0 0.0 copy-start
  0.0 0.8 copy_bitcast_fusion.1
  0.8 0.6 reduce_window_sum.13
  1.4 0.2 slice_reduce_fusion.1
  1.5 0.8 reshape.178
  2.3 0.1 copy.102
  2.4 0.6 fusion.39
  3.1 0.0 copy-done.11
  3.1 1.5 copy.66
  4.6 0.3 reshape.177
  4.9 0.0 copy-start.6
  4.9 1.1 multiply_convert_fusion.2
  5.9 0.7 convolution_bitcast_fusion
  6.7 2.1 fusion.43
  8.8 0.6 copy-done.1
  9.4 0.1 copy.71
  9.5 0.1 broadcast_in_dim.56
  9.6 1.6 pad_maximum_fusion.2
  11.2 11.3 %all-to-all-start = ((f32[32,72,256]{2,1,0:T(8,128)}), f32[32,72,256]{2,1,0:T(8,128)S(1)}, u32[]{:S(2)}, u32[]{:S(2)}) async-start(f32[32,72,256]{2,1,0:T(8,128)} %pad_maximum_fusion.2), calls=%async_computation | async-start | bytes 4718592 | tf_op jit(solution)/shard_map/all_to_all | solution.py:65
  22.6 3.2 %copy.78 = f32[32,2,32,256]{3,2,1,0:T(8,128)} copy(f32[32,2,32,256]{3,2,0,1:T(8,128)} %get-tuple-element.7) | data formatting | bytes 4194304 | tf_op jit(solution)/shard_map/slice | solution.py:62
  25.7 54.6 %all-to-all-done = f32[32,72,256]{2,1,0:T(8,128)S(1)} async-done(((f32[32,72,256]{2,1,0:T(8,128)}), f32[32,72,256]{2,1,0:T(8,128)S(1)}, u32[]{:S(2)}, u32[]{:S(2)}) %all-to-all-start) | async-done | bytes 2359328 | tf_op jit(solution)/shard_map/all_to_all | solution.py:65
  80.4 5.1 %all-to-all-start.2 = ((f32[32,64,256]{2,1,0:T(8,128)}), f32[32,64,256]{2,1,0:T(8,128)}, u32[]{:S(2)}, u32[]{:S(2)}) async-start(f32[32,64,256]{2,1,0:T(8,128)} %bitcast.103), calls=%async_computation.2 | async-start | bytes 4194304 | tf_op jit(solution)/shard_map/all_to_all | solution.py:65
  85.4 0.1 slice_reduce_fusion
  85.6 0.1 broadcast_in_dim.58
  85.7 0.6 select_reduce_fusion
  86.3 0.0 copy-done.14
  86.3 0.0 copy-done.15
  86.3 0.7 fusion.40
  87.0 1.8 reshape.182
  88.9 1.1 copy.74
  90.0 0.2 slice.68
  90.2 0.6 copy-done.9
  90.8 3.3 %fusion.22 = f32[32,1,2,32,256]{4,0,2,3,1:T(8,128)S(1)} fusion(f32[32,2,32,256,1]{3,2,1,0,4:T(8,128)S(1)} %bitcast.105, f32[32,2,32,2]{2,0,3,1:T(8,128)S(1)} %copy-done.9), kind=kOutput, calls=%fused_computation.30 | convolution fusion | flops 402653184 | bytes 4210688 | tf_op jit(solution)/shard_map/cjkJL,JcLpn->jckpn/dot_general | solution.py:76
  94.1 1.2 copy.75
  95.4 39.4 %all-to-all-done.2 = f32[32,64,256]{2,1,0:T(8,128)} async-done(((f32[32,64,256]{2,1,0:T(8,128)}), f32[32,64,256]{2,1,0:T(8,128)}, u32[]{:S(2)}, u32[]{:S(2)}) %all-to-all-start.2) | async-done | bytes 2097184 | tf_op jit(solution)/shard_map/all_to_all | solution.py:65
  134.7 4.8 %fusion.25 = f32[32,1,2,32,256]{4,0,2,3,1:T(8,128)S(1)} fusion(f32[32,2,32,256,1]{3,2,1,0,4:T(8,128)} %bitcast.27, f32[32,2,32,2]{2,0,3,1:T(8,128)S(1)} %copy-done.9), kind=kOutput, calls=%fused_computation.31 | convolution fusion | flops 402653184 | bytes 4210688 | tf_op jit(solution)/shard_map/cjkJL,JcLpn->jckpn/dot_general | solution.py:76
  139.5 2.5 copy.81
  142.1 0.1 reduce_sum.22
  142.2 0.2 slice_reduce_fusion.4
  142.4 0.1 broadcast_in_dim.63
  142.5 3.5 %pad_maximum_fusion.1 = (f32[32,72,256]{2,1,0:T(8,128)}, f32[32,72,256]{2,1,0:T(8,128)S(1)}) fusion(f32[32,8,256]{2,1,0:T(8,128)S(1)} %broadcast_in_dim.63, f32[32,64,256]{2,1,0:T(8,128)S(1)} %bitcast.106, f32[32,64,256]{2,1,0:T(8,128)} %bitcast.107), kind=kLoop, calls=%fused_computation.2 | loop fusion | flops 1179648 | bytes 9175040 | tf_op jit(solution)/shard_map/concatenate | solution.py:84
  145.9 62.9 %all_to_all.20 = f32[32,72,256]{2,1,0:T(8,128)} all-to-all(f32[32,72,256]{2,1,0:T(8,128)S(1)} %get-tuple-element.10), channel_id=1, replica_groups=mesh['ctx'=32,'head'=8] {'ctx'}, dimensions={0} | all-to-all | bytes 4718592 | tf_op jit(solution)/shard_map/all_to_all | solution.py:84
  208.8 4.4 %all-to-all-start.1 = ((f32[32,72,256]{2,1,0:T(8,128)}), f32[32,72,256]{2,1,0:T(8,128)S(1)}, u32[]{:S(2)}, u32[]{:S(2)}) async-start(f32[32,72,256]{2,1,0:T(8,128)} %get-tuple-element.9), calls=%async_computation.1 | async-start | bytes 4718592 | tf_op jit(solution)/shard_map/all_to_all | solution.py:84
  213.2 3.2 %reshape.218 = f32[2,128,1,32,64]{4,3,1,0,2:T(8,128)} reshape(bf16[256,2048]{1,0:T(8,128)(2,1)S(1)} %copy-done.5) | data formatting | bytes 3145728 | tf_op jit(solution)/shard_map/convert_element_type | solution.py:47
  216.5 4.8 %copy.85 = f32[2,128,1,32,64]{1,4,3,0,2:T(8,128)} copy(f32[2,128,1,32,64]{4,3,1,0,2:T(8,128)} %reshape.218) | data formatting | bytes 4194304 | tf_op jit(solution)/shard_map/convert_element_type | solution.py:47
  221.3 0.8 copy_bitcast_fusion
  222.1 1.1 fusion.44
  223.2 4.4 %fusion = f32[2,32,128,64]{2,3,1,0:T(8,128)} fusion(f32[32,2,128]{2,0,1:T(8,128)S(1)} %copy_bitcast_fusion, f32[32,2,128]{2,0,1:T(8,128)} %copy-done.11, f32[2,128,128]{2,1,0:T(8,128)S(1)} %fusion.44, pred[128,128]{1,0:T(8,128)(4,1)S(1)} %iota_compare_fusion, bf16[2,128,32,64]{1,0,3,2:T(2,128)(2,1)S(1)} %copy-done.7), kind=kOutput, calls=%fused_computation.5 | convolution fusion | flops 139460608 | bytes 3358720 | tf_op jit(solution)/shard_map/gqkts,ksgqp->ktgqp/dot_general | solution.py:103
  227.6 0.0 copy-done.3
  227.6 1.6 slice.77
  229.2 0.3 slice_reduce_fusion.2
  229.5 38.8 %all-to-all-done.1 = f32[32,72,256]{2,1,0:T(8,128)S(1)} async-done(((f32[32,72,256]{2,1,0:T(8,128)}), f32[32,72,256]{2,1,0:T(8,128)S(1)}, u32[]{:S(2)}, u32[]{:S(2)}) %all-to-all-start.1) | async-done | bytes 2359328 | tf_op jit(solution)/shard_map/all_to_all | solution.py:84
  268.3 0.2 slice.71
  268.6 0.3 slice_reduce_fusion.3
  268.9 1.6 copy-done.2
  270.5 0.0 copy-start.16
  270.6 1.7 fusion.31
  272.2 0.2 copy-done.4
  272.4 0.6 copy-done.8
  273.1 0.0 copy-done.12
  273.1 0.0 copy-done.16
  273.1 2.2 fusion.11
  275.3 3.0 %copy.100 = bf16[2,128,1,32,64]{4,3,1,0,2:T(8,128)(2,1)S(1)} copy(bf16[2,128,1,32,64]{1,4,3,0,2:T(8,128)(2,1)S(1)} %fusion.11) | data formatting | bytes 2097152 | tf_op jit(solution)/shard_map/convert_element_type | solution.py:114
  278.3 2.4 reshape.219
  (23 shorter events, 0.1 us)
Async XLA Ops:
  0.0 5.9 %copy-start = (bf16[256,256]{1,0:T(8,128)(2,1)S(1)}, bf16[256,256]{1,0:T(8,128)(2,1)}, u32[]{:S(2)}) copy-start(bf16[256,256]{1,0:T(8,128)(2,1)} %param.13) | copy-start | bytes 393220
  1.4 1.7 copy-start.11
  4.9 1.8 copy-start.6
  6.6 2.7 copy-start.1
  11.2 69.1 %all-to-all-start = ((f32[32,72,256]{2,1,0:T(8,128)}), f32[32,72,256]{2,1,0:T(8,128)S(1)}, u32[]{:S(2)}, u32[]{:S(2)}) async-start(f32[32,72,256]{2,1,0:T(8,128)} %pad_maximum_fusion.2), calls=%async_computation | async-start | bytes 4718592 | tf_op jit(solution)/shard_map/all_to_all | solution.py:65
  80.3 5.3 %copy-start.10 = (pred[1,64,64,64]{3,2,1,0:T(32,128)(4,1)S(1)}, pred[1,64,64,64]{3,2,1,0:T(32,128)(4,1)}, u32[]{:S(2)}) copy-start(pred[1,64,64,64]{3,2,1,0:T(32,128)(4,1)} %constant.14.clone) | copy-start | bytes 786436
  80.4 5.9 %copy-start.14 = (pred[64,64]{1,0:T(32,128)(4,1)S(1)}, pred[64,64]{1,0:T(32,128)(4,1)}, u32[]{:S(2)}) copy-start(pred[64,64]{1,0:T(32,128)(4,1)} %constant.20) | copy-start | bytes 12292
  80.4 5.9 %copy-start.15 = (pred[64,64]{1,0:T(32,128)(4,1)S(1)}, pred[64,64]{1,0:T(32,128)(4,1)}, u32[]{:S(2)}) copy-start(pred[64,64]{1,0:T(32,128)(4,1)} %constant.22) | copy-start | bytes 12292
  80.4 54.4 %all-to-all-start.2 = ((f32[32,64,256]{2,1,0:T(8,128)}), f32[32,64,256]{2,1,0:T(8,128)}, u32[]{:S(2)}, u32[]{:S(2)}) async-start(f32[32,64,256]{2,1,0:T(8,128)} %bitcast.103), calls=%async_computation.2 | async-start | bytes 4194304 | tf_op jit(solution)/shard_map/all_to_all | solution.py:65
  90.0 0.8 copy-start.9
  208.8 4.4 %copy-start.5 = (bf16[256,2048]{1,0:T(8,128)(2,1)S(1)}, bf16[256,2048]{1,0:T(8,128)(2,1)}, u32[]{:S(2)}) copy-start(bf16[256,2048]{1,0:T(8,128)(2,1)} %param.10) | copy-start | bytes 3145732
  208.8 59.5 %all-to-all-start.1 = ((f32[32,72,256]{2,1,0:T(8,128)}), f32[32,72,256]{2,1,0:T(8,128)S(1)}, u32[]{:S(2)}, u32[]{:S(2)}) async-start(f32[32,72,256]{2,1,0:T(8,128)} %get-tuple-element.9), calls=%async_computation.1 | async-start | bytes 4718592 | tf_op jit(solution)/shard_map/all_to_all | solution.py:84
  216.5 6.7 %copy-start.7 = (bf16[2,128,32,64]{1,0,3,2:T(2,128)(2,1)S(1)}, bf16[2,128,32,64]{1,0,3,2:T(2,128)(2,1)}, u32[]{:S(2)}) copy-start(bf16[2,128,32,64]{1,0,3,2:T(2,128)(2,1)} %copy-done.6) | copy-start | bytes 3145732
  223.2 4.4 %copy-start.3 = (f32[32,72,256]{2,1,0:T(8,128)S(1)}, f32[32,72,256]{2,1,0:T(8,128)}, u32[]{:S(2)}) copy-start(f32[32,72,256]{2,1,0:T(8,128)} %all_to_all.20) | copy-start | bytes 7077892
  268.3 2.2 copy-start.2
  270.5 1.9 copy-start.4
  270.5 2.5 copy-start.8
  270.5 2.5 copy-start.12
  270.5 2.5 copy-start.13
  270.5 2.5 copy-start.16

commit v4 on v2

--- a/solution.py
+++ b/solution.py
@@ -64,26 +64,28 @@
     own = np.zeros((devices, halves, devices, halves), bool)
     own[j, 1, j, 0] = True
     own_gain = jnp.sum(jnp.where(own[None], mixing, 0.0), axis=(3, 4))[:, :, 1]
-    solved = jnp.einsum(
-        "cjkJL,JcLpn->jckpn", jnp.where(own[None], 0.0, mixing), got_states,
-        precision=lax.Precision.HIGHEST, preferred_element_type=jnp.float32,
-    ).reshape(devices * per_chunk, rows, state_size)
+    others = jnp.where(own[None], 0.0, mixing)
+    if per_chunk == 1:
+        solved = jnp.einsum(
+            "uv,vpn->upn", others.reshape(devices * halves, devices * halves),
+            got[:, :rows].reshape(devices * halves, head_width, state_size),
+            precision=lax.Precision.HIGHEST, preferred_element_type=jnp.float32,
+        ).reshape(devices, rows, state_size)
+    else:
+        solved = jnp.einsum(
+            "cjkJL,JcLpn->jckpn", others, got_states,
+            precision=lax.Precision.HIGHEST, preferred_element_type=jnp.float32,
+        ).reshape(devices * per_chunk, rows, state_size)
     gain_rows = jnp.broadcast_to(
         jnp.transpose(own_gain).reshape(devices * per_chunk, 1, 1),
         (devices * per_chunk, extra, state_size),
     )
     back = lax.all_to_all(jnp.concatenate([solved, gain_rows], axis=1), "ctx", 0, 0, tiled=True)
-    half_rows = head_width
     gain = back[:, rows:rows + 1, :1]
-    entering = jnp.concatenate(
-        [
-            back[:, :half_rows],
-            back[:, half_rows:rows] + gain * span_states[:, :half_rows],
-        ],
-        axis=1,
-    )
-    state_bf = entering.astype(jnp.bfloat16).reshape(
-        group_count, per_group, halves, head_width, state_size
+    front_in = back[:, :head_width]
+    back_in = back[:, head_width:rows] + gain * span_states[:, :head_width]
+    state_bf = jnp.stack([front_in, back_in]).astype(jnp.bfloat16).reshape(
+        halves, group_count, per_group * head_width, state_size
     )
 
     scores = jnp.einsum("ktgn,ksgn->gkts", c_spans, b_spans, preferred_element_type=jnp.float32)
@@ -96,15 +98,17 @@
     )
     diagonal_part = jnp.einsum(
         "gqkts,ksgqp->ktgqp", weights, grouped_inputs, preferred_element_type=jnp.float32
-    )
+    ).reshape(halves, SPAN, head_count * head_width)
     state_part = jnp.einsum(
-        "ktgn,gqkpn->ktgqp", c_spans, state_bf, preferred_element_type=jnp.float32
-    )
-    decay_in = jnp.transpose(jnp.exp(cum_grouped), (2, 3, 0, 1))[..., None]
-    skip = skip_gain.reshape(group_count, per_group)[None, None, :, :, None]
-    output_rows = (
-        diagonal_part + state_part * decay_in + skip * grouped_inputs.astype(jnp.float32)
-    )
+        "ktgn,kgmn->ktgm", c_spans, state_bf, preferred_element_type=jnp.float32
+    ).reshape(halves, SPAN, head_count * head_width)
+    decay_in = jnp.broadcast_to(
+        jnp.transpose(jnp.exp(cumulative), (1, 2, 0))[..., None],
+        (halves, SPAN, head_count, head_width),
+    ).reshape(halves, SPAN, head_count * head_width)
+    skip = jnp.repeat(skip_gain, head_width)[None, None, :]
+    inputs = features.reshape(halves, SPAN, head_count * head_width).astype(jnp.float32)
+    output_rows = diagonal_part + state_part * decay_in + skip * inputs
     return output_rows.reshape(tok_rows, head_count * head_width).astype(jnp.bfloat16)
 
 

time: 265 us -> 267 us (level)
  waiting for transfers between devices: 91.3 us -> 98.1 us
  local copies, waits for them, and re-layouts: 31.9 us -> 25.5 us
  other arithmetic: 10.5 us -> 13.3 us
    convert_element_type x2 -> x0, local copies, waits for them, and re-layouts: 7.03 us -> none  [on_device(): weighted = (grouped_inputs * coeffs[..., None]).astype(jnp.bfloat16)]
    all_to_all x1, waiting for transfers between devices: 91.3 us -> 98.1 us  [on_device(): lax.all_to_all(jnp.concatenate([solved, gain_rows], axis=1), 'ctx', 0, 0,...]
    dot_general x0 -> x1, local copies, waits for them, and re-layouts: none -> 4.36 us  [on_device(): jnp.einsum('uv,vpn->upn', others.reshape(devices * halves, devices * halv...]
    convert_element_type x0 -> x1, other arithmetic: none -> 3.15 us  [on_device(): output_rows.reshape(tok_rows, head_count * head_width).astype(jnp.bfloat16)]
    convert_element_type x2 -> x1, local copies, waits for them, and re-layouts: 5.39 us -> 2.26 us  [on_device(): output_rows.reshape(tok_rows, head_count * head_width).astype(jnp.bfloat16)]
    reshape x0 -> x1, local copies, waits for them, and re-layouts: none -> 2.94 us  [on_device(): state_part = jnp.einsum('ktgn,kgmn->ktgm', c_spans, state_bf, preferred_e...]
  transfers between devices with their start and end apart: 1 -> 1, of which waited for: 1 -> 1; matrix products, arithmetic and copies ran while one was open for 4% -> 1% of each run, Pallas kernels for 0% -> 0%
where the time goes in v4:
time: 267 us; the launch traced here: 266 us
  blocking collectives  114 us (43%)
  waiting for transfers between devices  98.1 us (37%)
  local copies, waits for them, and re-layouts  25.5 us (10%)
  other arithmetic  13.3 us (5%)
  matrix products  10.6 us (4%)
  starting transfers between devices  5.2 us (2%)
    all_to_all x1, blocking collectives, on_device(): got = lax.all_to_all(payload, 'ctx', 0, 0, tiled=True)  114 us
    all_to_all x1, waiting for transfers between devices, on_device(): lax.all_to_all(jnp.concatenate([solved, gain_rows], axis=1), 'ctx', 0, 0,...  98.1 us
    dot_general x1, matrix products, on_device(): jnp.einsum('uv,vpn->upn', others.reshape(devices * halves, devices * halv...  5.97 us
  transfers between devices with their start and end apart: 1, of which 1 were waited for; matrix products, arithmetic and copies ran while one was open for 1% of the time, Pallas kernels for 0%

profile of v4, /device:TPU:8, one launch (start us, length us, event | category | flops | bytes accessed | tf_op | source)
XLA Modules:
  0.0 266.5 jit_solution(9733387355891392899)
XLA Ops:
  0.0 0.0 copy-start
  0.0 0.8 copy_bitcast_fusion.1
  0.8 0.6 reduce_window_sum.13
  1.4 0.2 slice_reduce_fusion.1
  1.5 0.8 reshape.144
  2.3 0.1 copy.68
  2.4 0.1 fusion.24
  2.5 1.5 copy.53
  4.0 0.3 reshape.142
  4.3 1.1 multiply_convert_fusion.2
  5.4 0.0 copy-done
  5.4 0.7 convolution_bitcast_fusion
  6.1 0.5 copy.59
  6.6 0.0 copy-start.1
  6.6 0.1 broadcast_in_dim.62
  6.7 0.4 pad_maximum_fusion
  7.1 1.5 copy-done.1
  8.6 0.0 copy-start.4
  8.6 0.0 copy-start.6
  8.7 0.0 copy-start.7
  8.7 113.5 %all_to_all.10 = f32[32,136,256]{2,1,0:T(8,128)S(1)} all-to-all(f32[32,136,256]{2,1,0:T(8,128)S(1)} %pad_maximum_fusion), channel_id=1, replica_groups=mesh['ctx'=32,'head'=8] {'ctx'}, dimensions={0} | all-to-all | bytes 8912896 | tf_op jit(solution)/shard_map/all_to_all | solution.py:56
  122.2 0.0 copy-start.2
  122.2 2.0 copy-done.2
  124.2 0.1 slice_reduce_fusion
  124.3 0.1 broadcast_in_dim.63
  124.4 0.0 copy-done.4
  124.5 0.6 select_reduce_fusion
  125.1 0.0 copy-done.6
  125.1 0.0 copy-done.7
  125.1 0.1 select_reduce_fusion.1
  125.2 0.0 slice-start
  125.2 2.2 slice-done
  127.4 6.0 %fusion = f32[64,64,256]{2,0,1:T(8,128)S(1)} fusion(f32[64,64,256]{2,1,0:T(8,128)S(1)} %bitcast.81, pred[64,64]{1,0:T(32,128)(4,1)S(1)} %copy-done.7, pred[64,64]{1,0:T(32,128)(4,1)S(1)} %copy-done.6, f32[64,64]{1,0:T(8,128)S(1)} %select_reduce_fusion), kind=kOutput, calls=%fused_computation.2 | convolution fusion | flops 805314560 | bytes 8413184 | tf_op jit(solution)/shard_map/uv,vpn->upn/dot_general | solution.py:69
  133.4 4.4 %copy.62 = f32[64,64,256]{2,1,0:T(8,128)} copy(f32[64,64,256]{2,0,1:T(8,128)S(1)} %fusion) | data formatting | bytes 8388608 | tf_op jit(solution)/shard_map/uv,vpn->upn/dot_general | solution.py:69
  137.7 0.1 reduce_sum.22
  137.8 0.2 slice_reduce_fusion.3
  138.0 0.1 broadcast_in_dim.68
  138.1 4.7 %pad_maximum_fusion.1 = f32[32,136,256]{2,1,0:T(8,128)} fusion(f32[32,8,256]{2,1,0:T(8,128)S(1)} %broadcast_in_dim.68, f32[32,128,256]{2,1,0:T(8,128)} %bitcast.82), kind=kLoop, calls=%fused_computation.1 | loop fusion | flops 1114112 | bytes 8912896 | tf_op jit(solution)/shard_map/concatenate | solution.py:83
  142.9 0.0 copy-start.5
  142.9 0.0 copy-start.3
  142.9 5.2 %all-to-all-start.1 = ((f32[32,136,256]{2,1,0:T(8,128)}), f32[32,136,256]{2,1,0:T(8,128)}, u32[]{:S(2)}, u32[]{:S(2)}) async-start(f32[32,136,256]{2,1,0:T(8,128)} %pad_maximum_fusion.1), calls=%async_computation.1 | async-start | bytes 8912896 | tf_op jit(solution)/shard_map/all_to_all | solution.py:83
  148.1 0.0 copy-done.5
  148.1 0.0 copy-done.3
  148.1 0.2 fusion.30
  148.3 1.6 fusion.18
  149.9 0.0 copy-start.8
  149.9 1.7 copy.55
  151.7 0.0 copy-done.8
  151.7 0.1 broadcast_in_dim.70
  151.8 0.1 mul.85
  151.8 98.1 %all-to-all-done.1 = f32[32,136,256]{2,1,0:T(8,128)} async-done(((f32[32,136,256]{2,1,0:T(8,128)}), f32[32,136,256]{2,1,0:T(8,128)}, u32[]{:S(2)}, u32[]{:S(2)}) %all-to-all-start.1) | async-done | bytes 4456480 | tf_op jit(solution)/shard_map/all_to_all | solution.py:83
  250.0 1.2 slice_reduce_fusion.2
  251.2 1.7 slice.52
  252.9 2.5 fusion.7
  255.4 2.1 fusion.8
  257.6 2.9 %copy.64 = f32[256,2048]{0,1:T(8,128)} copy(f32[256,2048]{1,0:T(8,128)} %bitcast.85) | data formatting | bytes 4194304 | tf_op jit(solution)/shard_map/reshape | solution.py:104
  260.5 0.5 broadcast_in_dim.69
  261.0 3.2 %fusion.5 = bf16[256,2048]{0,1:T(8,128)(2,1)} fusion(f32[256,2048]{0,1:T(8,128)} %copy.64, f32[256,8,2,128]{3,2,1,0:T(2,128)S(1)} %bitcast.84, f32[256,8,2,128]{3,2,1,0:T(2,128)S(1)} %bitcast.83, bf16[256,2048]{0,1:T(8,128)(2,1)S(1)} %copy.53, f32[2048]{0:T(1024)S(1)} %mul.85), kind=kLoop, calls=%fused_computation.10 | loop fusion | flops 3145728 | bytes 8396800 | tf_op jit(solution)/shard_map/convert_element_type | solution.py:112
  264.2 2.3 copy.66
  (6 shorter events, 0.1 us)
Async XLA Ops:
  0.0 5.4 %copy-start = (bf16[256,256]{1,0:T(8,128)(2,1)S(1)}, bf16[256,256]{1,0:T(8,128)(2,1)}, u32[]{:S(2)}) copy-start(bf16[256,256]{1,0:T(8,128)(2,1)} %param.13) | copy-start | bytes 393220
  6.6 2.1 copy-start.1
  8.6 115.8 %copy-start.4 = (pred[1,64,64,64]{3,2,1,0:T(32,128)(4,1)S(1)}, pred[1,64,64,64]{3,2,1,0:T(32,128)(4,1)}, u32[]{:S(2)}) copy-start(pred[1,64,64,64]{3,2,1,0:T(32,128)(4,1)} %constant.14.clone) | copy-start | bytes 786436
  8.6 116.4 %copy-start.6 = (pred[64,64]{1,0:T(32,128)(4,1)S(1)}, pred[64,64]{1,0:T(32,128)(4,1)}, u32[]{:S(2)}) copy-start(pred[64,64]{1,0:T(32,128)(4,1)} %constant.20) | copy-start | bytes 12292
  8.7 116.4 %copy-start.7 = (pred[64,64]{1,0:T(32,128)(4,1)S(1)}, pred[64,64]{1,0:T(32,128)(4,1)}, u32[]{:S(2)}) copy-start(pred[64,64]{1,0:T(32,128)(4,1)} %constant.22) | copy-start | bytes 12292
  122.2 2.0 copy-start.2
  125.2 2.2 slice-start
  142.9 5.2 %copy-start.5 = (f32[32,256]{1,0:T(8,128)S(1)}, f32[32,256]{1,0:T(8,128)}, u32[]{:S(2)}) copy-start(f32[32,256]{1,0:T(8,128)} %param.12) | copy-start | bytes 98308
  142.9 5.3 %copy-start.3 = (bf16[256,256]{1,0:T(8,128)(2,1)S(1)}, bf16[256,256]{1,0:T(8,128)(2,1)}, u32[]{:S(2)}) copy-start(bf16[256,256]{1,0:T(8,128)(2,1)} %param.14) | copy-start | bytes 393220
  142.9 107.1 %all-to-all-start.1 = ((f32[32,136,256]{2,1,0:T(8,128)}), f32[32,136,256]{2,1,0:T(8,128)}, u32[]{:S(2)}, u32[]{:S(2)}) async-start(f32[32,136,256]{2,1,0:T(8,128)} %pad_maximum_fusion.1), calls=%async_computation.1 | async-start | bytes 8912896 | tf_op jit(solution)/shard_map/all_to_all | solution.py:83
  149.9 1.8 copy-start.8

commit v5 on v2

--- a/solution.py
+++ b/solution.py
@@ -64,10 +64,18 @@
     own = np.zeros((devices, halves, devices, halves), bool)
     own[j, 1, j, 0] = True
     own_gain = jnp.sum(jnp.where(own[None], mixing, 0.0), axis=(3, 4))[:, :, 1]
-    solved = jnp.einsum(
-        "cjkJL,JcLpn->jckpn", jnp.where(own[None], 0.0, mixing), got_states,
-        precision=lax.Precision.HIGHEST, preferred_element_type=jnp.float32,
-    ).reshape(devices * per_chunk, rows, state_size)
+    others = jnp.where(own[None], 0.0, mixing)
+    if per_chunk == 1:
+        solved = jnp.einsum(
+            "uv,vpn->upn", others.reshape(devices * halves, devices * halves),
+            got[:, :rows].reshape(devices * halves, head_width, state_size),
+            precision=lax.Precision.HIGH, preferred_element_type=jnp.float32,
+        ).reshape(devices, rows, state_size)
+    else:
+        solved = jnp.einsum(
+            "cjkJL,JcLpn->jckpn", others, got_states,
+            precision=lax.Precision.HIGH, preferred_element_type=jnp.float32,
+        ).reshape(devices * per_chunk, rows, state_size)
     gain_rows = jnp.broadcast_to(
         jnp.transpose(own_gain).reshape(devices * per_chunk, 1, 1),
         (devices * per_chunk, extra, state_size),

time: 265 us -> 261 us (0.985)
    dot_general x0 -> x1, local copies, waits for them, and re-layouts: none -> 4.36 us  [on_device(): jnp.einsum('uv,vpn->upn', others.reshape(devices * halves, devices * halv...]
    transpose x1 -> x0, local copies, waits for them, and re-layouts: 4.36 us -> none  [on_device(): jnp.einsum('cjkJL,JcLpn->jckpn', jnp.where(own[None], 0.0, mixing), got_s...]
where the time goes in v5:
time: 261 us; the launch traced here: 260 us
  blocking collectives  114 us (44%)
  waiting for transfers between devices  91.3 us (35%)
  local copies, waits for them, and re-layouts  30.3 us (12%)
  other arithmetic  10.5 us (4%)
  matrix products  9.31 us (4%)
  starting transfers between devices  5.16 us (2%)
    all_to_all x1, blocking collectives, on_device(): got = lax.all_to_all(payload, 'ctx', 0, 0, tiled=True)  114 us
    all_to_all x1, waiting for transfers between devices, on_device(): lax.all_to_all(jnp.concatenate([solved, gain_rows], axis=1), 'ctx', 0, 0,...  91.3 us
    convert_element_type x2, local copies, waits for them, and re-layouts, on_device(): weighted = (grouped_inputs * coeffs[..., None]).astype(jnp.bfloat16)  7.03 us
    convert_element_type x2, local copies, waits for them, and re-layouts, on_device(): output_rows.reshape(tok_rows, head_count * head_width).astype(jnp.bfloat16)  5.39 us
  transfers between devices with their start and end apart: 1, of which 1 were waited for; matrix products, arithmetic and copies ran while one was open for 4% of the time, Pallas kernels for 0%

profile of v5, /device:TPU:8, one launch (start us, length us, event | category | flops | bytes accessed | tf_op | source)
XLA Modules:
  0.0 260.4 jit_solution(11368612573790852993)
XLA Ops:
  0.0 0.0 copy-start
  0.0 0.8 copy_bitcast_fusion.1
  0.8 0.6 reduce_window_sum.13
  1.4 0.2 slice_reduce_fusion.1
  1.5 0.8 reshape.153
  2.3 0.1 copy.70
  2.4 0.1 fusion.24
  2.5 1.5 copy.50
  4.0 0.3 reshape.152
  4.3 1.1 multiply_convert_fusion.2
  5.4 0.0 copy-done
  5.4 0.7 convolution_bitcast_fusion
  6.1 0.5 copy.55
  6.6 0.0 copy-start.1
  6.6 0.1 broadcast_in_dim.54
  6.7 0.4 pad_maximum_fusion
  7.1 1.5 copy-done.1
  8.6 0.0 copy-start.6
  8.6 0.0 copy-start.8
  8.7 0.0 copy-start.9
  8.7 113.5 %all_to_all.10 = f32[32,136,256]{2,1,0:T(8,128)S(1)} all-to-all(f32[32,136,256]{2,1,0:T(8,128)S(1)} %pad_maximum_fusion), channel_id=1, replica_groups=mesh['ctx'=32,'head'=8] {'ctx'}, dimensions={0} | all-to-all | bytes 8912896 | tf_op jit(solution)/shard_map/all_to_all | solution.py:56
  122.2 0.0 copy-start.2
  122.2 2.0 copy-done.2
  124.2 0.1 slice_reduce_fusion
  124.3 0.1 broadcast_in_dim.55
  124.4 0.0 copy-done.6
  124.5 0.6 select_reduce_fusion
  125.1 0.0 copy-done.8
  125.1 0.0 copy-done.9
  125.1 0.1 select_reduce_fusion.1
  125.2 0.0 slice-start
  125.2 2.2 slice-done
  127.4 4.2 %fusion = f32[64,64,256]{2,0,1:T(8,128)S(1)} fusion(f32[64,64,256]{2,1,0:T(8,128)S(1)} %bitcast.80, pred[64,64]{1,0:T(32,128)(4,1)S(1)} %copy-done.9, pred[64,64]{1,0:T(32,128)(4,1)S(1)} %copy-done.8, f32[64,64]{1,0:T(8,128)S(1)} %select_reduce_fusion), kind=kOutput, calls=%fused_computation.2 | convolution fusion | flops 402661376 | bytes 8413184 | tf_op jit(solution)/shard_map/uv,vpn->upn/dot_general | solution.py:69
  131.6 4.4 %copy.58 = f32[64,64,256]{2,1,0:T(8,128)} copy(f32[64,64,256]{2,0,1:T(8,128)S(1)} %fusion) | data formatting | bytes 8388608 | tf_op jit(solution)/shard_map/uv,vpn->upn/dot_general | solution.py:69
  136.0 0.1 reduce_sum.22
  136.1 0.2 slice_reduce_fusion.3
  136.3 0.1 broadcast_in_dim.60
  136.4 4.7 %pad_maximum_fusion.1 = f32[32,136,256]{2,1,0:T(8,128)} fusion(f32[32,8,256]{2,1,0:T(8,128)S(1)} %broadcast_in_dim.60, f32[32,128,256]{2,1,0:T(8,128)} %bitcast.81), kind=kLoop, calls=%fused_computation.1 | loop fusion | flops 1114112 | bytes 8912896 | tf_op jit(solution)/shard_map/concatenate | solution.py:83
  141.1 0.0 copy-start.3
  141.1 5.2 %all-to-all-start.1 = ((f32[32,136,256]{2,1,0:T(8,128)}), f32[32,136,256]{2,1,0:T(8,128)}, u32[]{:S(2)}, u32[]{:S(2)}) async-start(f32[32,136,256]{2,1,0:T(8,128)} %pad_maximum_fusion.1), calls=%async_computation.1 | async-start | bytes 8912896 | tf_op jit(solution)/shard_map/all_to_all | solution.py:83
  146.3 0.0 copy-done.3
  146.3 3.2 %reshape.183 = f32[2,128,1,32,64]{4,3,1,0,2:T(8,128)} reshape(bf16[256,2048]{1,0:T(8,128)(2,1)S(1)} %copy-done.3) | data formatting | bytes 3145728 | tf_op jit(solution)/shard_map/convert_element_type | solution.py:46
  149.5 0.0 copy-start.7
  149.5 0.0 copy-start.5
  149.5 3.8 %copy.61 = f32[2,128,1,32,64]{1,4,3,0,2:T(8,128)S(1)} copy(f32[2,128,1,32,64]{4,3,1,0,2:T(8,128)} %reshape.183) | data formatting | bytes 4194304 | tf_op jit(solution)/shard_map/convert_element_type | solution.py:46
  153.4 0.0 copy-done.7
  153.4 0.0 copy-done.5
  153.4 0.2 fusion.29
  153.6 3.4 %fusion.2 = f32[2,32,128,64]{2,3,1,0:T(8,128)} fusion(f32[32,2,128]{2,0,1:T(8,128)S(1)} %copy_bitcast_fusion, f32[32,2,128]{2,0,1:T(8,128)S(1)} %reduce_window_sum.13, f32[2,128,128]{2,1,0:T(8,128)S(1)} %fusion.29, pred[128,128]{1,0:T(8,128)(4,1)S(1)} %iota_compare_fusion, bf16[2,128,32,64]{1,0,3,2:T(2,128)(2,1)S(1)} %reshape.152), kind=kOutput, calls=%fused_computation.6 | convolution fusion | flops 139460608 | bytes 3358720 | tf_op jit(solution)/shard_map/gqkts,ksgqp->ktgqp/dot_general | solution.py:105
  156.9 91.3 %all-to-all-done.1 = f32[32,136,256]{2,1,0:T(8,128)} async-done(((f32[32,136,256]{2,1,0:T(8,128)}), f32[32,136,256]{2,1,0:T(8,128)}, u32[]{:S(2)}, u32[]{:S(2)}) %all-to-all-start.1) | async-done | bytes 4456480 | tf_op jit(solution)/shard_map/all_to_all | solution.py:83
  248.3 1.2 slice_reduce_fusion.2
  249.5 1.7 slice.52
  251.2 0.0 copy-start.4
  251.2 0.0 copy-start.10
  251.3 2.6 %fusion.4 = bf16[32,64,256]{2,1,0:T(8,128)(2,1)S(1)} fusion(f32[32,128,256]{2,1,0:T(8,128)} %bitcast.79, f32[32,136,256]{2,1,0:T(8,128)} %all-to-all-done.1, f32[32]{0:T(128)S(1)} %slice_reduce_fusion.2), kind=kLoop, calls=%fused_computation.9 | loop fusion | flops 1572864 | bytes 5243008 | tf_op jit(solution)/shard_map/convert.2
  253.9 0.2 pad_maximum_fusion.2
  254.1 0.0 copy-done.4
  254.1 0.0 copy-done.10
  254.1 0.8 fusion.7
  255.0 3.0 %copy.68 = bf16[2,128,1,32,64]{4,3,1,0,2:T(8,128)(2,1)S(1)} copy(bf16[2,128,1,32,64]{1,4,3,0,2:T(8,128)(2,1)S(1)} %fusion.7) | data formatting | bytes 2097152 | tf_op jit(solution)/shard_map/convert_element_type | solution.py:116
  258.0 2.4 reshape.184
  (4 shorter events, 0.1 us)
Async XLA Ops:
  0.0 5.4 %copy-start = (bf16[256,256]{1,0:T(8,128)(2,1)S(1)}, bf16[256,256]{1,0:T(8,128)(2,1)}, u32[]{:S(2)}) copy-start(bf16[256,256]{1,0:T(8,128)(2,1)} %param.13) | copy-start | bytes 393220
  6.6 2.1 copy-start.1
  8.6 115.8 %copy-start.6 = (pred[1,64,64,64]{3,2,1,0:T(32,128)(4,1)S(1)}, pred[1,64,64,64]{3,2,1,0:T(32,128)(4,1)}, u32[]{:S(2)}) copy-start(pred[1,64,64,64]{3,2,1,0:T(32,128)(4,1)} %constant.14.clone) | copy-start | bytes 786436
  8.6 116.4 %copy-start.8 = (pred[64,64]{1,0:T(32,128)(4,1)S(1)}, pred[64,64]{1,0:T(32,128)(4,1)}, u32[]{:S(2)}) copy-start(pred[64,64]{1,0:T(32,128)(4,1)} %constant.20) | copy-start | bytes 12292
  8.7 116.4 %copy-start.9 = (pred[64,64]{1,0:T(32,128)(4,1)S(1)}, pred[64,64]{1,0:T(32,128)(4,1)}, u32[]{:S(2)}) copy-start(pred[64,64]{1,0:T(32,128)(4,1)} %constant.22) | copy-start | bytes 12292
  122.2 2.0 copy-start.2
  125.2 2.2 slice-start
  141.1 5.2 %copy-start.3 = (bf16[256,2048]{1,0:T(8,128)(2,1)S(1)}, bf16[256,2048]{1,0:T(8,128)(2,1)}, u32[]{:S(2)}) copy-start(bf16[256,2048]{1,0:T(8,128)(2,1)} %param.10) | copy-start | bytes 3145732
  141.1 107.1 %all-to-all-start.1 = ((f32[32,136,256]{2,1,0:T(8,128)}), f32[32,136,256]{2,1,0:T(8,128)}, u32[]{:S(2)}, u32[]{:S(2)}) async-start(f32[32,136,256]{2,1,0:T(8,128)} %pad_maximum_fusion.1), calls=%async_computation.1 | async-start | bytes 8912896 | tf_op jit(solution)/shard_map/all_to_all | solution.py:83
  149.5 3.8 %copy-start.7 = (f32[32,256]{1,0:T(8,128)S(1)}, f32[32,256]{1,0:T(8,128)}, u32[]{:S(2)}) copy-start(f32[32,256]{1,0:T(8,128)} %param.12) | copy-start | bytes 98308
  149.5 3.9 %copy-start.5 = (bf16[256,256]{1,0:T(8,128)(2,1)S(1)}, bf16[256,256]{1,0:T(8,128)(2,1)}, u32[]{:S(2)}) copy-start(bf16[256,256]{1,0:T(8,128)(2,1)} %param.14) | copy-start | bytes 393220
  251.2 2.9 %copy-start.4 = (f32[2,32,128,64]{2,3,1,0:T(8,128)S(1)}, f32[2,32,128,64]{2,3,1,0:T(8,128)}, u32[]{:S(2)}) copy-start(f32[2,32,128,64]{2,3,1,0:T(8,128)} %fusion.2) | copy-start | bytes 6291460
  251.2 2.9 %copy-start.10 = (f32[32]{0:T(128)S(1)}, f32[32]{0:T(128)}, u32[]{:S(2)}) copy-start(f32[32]{0:T(128)} %param.15) | copy-start | bytes 388

commit v6 on v5

--- a/solution.py
+++ b/solution.py
@@ -47,46 +47,43 @@
     span_states = jnp.einsum(
         "ksgn,ksgqp->gqkpn", b_spans, weighted, preferred_element_type=jnp.float32
     ).reshape(head_count, rows, state_size)
-    tail = jnp.concatenate(
-        [totals, jnp.zeros((head_count, extra - halves), jnp.float32)], axis=1
-    )
+    tail = jnp.zeros((extra, state_size), jnp.float32)
+    tail = tail.at[:halves, :head_count].set(jnp.transpose(totals))
     payload = jnp.concatenate(
-        [span_states, jnp.broadcast_to(tail[:, :, None], (head_count, extra, state_size))], axis=1
+        [span_states, jnp.broadcast_to(tail[None], (head_count, extra, state_size))], axis=1
     )
     got = lax.all_to_all(payload, "ctx", 0, 0, tiled=True)
     got_states = got[:, :rows].reshape(devices, per_chunk, halves, head_width, state_size)
-    got_decay = got[:, rows:rows + halves, 0].reshape(devices, per_chunk, halves)
+    all_decay = got[:, rows:rows + halves, :head_count]
+    me = lax.axis_index("ctx")
+    mine = lax.dynamic_slice_in_dim(all_decay, me * per_chunk, per_chunk, axis=2)
 
     mixing = chain_mixing(
-        jnp.transpose(got_decay, (1, 0, 2)).reshape(per_chunk, devices * halves), devices, halves
+        jnp.transpose(mine, (2, 0, 1)).reshape(per_chunk, devices * halves), devices, halves
     )
     j = np.arange(devices)
     own = np.zeros((devices, halves, devices, halves), bool)
     own[j, 1, j, 0] = True
-    own_gain = jnp.sum(jnp.where(own[None], mixing, 0.0), axis=(3, 4))[:, :, 1]
     others = jnp.where(own[None], 0.0, mixing)
     if per_chunk == 1:
         solved = jnp.einsum(
             "uv,vpn->upn", others.reshape(devices * halves, devices * halves),
             got[:, :rows].reshape(devices * halves, head_width, state_size),
-            precision=lax.Precision.HIGH, preferred_element_type=jnp.float32,
+            precision=lax.Precision.HIGHEST, preferred_element_type=jnp.float32,
         ).reshape(devices, rows, state_size)
     else:
         solved = jnp.einsum(
             "cjkJL,JcLpn->jckpn", others, got_states,
-            precision=lax.Precision.HIGH, preferred_element_type=jnp.float32,
+            precision=lax.Precision.HIGHEST, preferred_element_type=jnp.float32,
         ).reshape(devices * per_chunk, rows, state_size)
-    gain_rows = jnp.broadcast_to(
-        jnp.transpose(own_gain).reshape(devices * per_chunk, 1, 1),
-        (devices * per_chunk, extra, state_size),
-    )
-    back = lax.all_to_all(jnp.concatenate([solved, gain_rows], axis=1), "ctx", 0, 0, tiled=True)
+    back = lax.all_to_all(solved, "ctx", 0, 0, tiled=True)
+    later = (np.arange(devices)[:, None] > me)
+    gain = jnp.exp(jnp.sum(jnp.where(later, jnp.sum(all_decay, axis=1), 0.0), axis=0))
     half_rows = head_width
-    gain = back[:, rows:rows + 1, :1]
     entering = jnp.concatenate(
         [
             back[:, :half_rows],
-            back[:, half_rows:rows] + gain * span_states[:, :half_rows],
+            back[:, half_rows:rows] + gain[:, None, None] * span_states[:, :half_rows],
         ],
         axis=1,
     )

time: 261 us -> 255 us (0.977)
  blocking collectives: 114 us -> 0 us
  waiting for transfers between devices: 91.3 us -> 188 us
  starting transfers between devices: 5.16 us -> 18.8 us
  local copies, waits for them, and re-layouts: 30.3 us -> 27.4 us
    all_to_all x1 -> x0, blocking collectives: 114 us -> none  [on_device(): got = lax.all_to_all(payload, 'ctx', 0, 0, tiled=True)]
    all_to_all x1 -> x2, waiting for transfers between devices: 91.3 us -> 188 us  [the longest x1 102 us: on_device(): got = lax.all_to_all(payload, 'ctx', 0, 0, tiled=True)]
    all_to_all x1 -> x2, starting transfers between devices: 5.16 us -> 18.8 us  [the longest x1 11.7 us: on_device(): got = lax.all_to_all(payload, 'ctx', 0, 0, tiled=True)]
    concatenate x3 -> x2, other arithmetic: 5.36 us -> 2.73 us  [the longest x1 2.52 us: on_device(): jnp.concatenate([span_states, jnp.broadcast_to(tail[None], (head_count, e...]
  transfers between devices with their start and end apart: 1 -> 2, of which waited for: 1 -> 2; matrix products, arithmetic and copies ran while one was open for 4% -> 4% of each run, Pallas kernels for 0% -> 0%
where the time goes in v6:
time: 255 us
  waiting for transfers between devices  188 us (74%)
  local copies, waits for them, and re-layouts  27.4 us (11%)
  starting transfers between devices  18.8 us (7%)
  matrix products  11 us (4%)
  other arithmetic  8.76 us (3%)
    all_to_all x1, waiting for transfers between devices, on_device(): got = lax.all_to_all(payload, 'ctx', 0, 0, tiled=True)  102 us
    all_to_all x1, waiting for transfers between devices, on_device(): back = lax.all_to_all(solved, 'ctx', 0, 0, tiled=True)  86 us
    all_to_all x1, starting transfers between devices, on_device(): got = lax.all_to_all(payload, 'ctx', 0, 0, tiled=True)  11.7 us
    all_to_all x1, starting transfers between devices, on_device(): back = lax.all_to_all(solved, 'ctx', 0, 0, tiled=True)  7.1 us
    convert_element_type x2, local copies, waits for them, and re-layouts, on_device(): weighted = (grouped_inputs * coeffs[..., None]).astype(jnp.bfloat16)  7.04 us
    dot_general x1, matrix products, on_device(): jnp.einsum('uv,vpn->upn', others.reshape(devices * halves, devices * halv...  5.96 us
    convert_element_type x2, local copies, waits for them, and re-layouts, on_device(): output_rows.reshape(tok_rows, head_count * head_width).astype(jnp.bfloat16)  5.39 us
  transfers between devices with their start and end apart: 2, of which 2 were waited for; matrix products, arithmetic and copies ran while one was open for 4% of the time, Pallas kernels for 0%

profile of v6, /device:TPU:8, one launch (start us, length us, event | category | flops | bytes accessed | tf_op | source)
XLA Modules:
  0.0 254.8 jit_solution(14569066816972034831)
XLA Ops:
  0.0 0.0 copy-start
  0.0 0.8 copy_bitcast_fusion.1
  0.8 0.6 reduce_window_sum.13
  1.4 0.2 slice_reduce_fusion
  1.5 0.8 reshape.190
  2.3 0.1 fusion.24
  2.4 1.5 copy.33
  3.9 0.3 reshape.189
  4.2 1.1 multiply_convert_fusion.2
  5.3 0.0 copy-done
  5.3 0.7 convolution_bitcast_fusion
  6.0 0.5 copy.38
  6.5 0.0 copy-start.1
  6.5 1.9 copy-done.1
  8.4 2.5 pad_maximum_fusion
  10.9 0.0 copy-start.5
  11.0 11.7 %all-to-all-start = ((f32[32,136,256]{2,1,0:T(8,128)}), f32[32,136,256]{2,1,0:T(8,128)}, u32[]{:S(2)}, u32[]{:S(2)}) async-start(f32[32,136,256]{2,1,0:T(8,128)} %pad_maximum_fusion), calls=%async_computation | async-start | bytes 8912896 | tf_op jit(solution)/shard_map/all_to_all | solution.py:55
  22.7 102.4 %all-to-all-done = f32[32,136,256]{2,1,0:T(8,128)} async-done(((f32[32,136,256]{2,1,0:T(8,128)}), f32[32,136,256]{2,1,0:T(8,128)}, u32[]{:S(2)}, u32[]{:S(2)}) %all-to-all-start) | async-done | bytes 4456480 | tf_op jit(solution)/shard_map/all_to_all | solution.py:55
  125.1 1.0 slice_reduce_fusion.1
  126.1 0.2 dynamic-slice_reduce_fusion
  126.3 0.1 broadcast_in_dim.64
  126.4 0.0 copy-done.5
  126.4 0.6 select_reduce_fusion
  127.0 0.0 copy-start.7
  127.0 0.0 copy-start.8
  127.0 2.6 %slice.47 = f32[32,128,256]{2,1,0:T(8,128)S(1)} slice(f32[32,136,256]{2,1,0:T(8,128)} %all-to-all-done), slice={[0:32], [0:128], [0:256]} | slice | bytes 8388608 | tf_op jit(solution)/shard_map/slice | solution.py:71
  129.6 0.0 copy-done.7
  129.6 0.0 copy-done.8
  129.6 6.0 %fusion = f32[64,64,256]{2,0,1:T(8,128)S(1)} fusion(f32[64,64,256]{2,1,0:T(8,128)S(1)} %bitcast.84, pred[64,64]{1,0:T(32,128)(4,1)S(1)} %copy-done.8, pred[64,64]{1,0:T(32,128)(4,1)S(1)} %copy-done.7, f32[64,64]{1,0:T(8,128)S(1)} %select_reduce_fusion), kind=kOutput, calls=%fused_computation.1 | convolution fusion | flops 805314560 | bytes 8413184 | tf_op jit(solution)/shard_map/uv,vpn->upn/dot_general | solution.py:69
  135.6 4.4 %copy.40 = f32[64,64,256]{2,1,0:T(8,128)} copy(f32[64,64,256]{2,0,1:T(8,128)S(1)} %fusion) | data formatting | bytes 8388608 | tf_op jit(solution)/shard_map/uv,vpn->upn/dot_general | solution.py:69
  140.0 0.0 copy-start.2
  140.0 7.1 %all-to-all-start.1 = ((f32[32,128,256]{2,1,0:T(8,128)}), f32[32,128,256]{2,1,0:T(8,128)}, u32[]{:S(2)}, u32[]{:S(2)}) async-start(f32[32,128,256]{2,1,0:T(8,128)} %bitcast.83), calls=%async_computation.1 | async-start | bytes 8388608 | tf_op jit(solution)/shard_map/all_to_all | solution.py:79
  147.1 0.0 copy-done.2
  147.1 3.2 %reshape.211 = f32[2,128,1,32,64]{4,3,1,0,2:T(8,128)} reshape(bf16[256,2048]{1,0:T(8,128)(2,1)S(1)} %copy-done.2) | data formatting | bytes 3145728 | tf_op jit(solution)/shard_map/convert_element_type | solution.py:46
  150.3 0.0 copy-start.10
  150.3 0.0 copy-start.6
  150.3 0.0 copy-start.4
  150.3 3.8 %copy.43 = f32[2,128,1,32,64]{1,4,3,0,2:T(8,128)S(1)} copy(f32[2,128,1,32,64]{4,3,1,0,2:T(8,128)} %reshape.211) | data formatting | bytes 4194304 | tf_op jit(solution)/shard_map/convert_element_type | solution.py:46
  154.2 0.0 copy-done.10
  154.2 0.0 copy-done.6
  154.2 0.0 copy-done.4
  154.2 0.2 fusion.31
  154.4 3.3 %fusion.2 = f32[2,32,128,64]{2,3,1,0:T(8,128)} fusion(f32[32,2,128]{2,0,1:T(8,128)S(1)} %copy_bitcast_fusion, f32[32,2,128]{2,0,1:T(8,128)S(1)} %reduce_window_sum.13, f32[2,128,128]{2,1,0:T(8,128)S(1)} %fusion.31, pred[128,128]{1,0:T(8,128)(4,1)S(1)} %iota_compare_fusion, bf16[2,128,32,64]{1,0,3,2:T(2,128)(2,1)S(1)} %reshape.189), kind=kOutput, calls=%fused_computation.5 | convolution fusion | flops 139460608 | bytes 3358720 | tf_op jit(solution)/shard_map/gqkts,ksgqp->ktgqp/dot_general | solution.py:102
  157.8 0.1 select_reduce_fusion.1
  157.9 86.0 %all-to-all-done.1 = f32[32,128,256]{2,1,0:T(8,128)} async-done(((f32[32,128,256]{2,1,0:T(8,128)}), f32[32,128,256]{2,1,0:T(8,128)}, u32[]{:S(2)}, u32[]{:S(2)}) %all-to-all-start.1) | async-done | bytes 4194336 | tf_op jit(solution)/shard_map/all_to_all | solution.py:79
  243.9 1.7 slice.60
  245.6 0.0 copy-start.3
  245.6 0.0 copy-start.9
  245.6 2.6 %fusion.4 = bf16[32,64,256]{2,1,0:T(8,128)(2,1)S(1)} fusion(f32[32,128,256]{2,1,0:T(8,128)} %bitcast.82, f32[32,128,256]{2,1,0:T(8,128)} %all-to-all-done.1, f32[32]{0:T(128)S(1)} %exp.52), kind=kLoop, calls=%fused_computation.8 | loop fusion | flops 1572864 | bytes 5243008 | tf_op jit(solution)/shard_map/convert.2
  248.3 0.2 pad_maximum_fusion.1
  248.5 0.0 copy-done.3
  248.5 0.0 copy-done.9
  248.5 0.8 fusion.7
  249.4 3.0 %copy.50 = bf16[2,128,1,32,64]{4,3,1,0,2:T(8,128)(2,1)S(1)} copy(bf16[2,128,1,32,64]{1,4,3,0,2:T(8,128)(2,1)S(1)} %fusion.7) | data formatting | bytes 2097152 | tf_op jit(solution)/shard_map/convert_element_type | solution.py:113
  252.3 2.4 reshape.212
  (7 shorter events, 0.1 us)
Async XLA Ops:
  0.0 5.3 %copy-start = (bf16[256,256]{1,0:T(8,128)(2,1)S(1)}, bf16[256,256]{1,0:T(8,128)(2,1)}, u32[]{:S(2)}) copy-start(bf16[256,256]{1,0:T(8,128)(2,1)} %param.15) | copy-start | bytes 393220
  6.5 1.9 copy-start.1
  10.9 115.4 %copy-start.5 = (pred[1,64,64,64]{3,2,1,0:T(32,128)(4,1)S(1)}, pred[1,64,64,64]{3,2,1,0:T(32,128)(4,1)}, u32[]{:S(2)}) copy-start(pred[1,64,64,64]{3,2,1,0:T(32,128)(4,1)} %constant.53.clone) | copy-start | bytes 786436
  11.0 114.2 %all-to-all-start = ((f32[32,136,256]{2,1,0:T(8,128)}), f32[32,136,256]{2,1,0:T(8,128)}, u32[]{:S(2)}, u32[]{:S(2)}) async-start(f32[32,136,256]{2,1,0:T(8,128)} %pad_maximum_fusion), calls=%async_computation | async-start | bytes 8912896 | tf_op jit(solution)/shard_map/all_to_all | solution.py:55
  127.0 2.6 %copy-start.7 = (pred[64,64]{1,0:T(32,128)(4,1)S(1)}, pred[64,64]{1,0:T(32,128)(4,1)}, u32[]{:S(2)}) copy-start(pred[64,64]{1,0:T(32,128)(4,1)} %constant.60) | copy-start | bytes 12292
  127.0 2.6 %copy-start.8 = (pred[64,64]{1,0:T(32,128)(4,1)S(1)}, pred[64,64]{1,0:T(32,128)(4,1)}, u32[]{:S(2)}) copy-start(pred[64,64]{1,0:T(32,128)(4,1)} %constant.61) | copy-start | bytes 12292
  140.0 7.1 %copy-start.2 = (bf16[256,2048]{1,0:T(8,128)(2,1)S(1)}, bf16[256,2048]{1,0:T(8,128)(2,1)}, u32[]{:S(2)}) copy-start(bf16[256,2048]{1,0:T(8,128)(2,1)} %param.12) | copy-start | bytes 3145732
  140.0 103.9 %all-to-all-start.1 = ((f32[32,128,256]{2,1,0:T(8,128)}), f32[32,128,256]{2,1,0:T(8,128)}, u32[]{:S(2)}, u32[]{:S(2)}) async-start(f32[32,128,256]{2,1,0:T(8,128)} %bitcast.83), calls=%async_computation.1 | async-start | bytes 8388608 | tf_op jit(solution)/shard_map/all_to_all | solution.py:79
  150.3 3.8 %copy-start.10 = (s32[32,1]{0,1:T(1,128)S(1)}, s32[32,1]{0,1:T(1,128)}, u32[]{:S(2)}) copy-start(s32[32,1]{0,1:T(1,128)} %constant.56.clone) | copy-start | bytes 388
  150.3 3.9 %copy-start.6 = (f32[32,256]{1,0:T(8,128)S(1)}, f32[32,256]{1,0:T(8,128)}, u32[]{:S(2)}) copy-start(f32[32,256]{1,0:T(8,128)} %param.14) | copy-start | bytes 98308
  150.3 3.9 %copy-start.4 = (bf16[256,256]{1,0:T(8,128)(2,1)S(1)}, bf16[256,256]{1,0:T(8,128)(2,1)}, u32[]{:S(2)}) copy-start(bf16[256,256]{1,0:T(8,128)(2,1)} %param.16) | copy-start | bytes 393220
  245.6 2.9 %copy-start.3 = (f32[2,32,128,64]{2,3,1,0:T(8,128)S(1)}, f32[2,32,128,64]{2,3,1,0:T(8,128)}, u32[]{:S(2)}) copy-start(f32[2,32,128,64]{2,3,1,0:T(8,128)} %fusion.2) | copy-start | bytes 6291460
  245.6 2.9 %copy-start.9 = (f32[32]{0:T(128)S(1)}, f32[32]{0:T(128)}, u32[]{:S(2)}) copy-start(f32[32]{0:T(128)} %param.17) | copy-start | bytes 388

commit v7 on v6

--- a/solution.py
+++ b/solution.py
@@ -79,17 +79,11 @@
     back = lax.all_to_all(solved, "ctx", 0, 0, tiled=True)
     later = (np.arange(devices)[:, None] > me)
     gain = jnp.exp(jnp.sum(jnp.where(later, jnp.sum(all_decay, axis=1), 0.0), axis=0))
-    half_rows = head_width
-    entering = jnp.concatenate(
-        [
-            back[:, :half_rows],
-            back[:, half_rows:rows] + gain[:, None, None] * span_states[:, :half_rows],
-        ],
-        axis=1,
-    )
-    state_bf = entering.astype(jnp.bfloat16).reshape(
-        group_count, per_group, halves, head_width, state_size
-    )
+    state_halves = [
+        back[:, :head_width].astype(jnp.bfloat16).reshape(head_count * head_width, state_size),
+        (back[:, head_width:rows] + gain[:, None, None] * span_states[:, :head_width])
+        .astype(jnp.bfloat16).reshape(head_count * head_width, state_size),
+    ]
 
     scores = jnp.einsum("ktgn,ksgn->gkts", c_spans, b_spans, preferred_element_type=jnp.float32)
     causal = jnp.arange(SPAN)[:, None] >= jnp.arange(SPAN)[None, :]
@@ -101,16 +95,26 @@
     )
     diagonal_part = jnp.einsum(
         "gqkts,ksgqp->ktgqp", weights, grouped_inputs, preferred_element_type=jnp.float32
-    )
-    state_part = jnp.einsum(
-        "ktgn,gqkpn->ktgqp", c_spans, state_bf, preferred_element_type=jnp.float32
-    )
-    decay_in = jnp.transpose(jnp.exp(cum_grouped), (2, 3, 0, 1))[..., None]
-    skip = skip_gain.reshape(group_count, per_group)[None, None, :, :, None]
-    output_rows = (
-        diagonal_part + state_part * decay_in + skip * grouped_inputs.astype(jnp.float32)
-    )
-    return output_rows.reshape(tok_rows, head_count * head_width).astype(jnp.bfloat16)
+    ).reshape(halves, SPAN, head_count * head_width)
+    decay_in = jnp.repeat(jnp.transpose(jnp.exp(cumulative), (1, 2, 0)), head_width, axis=2)
+    skip = jnp.repeat(skip_gain, head_width)[None, :]
+    inputs = features.reshape(halves, SPAN, head_count * head_width).astype(jnp.float32)
+    per_group_width = per_group * head_width
+    outs = []
+    for k in range(halves):
+        state_part = jnp.concatenate(
+            [
+                jnp.dot(
+                    c_spans[k, :, g],
+                    state_halves[k][g * per_group_width:(g + 1) * per_group_width].T,
+                    preferred_element_type=jnp.float32,
+                )
+                for g in range(group_count)
+            ],
+            axis=1,
+        )
+        outs.append(diagonal_part[k] + state_part * decay_in[k] + skip * inputs[k])
+    return jnp.concatenate(outs, axis=0).astype(jnp.bfloat16)
 
 
 def solution(mesh):

time: 255 us -> 251 us (0.984)
  local copies, waits for them, and re-layouts: 27.4 us -> 23.2 us
    convert_element_type x4 -> x0, local copies, waits for them, and re-layouts: 12.4 us -> none  [the longest x2 7.04 us: on_device(): weighted = (grouped_inputs * coeffs[..., None]).astype(jnp.bfloat16)]
    squeeze x0 -> x2, local copies, waits for them, and re-layouts: none -> 3.91 us  [on_device(): outs.append(diagonal_part[k] + state_part * decay_in[k] + skip * inputs[k])]
    broadcast_in_dim x0 -> x5, local copies, waits for them, and re-layouts: none -> 2.84 us  [the longest x4 2.77 us: on_device(): jnp.repeat(jnp.transpose(jnp.exp(cumulative), (1, 2, 0)), head_width, axi...]
    convert_element_type x0 -> x2, other arithmetic: none -> 2.81 us  [the longest x1 2.58 us: on_device(): state_halves = [back[:, :head_width].astype(jnp.bfloat16).reshape(head_co...]
    another operation x1 -> x0, other arithmetic: 2.64 us -> none
  transfers between devices with their start and end apart: 2 -> 2, of which waited for: 2 -> 2; matrix products, arithmetic and copies ran while one was open for 4% -> 5% of each run, Pallas kernels for 0% -> 0%
where the time goes in v7:
time: 251 us
  waiting for transfers between devices  187 us (75%)
  local copies, waits for them, and re-layouts  23.2 us (9%)
  starting transfers between devices  18.8 us (7%)
  matrix products  11.4 us (5%)
  other arithmetic  9.79 us (4%)
    all_to_all x1, waiting for transfers between devices, on_device(): got = lax.all_to_all(payload, 'ctx', 0, 0, tiled=True)  102 us
    all_to_all x1, waiting for transfers between devices, on_device(): back = lax.all_to_all(solved, 'ctx', 0, 0, tiled=True)  84.6 us
    all_to_all x1, starting transfers between devices, on_device(): got = lax.all_to_all(payload, 'ctx', 0, 0, tiled=True)  11.7 us
    all_to_all x1, starting transfers between devices, on_device(): back = lax.all_to_all(solved, 'ctx', 0, 0, tiled=True)  7.05 us
    dot_general x1, matrix products, on_device(): jnp.einsum('uv,vpn->upn', others.reshape(devices * halves, devices * halv...  5.96 us
  transfers between devices with their start and end apart: 2, of which 2 were waited for; matrix products, arithmetic and copies ran while one was open for 5% of the time, Pallas kernels for 0%

profile of v7, /device:TPU:8, one launch (start us, length us, event | category | flops | bytes accessed | tf_op | source)
XLA Modules:
  0.0 250.6 jit_solution(7968361085813930948)
XLA Ops:
  0.0 0.0 copy-start
  0.0 0.8 copy_bitcast_fusion.1
  0.8 0.6 reduce_window_sum.13
  1.4 0.2 slice_reduce_fusion
  1.5 0.8 reshape.180
  2.3 0.1 fusion.27
  2.4 1.5 copy.36
  3.9 0.3 reshape.179
  4.2 0.0 copy-start.3
  4.2 1.1 multiply_convert_fusion.2
  5.3 0.0 copy-done
  5.3 0.7 convolution_bitcast_fusion.2
  6.0 0.5 copy.41
  6.5 0.0 copy-done.3
  6.5 0.0 copy-start.1
  6.6 1.9 copy-done.1
  8.5 2.5 %pad_maximum_fusion = f32[32,136,256]{2,1,0:T(8,128)} fusion(f32[32,8,256]{2,1,0:T(8,128)S(1)} %broadcast_in_dim.74, f32[32,128,256]{2,1,0:T(8,128)S(1)} %bitcast.88), kind=kLoop, calls=%fused_computation | loop fusion | flops 1114112 | bytes 8912896 | tf_op jit(solution)/shard_map/concatenate | solution.py:52
  11.0 11.7 %all-to-all-start = ((f32[32,136,256]{2,1,0:T(8,128)}), f32[32,136,256]{2,1,0:T(8,128)}, u32[]{:S(2)}, u32[]{:S(2)}) async-start(f32[32,136,256]{2,1,0:T(8,128)} %pad_maximum_fusion), calls=%async_computation | async-start | bytes 8912896 | tf_op jit(solution)/shard_map/all_to_all | solution.py:55
  22.7 102.4 %all-to-all-done = f32[32,136,256]{2,1,0:T(8,128)} async-done(((f32[32,136,256]{2,1,0:T(8,128)}), f32[32,136,256]{2,1,0:T(8,128)}, u32[]{:S(2)}, u32[]{:S(2)}) %all-to-all-start) | async-done | bytes 4456480 | tf_op jit(solution)/shard_map/all_to_all | solution.py:55
  125.2 1.0 slice_reduce_fusion.1
  126.1 0.2 dynamic-slice_reduce_fusion
  126.3 0.1 broadcast_in_dim.75
  126.4 0.0 copy-done.9
  126.4 0.6 select_reduce_fusion
  127.0 0.0 copy-start.11
  127.1 0.0 copy-start.12
  127.1 2.6 %slice.96 = f32[32,128,256]{2,1,0:T(8,128)S(1)} slice(f32[32,136,256]{2,1,0:T(8,128)} %all-to-all-done), slice={[0:32], [0:128], [0:256]} | slice | bytes 8388608 | tf_op jit(solution)/shard_map/slice | solution.py:71
  129.6 0.0 copy-done.11
  129.6 0.0 copy-done.12
  129.7 6.0 %fusion = f32[64,64,256]{2,0,1:T(8,128)S(1)} fusion(f32[64,64,256]{2,1,0:T(8,128)S(1)} %bitcast.91, pred[64,64]{1,0:T(32,128)(4,1)S(1)} %copy-done.12, pred[64,64]{1,0:T(32,128)(4,1)S(1)} %copy-done.11, f32[64,64]{1,0:T(8,128)S(1)} %select_reduce_fusion), kind=kOutput, calls=%fused_computation.1 | convolution fusion | flops 805314560 | bytes 8413184 | tf_op jit(solution)/shard_map/uv,vpn->upn/dot_general | solution.py:69
  135.6 4.5 %copy.43 = f32[64,64,256]{2,1,0:T(8,128)} copy(f32[64,64,256]{2,0,1:T(8,128)S(1)} %fusion) | data formatting | bytes 8388608 | tf_op jit(solution)/shard_map/uv,vpn->upn/dot_general | solution.py:69
  140.1 7.0 %all-to-all-start.1 = ((f32[32,128,256]{2,1,0:T(8,128)}), f32[32,128,256]{2,1,0:T(8,128)}, u32[]{:S(2)}, u32[]{:S(2)}) async-start(f32[32,128,256]{2,1,0:T(8,128)} %bitcast.90), calls=%async_computation.1 | async-start | bytes 8388608 | tf_op jit(solution)/shard_map/all_to_all | solution.py:79
  147.2 0.0 copy-done.2
  147.2 0.2 convert_element_type.30
  147.5 0.0 copy-done.10
  147.5 0.0 copy-done.8
  147.5 0.2 fusion.35
  147.7 3.6 %fusion.19 = f32[2,128,1,32,64]{1,4,3,0,2:T(8,128)S(1)} fusion(f32[32,2,128]{2,0,1:T(8,128)S(1)} %copy_bitcast_fusion, f32[32,2,128]{2,0,1:T(8,128)S(1)} %reduce_window_sum.13, f32[2,128,128]{2,1,0:T(8,128)S(1)} %fusion.35, pred[128,128]{1,0:T(8,128)(4,1)S(1)} %iota_compare_fusion, bf16[2,128,32,64]{1,0,3,2:T(2,128)(2,1)} %copy-done.3), kind=kOutput, calls=%fused_computation.28 | convolution fusion | flops 139460608 | bytes 3358720 | tf_op jit(solution)/shard_map/gqkts,ksgqp->ktgqp/dot_general | solution.py:96
  151.3 0.0 copy-start.13
  151.3 1.2 fusion.34
  152.4 1.3 copy.47
  153.8 0.0 copy-start.14
  153.8 0.1 broadcast_in_dim.85
  153.9 1.3 copy.46
  155.2 0.0 copy-done.13
  155.2 0.1 broadcast_in_dim.81
  155.3 0.1 mul.87
  155.3 2.6 %copy.45 = f32[128,2048]{1,0:T(8,128)} copy(f32[128,2048]{0,1:T(8,128)} %bitcast.94) | data formatting | bytes 2097152 | tf_op jit(solution)/shard_map/squeeze | solution.py:116
  157.9 0.1 broadcast_in_dim.79
  158.0 1.3 copy.44
  159.3 0.0 copy-done.14
  159.3 0.1 select_reduce_fusion.1
  159.4 84.6 %all-to-all-done.1 = f32[32,128,256]{2,1,0:T(8,128)} async-done(((f32[32,128,256]{2,1,0:T(8,128)}), f32[32,128,256]{2,1,0:T(8,128)}, u32[]{:S(2)}, u32[]{:S(2)}) %all-to-all-start.1) | async-done | bytes 4194336 | tf_op jit(solution)/shard_map/all_to_all | solution.py:79
  244.0 2.6 %fusion.12 = bf16[32,64,256]{2,1,0:T(8,128)(2,1)S(1)} fusion(f32[32,128,256]{2,1,0:T(8,128)} %bitcast.89, f32[32,128,256]{2,1,0:T(8,128)} %all-to-all-done.1, f32[32]{0:T(128)S(1)} %exp.50), kind=kLoop, calls=%fused_computation.18 | loop fusion | flops 1572864 | bytes 5243008 | tf_op jit(solution)/shard_map/convert_element_type | solution.py:85
  246.6 0.0 copy-start.5
  246.6 0.0 copy-start.7
  246.6 0.0 copy-done.4
  246.6 0.0 copy-done.6
  246.6 0.5 fusion.8
  247.2 1.8 slice.126
  249.0 0.0 copy-done.5
  249.0 0.0 copy-done.7
  249.0 0.5 fusion.9
  249.5 1.1 pad_maximum_fusion.1
  (15 shorter events, 0.1 us)
Async XLA Ops:
  0.0 5.3 %copy-start = (bf16[256,256]{1,0:T(8,128)(2,1)S(1)}, bf16[256,256]{1,0:T(8,128)(2,1)}, u32[]{:S(2)}) copy-start(bf16[256,256]{1,0:T(8,128)(2,1)} %param.15) | copy-start | bytes 393220
  4.2 2.3 copy-start.3
  6.5 1.9 copy-start.1
  11.0 115.4 %copy-start.9 = (pred[1,64,64,64]{3,2,1,0:T(32,128)(4,1)S(1)}, pred[1,64,64,64]{3,2,1,0:T(32,128)(4,1)}, u32[]{:S(2)}) copy-start(pred[1,64,64,64]{3,2,1,0:T(32,128)(4,1)} %constant.53.clone) | copy-start | bytes 786436
  11.0 114.2 %all-to-all-start = ((f32[32,136,256]{2,1,0:T(8,128)}), f32[32,136,256]{2,1,0:T(8,128)}, u32[]{:S(2)}, u32[]{:S(2)}) async-start(f32[32,136,256]{2,1,0:T(8,128)} %pad_maximum_fusion), calls=%async_computation | async-start | bytes 8912896 | tf_op jit(solution)/shard_map/all_to_all | solution.py:55
  127.0 2.6 %copy-start.11 = (pred[64,64]{1,0:T(32,128)(4,1)S(1)}, pred[64,64]{1,0:T(32,128)(4,1)}, u32[]{:S(2)}) copy-start(pred[64,64]{1,0:T(32,128)(4,1)} %constant.60) | copy-start | bytes 12292
  127.1 2.6 %copy-start.12 = (pred[64,64]{1,0:T(32,128)(4,1)S(1)}, pred[64,64]{1,0:T(32,128)(4,1)}, u32[]{:S(2)}) copy-start(pred[64,64]{1,0:T(32,128)(4,1)} %constant.61) | copy-start | bytes 12292
  140.1 7.1 %copy-start.2 = (bf16[256,2048]{1,0:T(8,128)(2,1)S(1)}, bf16[256,2048]{1,0:T(8,128)(2,1)}, u32[]{:S(2)}) copy-start(bf16[256,2048]{1,0:T(8,128)(2,1)} %param.12) | copy-start | bytes 3145732
  140.1 7.3 %copy-start.10 = (f32[32,256]{1,0:T(8,128)S(1)}, f32[32,256]{1,0:T(8,128)}, u32[]{:S(2)}) copy-start(f32[32,256]{1,0:T(8,128)} %param.14) | copy-start | bytes 98308
  140.1 7.4 %copy-start.8 = (bf16[256,256]{1,0:T(8,128)(2,1)S(1)}, bf16[256,256]{1,0:T(8,128)(2,1)}, u32[]{:S(2)}) copy-start(bf16[256,256]{1,0:T(8,128)(2,1)} %param.16) | copy-start | bytes 393220
  140.1 103.9 %all-to-all-start.1 = ((f32[32,128,256]{2,1,0:T(8,128)}), f32[32,128,256]{2,1,0:T(8,128)}, u32[]{:S(2)}, u32[]{:S(2)}) async-start(f32[32,128,256]{2,1,0:T(8,128)} %bitcast.90), calls=%async_computation.1 | async-start | bytes 8388608 | tf_op jit(solution)/shard_map/all_to_all | solution.py:79
  151.3 3.9 %copy-start.13 = (f32[32]{0:T(128)S(1)}, f32[32]{0:T(128)}, u32[]{:S(2)}) copy-start(f32[32]{0:T(128)} %param.17) | copy-start | bytes 388
  153.8 5.6 %copy-start.14 = (s32[32,1]{0,1:T(1,128)S(1)}, s32[32,1]{0,1:T(1,128)}, u32[]{:S(2)}) copy-start(s32[32,1]{0,1:T(1,128)} %constant.56.clone) | copy-start | bytes 388
  159.3 87.3 %copy-start.4 = (f32[128,2048]{1,0:T(8,128)S(1)}, f32[128,2048]{1,0:T(8,128)}, u32[]{:S(2)}) copy-start(f32[128,2048]{1,0:T(8,128)} %copy.47) | copy-start | bytes 3145732
  244.0 2.6 %copy-start.6 = (f32[128,2048]{1,0:T(8,128)S(1)}, f32[128,2048]{1,0:T(8,128)}, u32[]{:S(2)}) copy-start(f32[128,2048]{1,0:T(8,128)} %copy.46) | copy-start | bytes 3145732
  246.6 2.4 copy-start.5
  246.6 2.4 copy-start.7

commit v8 on v7

--- a/solution.py
+++ b/solution.py
@@ -47,15 +47,12 @@
     span_states = jnp.einsum(
         "ksgn,ksgqp->gqkpn", b_spans, weighted, preferred_element_type=jnp.float32
     ).reshape(head_count, rows, state_size)
-    tail = jnp.zeros((extra, state_size), jnp.float32)
-    tail = tail.at[:halves, :head_count].set(jnp.transpose(totals))
-    payload = jnp.concatenate(
-        [span_states, jnp.broadcast_to(tail[None], (head_count, extra, state_size))], axis=1
-    )
-    got = lax.all_to_all(payload, "ctx", 0, 0, tiled=True)
-    got_states = got[:, :rows].reshape(devices, per_chunk, halves, head_width, state_size)
-    all_decay = got[:, rows:rows + halves, :head_count]
     me = lax.axis_index("ctx")
+    spread = jnp.zeros((devices, halves, head_count), jnp.float32)
+    spread = lax.dynamic_update_slice_in_dim(spread, jnp.transpose(totals)[None], me, axis=0)
+    all_decay = lax.psum(spread, "ctx")
+    got = lax.all_to_all(span_states, "ctx", 0, 0, tiled=True)
+    got_states = got.reshape(devices, per_chunk, halves, head_width, state_size)
     mine = lax.dynamic_slice_in_dim(all_decay, me * per_chunk, per_chunk, axis=2)
 
     mixing = chain_mixing(
@@ -68,7 +65,7 @@
     if per_chunk == 1:
         solved = jnp.einsum(
             "uv,vpn->upn", others.reshape(devices * halves, devices * halves),
-            got[:, :rows].reshape(devices * halves, head_width, state_size),
+            got.reshape(devices * halves, head_width, state_size),
             precision=lax.Precision.HIGHEST, preferred_element_type=jnp.float32,
         ).reshape(devices, rows, state_size)
     else:

time: 251 us -> 345 us (1.37)
  blocking collectives: 0 us -> 233 us
  waiting for transfers between devices: 187 us -> 53.5 us
    psum x0 -> x1, blocking collectives: none -> 233 us  [on_device(): all_decay = lax.psum(spread, 'ctx')]
    all_to_all x1, waiting for transfers between devices: 102 us -> 0.01 us  [on_device(): got = lax.all_to_all(span_states, 'ctx', 0, 0, tiled=True)]
    all_to_all x1, waiting for transfers between devices: 84.6 us -> 53.5 us  [on_device(): back = lax.all_to_all(solved, 'ctx', 0, 0, tiled=True)]
  transfers between devices with their start and end apart: 2 -> 2, of which waited for: 2 -> 1; matrix products, arithmetic and copies ran while one was open for 5% -> 4% of each run, Pallas kernels for 0% -> 0%
where the time goes in v8:
time: 345 us; the launch traced here: 344 us
  blocking collectives  233 us (68%)
  waiting for transfers between devices  53.5 us (16%)
  local copies, waits for them, and re-layouts  20.4 us (6%)
  starting transfers between devices  16.8 us (5%)
  matrix products  13.9 us (4%)
  other arithmetic  6.54 us (2%)
    psum x1, blocking collectives, on_device(): all_decay = lax.psum(spread, 'ctx')  233 us
    all_to_all x1, waiting for transfers between devices, on_device(): back = lax.all_to_all(solved, 'ctx', 0, 0, tiled=True)  53.5 us
    all_to_all x1, starting transfers between devices, on_device(): got = lax.all_to_all(span_states, 'ctx', 0, 0, tiled=True)  11.6 us
    dot_general x1, matrix products, on_device(): jnp.einsum('uv,vpn->upn', others.reshape(devices * halves, devices * halv...  8.4 us
  transfers between devices with their start and end apart: 2, of which 1 were waited for; matrix products, arithmetic and copies ran while one was open for 4% of the time, Pallas kernels for 0%

profile of v8, /device:TPU:8, one launch (start us, length us, event | category | flops | bytes accessed | tf_op | source)
XLA Modules:
  0.0 344.3 jit_solution(12947823522675433255)
XLA Ops:
  0.0 0.0 copy-start
  0.0 0.8 copy_bitcast_fusion.1
  0.8 0.6 reduce_window_sum.13
  1.4 0.2 slice_reduce_fusion
  1.5 0.8 reshape.145
  2.3 0.1 fusion.26
  2.4 1.5 copy.52
  3.9 0.3 reshape.142
  4.2 0.0 copy-start.2
  4.2 1.1 multiply_convert_fusion.2
  5.3 0.0 copy-done
  5.3 0.7 convolution_bitcast_fusion.2
  6.0 2.2 copy.58
  8.2 0.0 copy-done.2
  8.3 0.0 copy-start.10
  8.3 0.0 copy-start.11
  8.3 11.6 %all-to-all-start = ((f32[32,128,256]{2,1,0:T(8,128)}), f32[32,128,256]{2,1,0:T(8,128)}, u32[]{:S(2)}, u32[]{:S(2)}) async-start(f32[32,128,256]{2,1,0:T(8,128)} %bitcast.92), calls=%async_computation | async-start | bytes 8388608 | tf_op jit(solution)/shard_map/all_to_all | solution.py:54
  19.9 0.1 copy.54
  20.0 0.1 dynamic_update_slice.3
  20.1 232.9 %psum.7 = f32[32,2,32]{1,0,2:T(8,128)S(1)} all-reduce(f32[32,2,32]{1,0,2:T(8,128)S(1)} %dynamic_update_slice.3), channel_id=1, replica_groups=mesh['ctx'=32,'head'=8] {'ctx'}, use_global_device_ids=true, to_apply=%region_1.2 | all-reduce | flops 2048 | bytes 16384 | tf_op jit(solution)/shard_map/psum | solution.py:53
  253.0 0.1 broadcast_in_dim.72
  253.1 0.0 copy-done.8
  253.1 0.6 select_reduce_fusion
  253.7 0.0 all-to-all-done
  253.8 0.0 copy-done.10
  253.8 0.0 copy-done.11
  253.8 8.4 %fusion = f32[64,64,256]{2,0,1:T(8,128)S(1)} fusion(f32[64,64,256]{2,1,0:T(8,128)} %bitcast.17, pred[64,64]{1,0:T(32,128)(4,1)S(1)} %copy-done.11, pred[64,64]{1,0:T(32,128)(4,1)S(1)} %copy-done.10, f32[64,64]{1,0:T(8,128)S(1)} %select_reduce_fusion), kind=kOutput, calls=%fused_computation | convolution fusion | flops 805314560 | bytes 8413184 | tf_op jit(solution)/shard_map/uv,vpn->upn/dot_general | solution.py:66
  262.2 4.4 %copy.60 = f32[64,64,256]{2,1,0:T(8,128)} copy(f32[64,64,256]{2,0,1:T(8,128)S(1)} %fusion) | data formatting | bytes 8388608 | tf_op jit(solution)/shard_map/uv,vpn->upn/dot_general | solution.py:66
  266.6 0.0 copy-start.1
  266.6 0.0 copy-start.13
  266.6 0.0 copy-start.9
  266.6 5.2 %all-to-all-start.1 = ((f32[32,128,256]{2,1,0:T(8,128)}), f32[32,128,256]{2,1,0:T(8,128)}, u32[]{:S(2)}, u32[]{:S(2)}) async-start(f32[32,128,256]{2,1,0:T(8,128)} %bitcast.94), calls=%async_computation.1 | async-start | bytes 8388608 | tf_op jit(solution)/shard_map/all_to_all | solution.py:76
  271.8 0.2 reduce_sum.28
  272.0 0.0 copy-done.1
  272.0 0.2 convert_element_type.30
  272.2 0.0 copy-done.13
  272.3 0.1 select_reduce_fusion.1
  272.4 0.0 copy-done.9
  272.4 0.0 copy-done.7
  272.4 0.2 fusion.35
  272.6 3.6 %fusion.19 = f32[2,128,1,32,64]{1,4,3,0,2:T(8,128)S(1)} fusion(f32[32,2,128]{2,0,1:T(8,128)S(1)} %copy_bitcast_fusion, f32[32,2,128]{2,0,1:T(8,128)S(1)} %reduce_window_sum.13, f32[2,128,128]{2,1,0:T(8,128)S(1)} %fusion.35, pred[128,128]{1,0:T(8,128)(4,1)S(1)} %iota_compare_fusion, bf16[2,128,32,64]{1,0,3,2:T(2,128)(2,1)} %copy-done.2), kind=kOutput, calls=%fused_computation.27 | convolution fusion | flops 139460608 | bytes 3358720 | tf_op jit(solution)/shard_map/gqkts,ksgqp->ktgqp/dot_general | solution.py:93
  276.2 0.0 copy-start.12
  276.2 1.2 fusion.34
  277.4 1.3 copy.64
  278.7 0.1 broadcast_in_dim.82
  278.8 1.3 copy.63
  280.2 0.0 copy-done.12
  280.2 0.1 broadcast_in_dim.78
  280.2 0.1 mul.87
  280.3 2.6 copy.62
  282.9 0.1 broadcast_in_dim.76
  283.0 1.3 copy.61
  284.3 53.5 %all-to-all-done.1 = f32[32,128,256]{2,1,0:T(8,128)} async-done(((f32[32,128,256]{2,1,0:T(8,128)}), f32[32,128,256]{2,1,0:T(8,128)}, u32[]{:S(2)}, u32[]{:S(2)}) %all-to-all-start.1) | async-done | bytes 4194336 | tf_op jit(solution)/shard_map/all_to_all | solution.py:76
  337.8 2.6 fusion.12
  340.4 0.0 copy-start.4
  340.4 0.0 copy-start.6
  340.4 0.0 copy-done.3
  340.4 0.0 copy-done.5
  340.4 0.5 fusion.8
  340.9 1.8 slice.95
  342.7 0.0 copy-done.4
  342.7 0.0 copy-done.6
  342.7 0.5 fusion.9
  343.3 1.1 pad_maximum_fusion
  (13 shorter events, 0.1 us)
Async XLA Ops:
  0.0 5.3 %copy-start = (bf16[256,256]{1,0:T(8,128)(2,1)S(1)}, bf16[256,256]{1,0:T(8,128)(2,1)}, u32[]{:S(2)}) copy-start(bf16[256,256]{1,0:T(8,128)(2,1)} %param.13) | copy-start | bytes 393220
  4.2 4.0 %copy-start.2 = (bf16[2,128,32,64]{1,0,3,2:T(2,128)(2,1)}, bf16[2,128,32,64]{1,0,3,2:T(2,128)(2,1)S(1)}, u32[]{:S(2)}) copy-start(bf16[2,128,32,64]{1,0,3,2:T(2,128)(2,1)S(1)} %reshape.142) | copy-start | bytes 3145732
  8.3 244.9 %copy-start.8 = (pred[1,64,64,64]{3,2,1,0:T(32,128)(4,1)S(1)}, pred[1,64,64,64]{3,2,1,0:T(32,128)(4,1)}, u32[]{:S(2)}) copy-start(pred[1,64,64,64]{3,2,1,0:T(32,128)(4,1)} %constant.26.clone) | copy-start | bytes 786436
  8.3 245.5 %copy-start.10 = (pred[64,64]{1,0:T(32,128)(4,1)S(1)}, pred[64,64]{1,0:T(32,128)(4,1)}, u32[]{:S(2)}) copy-start(pred[64,64]{1,0:T(32,128)(4,1)} %constant.31) | copy-start | bytes 12292
  8.3 245.5 %copy-start.11 = (pred[64,64]{1,0:T(32,128)(4,1)S(1)}, pred[64,64]{1,0:T(32,128)(4,1)}, u32[]{:S(2)}) copy-start(pred[64,64]{1,0:T(32,128)(4,1)} %constant.32) | copy-start | bytes 12292
  8.3 245.5 %all-to-all-start = ((f32[32,128,256]{2,1,0:T(8,128)}), f32[32,128,256]{2,1,0:T(8,128)}, u32[]{:S(2)}, u32[]{:S(2)}) async-start(f32[32,128,256]{2,1,0:T(8,128)} %bitcast.92), calls=%async_computation | async-start | bytes 8388608 | tf_op jit(solution)/shard_map/all_to_all | solution.py:54
  266.6 5.4 %copy-start.1 = (bf16[256,2048]{1,0:T(8,128)(2,1)S(1)}, bf16[256,2048]{1,0:T(8,128)(2,1)}, u32[]{:S(2)}) copy-start(bf16[256,2048]{1,0:T(8,128)(2,1)} %param.10) | copy-start | bytes 3145732
  266.6 5.7 %copy-start.13 = (s32[32,1]{0,1:T(1,128)S(1)}, s32[32,1]{0,1:T(1,128)}, u32[]{:S(2)}) copy-start(s32[32,1]{0,1:T(1,128)} %constant.29.clone) | copy-start | bytes 388
  266.6 5.8 %copy-start.9 = (f32[32,256]{1,0:T(8,128)S(1)}, f32[32,256]{1,0:T(8,128)}, u32[]{:S(2)}) copy-start(f32[32,256]{1,0:T(8,128)} %param.12) | copy-start | bytes 98308
  266.6 5.9 %copy-start.7 = (bf16[256,256]{1,0:T(8,128)(2,1)S(1)}, bf16[256,256]{1,0:T(8,128)(2,1)}, u32[]{:S(2)}) copy-start(bf16[256,256]{1,0:T(8,128)(2,1)} %param.14) | copy-start | bytes 393220
  266.6 71.2 %all-to-all-start.1 = ((f32[32,128,256]{2,1,0:T(8,128)}), f32[32,128,256]{2,1,0:T(8,128)}, u32[]{:S(2)}, u32[]{:S(2)}) async-start(f32[32,128,256]{2,1,0:T(8,128)} %bitcast.94), calls=%async_computation.1 | async-start | bytes 8388608 | tf_op jit(solution)/shard_map/all_to_all | solution.py:76
  276.2 3.9 %copy-start.12 = (f32[32]{0:T(128)S(1)}, f32[32]{0:T(128)}, u32[]{:S(2)}) copy-start(f32[32]{0:T(128)} %param.15) | copy-start | bytes 388
  284.3 56.1 %copy-start.3 = (f32[128,2048]{1,0:T(8,128)S(1)}, f32[128,2048]{1,0:T(8,128)}, u32[]{:S(2)}) copy-start(f32[128,2048]{1,0:T(8,128)} %copy.64) | copy-start | bytes 3145732
  337.8 2.6 copy-start.5
  340.4 2.4 copy-start.4
  340.4 2.4 copy-start.6

commit v9 on v7

--- a/solution.py
+++ b/solution.py
@@ -79,9 +79,12 @@
     back = lax.all_to_all(solved, "ctx", 0, 0, tiled=True)
     later = (np.arange(devices)[:, None] > me)
     gain = jnp.exp(jnp.sum(jnp.where(later, jnp.sum(all_decay, axis=1), 0.0), axis=0))
+    own_front = jnp.einsum(
+        "sgn,sgqp->gqpn", b_spans[0], weighted[0], preferred_element_type=jnp.float32
+    ).reshape(head_count, head_width, state_size)
     state_halves = [
         back[:, :head_width].astype(jnp.bfloat16).reshape(head_count * head_width, state_size),
-        (back[:, head_width:rows] + gain[:, None, None] * span_states[:, :head_width])
+        (back[:, head_width:rows] + gain[:, None, None] * own_front)
         .astype(jnp.bfloat16).reshape(head_count * head_width, state_size),
     ]
 

time: 251 us -> 249 us (level)
  waiting for transfers between devices: 187 us -> 181 us
  local copies, waits for them, and re-layouts: 23.2 us -> 27.5 us
    all_to_all x1, waiting for transfers between devices: 84.6 us -> 78.8 us  [on_device(): back = lax.all_to_all(solved, 'ctx', 0, 0, tiled=True)]
    convert_element_type x0 -> x1, local copies, waits for them, and re-layouts: none -> 3.22 us  [on_device(): weighted = (grouped_inputs * coeffs[..., None]).astype(jnp.bfloat16)]
    convert_element_type x1 -> x0, other arithmetic: 2.58 us -> none  [on_device(): state_halves = [back[:, :head_width].astype(jnp.bfloat16).reshape(head_co...]
  transfers between devices with their start and end apart: 2 -> 2, of which waited for: 2 -> 2; matrix products, arithmetic and copies ran while one was open for 5% -> 7% of each run, Pallas kernels for 0% -> 0%
where the time goes in v9:
time: 249 us; the launch traced here: 248 us
  waiting for transfers between devices  181 us (73%)
  local copies, waits for them, and re-layouts  27.5 us (11%)
  starting transfers between devices  18.8 us (8%)
  matrix products  11.6 us (5%)
  other arithmetic  8.58 us (3%)
    all_to_all x1, waiting for transfers between devices, on_device(): got = lax.all_to_all(payload, 'ctx', 0, 0, tiled=True)  102 us
    all_to_all x1, waiting for transfers between devices, on_device(): back = lax.all_to_all(solved, 'ctx', 0, 0, tiled=True)  78.8 us
    all_to_all x1, starting transfers between devices, on_device(): got = lax.all_to_all(payload, 'ctx', 0, 0, tiled=True)  11.7 us
    all_to_all x1, starting transfers between devices, on_device(): back = lax.all_to_all(solved, 'ctx', 0, 0, tiled=True)  7.05 us
    dot_general x1, matrix products, on_device(): jnp.einsum('uv,vpn->upn', others.reshape(devices * halves, devices * halv...  5.96 us
    broadcast_in_dim x4, local copies, waits for them, and re-layouts, on_device(): jnp.repeat(jnp.transpose(jnp.exp(cumulative), (1, 2, 0)), head_width, axi...  4.99 us
  transfers between devices with their start and end apart: 2, of which 2 were waited for; matrix products, arithmetic and copies ran while one was open for 7% of the time, Pallas kernels for 0%

profile of v9, /device:TPU:8, one launch (start us, length us, event | category | flops | bytes accessed | tf_op | source)
XLA Modules:
  0.0 248.2 jit_solution(7148186267528790909)
XLA Ops:
  0.0 0.0 copy-start
  0.0 0.8 copy-done
  0.8 0.6 reduce_window_sum.13
  1.3 0.2 slice_reduce_fusion
  1.5 0.8 reshape.208
  2.3 0.1 fusion.31
  2.4 0.0 copy-start.13
  2.4 1.5 copy.39
  3.9 0.3 reshape.207
  4.2 0.0 copy-start.4
  4.2 1.1 multiply_convert_fusion.2
  5.3 0.0 copy-done.10
  5.3 0.7 convolution_bitcast_fusion.2
  6.0 0.5 copy.44
  6.5 0.0 copy-done.4
  6.5 2.6 %pad_maximum_fusion = f32[32,136,256]{2,1,0:T(8,128)} fusion(f32[32,8,256]{2,1,0:T(8,128)S(1)} %broadcast_in_dim.74, f32[32,128,256]{2,1,0:T(8,128)S(1)} %bitcast.93), kind=kLoop, calls=%fused_computation | loop fusion | flops 1114112 | bytes 8912896 | tf_op jit(solution)/shard_map/concatenate | solution.py:52
  9.1 11.7 %all-to-all-start = ((f32[32,136,256]{2,1,0:T(8,128)}), f32[32,136,256]{2,1,0:T(8,128)}, u32[]{:S(2)}, u32[]{:S(2)}) async-start(f32[32,136,256]{2,1,0:T(8,128)} %pad_maximum_fusion), calls=%async_computation | async-start | bytes 8912896 | tf_op jit(solution)/shard_map/all_to_all | solution.py:55
  20.8 102.4 %all-to-all-done = f32[32,136,256]{2,1,0:T(8,128)} async-done(((f32[32,136,256]{2,1,0:T(8,128)}), f32[32,136,256]{2,1,0:T(8,128)}, u32[]{:S(2)}, u32[]{:S(2)}) %all-to-all-start) | async-done | bytes 4456480 | tf_op jit(solution)/shard_map/all_to_all | solution.py:55
  123.3 1.0 slice_reduce_fusion.1
  124.2 0.2 dynamic-slice_reduce_fusion
  124.4 0.1 broadcast_in_dim.75
  124.5 0.0 copy-done.12
  124.5 0.6 select_reduce_fusion
  125.1 0.0 copy-start.15
  125.2 0.0 copy-start.16
  125.2 2.6 %slice.101 = f32[32,128,256]{2,1,0:T(8,128)S(1)} slice(f32[32,136,256]{2,1,0:T(8,128)} %all-to-all-done), slice={[0:32], [0:128], [0:256]} | slice | bytes 8388608 | tf_op jit(solution)/shard_map/slice | solution.py:71
  127.7 0.0 copy-done.15
  127.7 0.0 copy-done.16
  127.8 6.0 %fusion = f32[64,64,256]{2,0,1:T(8,128)S(1)} fusion(f32[64,64,256]{2,1,0:T(8,128)S(1)} %bitcast.94, pred[64,64]{1,0:T(32,128)(4,1)S(1)} %copy-done.16, pred[64,64]{1,0:T(32,128)(4,1)S(1)} %copy-done.15, f32[64,64]{1,0:T(8,128)S(1)} %select_reduce_fusion), kind=kOutput, calls=%fused_computation.1 | convolution fusion | flops 805314560 | bytes 8413184 | tf_op jit(solution)/shard_map/uv,vpn->upn/dot_general | solution.py:69
  133.7 4.4 %copy.46 = f32[64,64,256]{2,1,0:T(8,128)} copy(f32[64,64,256]{2,0,1:T(8,128)S(1)} %fusion) | data formatting | bytes 8388608 | tf_op jit(solution)/shard_map/uv,vpn->upn/dot_general | solution.py:69
  138.1 7.1 %all-to-all-start.1 = ((f32[32,128,256]{2,1,0:T(8,128)}), f32[32,128,256]{2,1,0:T(8,128)}, u32[]{:S(2)}, u32[]{:S(2)}) async-start(f32[32,128,256]{2,1,0:T(8,128)} %bitcast.92), calls=%async_computation.1 | async-start | bytes 8388608 | tf_op jit(solution)/shard_map/all_to_all | solution.py:79
  145.2 0.0 copy-done.13
  145.2 0.0 copy-done.1
  145.2 3.2 %reshape.232 = f32[2,128,1,32,64]{4,3,1,0,2:T(8,128)} reshape(bf16[256,2048]{1,0:T(8,128)(2,1)S(1)} %copy-done.1) | data formatting | bytes 3145728 | tf_op jit(solution)/shard_map/convert_element_type | solution.py:46
  148.4 1.6 convert_element_type.49
  150.0 0.8 slice-done
  150.8 2.3 copy.56
  153.1 0.0 copy-done.14
  153.1 0.0 copy-done.11
  153.1 0.2 fusion.39
  153.3 0.0 copy-done.5
  153.3 1.6 fusion.18
  154.9 0.3 fusion.38
  155.2 1.3 copy.52
  156.5 0.0 copy-start.18
  156.5 0.0 copy-start.3
  156.6 0.0 slice-start.1
  156.6 0.1 broadcast_in_dim.85
  156.6 1.3 copy.51
  157.9 0.0 copy-done.17
  157.9 0.1 broadcast_in_dim.81
  158.0 0.1 mul.97
  158.1 1.4 copy.48
  159.5 1.1 broadcast_in_dim.79
  160.6 2.6 %copy.47 = f32[128,2048]{1,0:T(8,128)} copy(f32[128,2048]{0,1:T(8,128)} %bitcast.97) | data formatting | bytes 2097152 | tf_op jit(solution)/shard_map/broadcast_in_dim | solution.py:102
  163.1 0.1 select_reduce_fusion.1
  163.2 78.8 %all-to-all-done.1 = f32[32,128,256]{2,1,0:T(8,128)} async-done(((f32[32,128,256]{2,1,0:T(8,128)}), f32[32,128,256]{2,1,0:T(8,128)}, u32[]{:S(2)}, u32[]{:S(2)}) %all-to-all-start.1) | async-done | bytes 4194336 | tf_op jit(solution)/shard_map/all_to_all | solution.py:79
  242.0 2.2 fusion.11
  244.2 0.5 fusion.8
  244.7 1.8 slice.133
  246.6 0.0 copy-done.7
  246.6 0.0 copy-done.9
  246.6 0.5 fusion.9
  247.1 1.1 pad_maximum_fusion.1
  (29 shorter events, 0.1 us)
Async XLA Ops:
  0.0 0.8 copy-start
  0.0 5.3 %copy-start.10 = (bf16[256,256]{1,0:T(8,128)(2,1)S(1)}, bf16[256,256]{1,0:T(8,128)(2,1)}, u32[]{:S(2)}) copy-start(bf16[256,256]{1,0:T(8,128)(2,1)} %param.15) | copy-start | bytes 393220
  2.4 142.8 %copy-start.13 = (f32[2,128,32]{1,2,0:T(8,128)}, f32[2,128,32]{1,2,0:T(8,128)S(1)}, u32[]{:S(2)}) copy-start(f32[2,128,32]{1,2,0:T(8,128)S(1)} %fusion.31) | copy-start | bytes 98308
  4.2 2.3 copy-start.4
  9.1 115.4 %copy-start.12 = (pred[1,64,64,64]{3,2,1,0:T(32,128)(4,1)S(1)}, pred[1,64,64,64]{3,2,1,0:T(32,128)(4,1)}, u32[]{:S(2)}) copy-start(pred[1,64,64,64]{3,2,1,0:T(32,128)(4,1)} %constant.53.clone) | copy-start | bytes 786436
  9.1 114.2 %all-to-all-start = ((f32[32,136,256]{2,1,0:T(8,128)}), f32[32,136,256]{2,1,0:T(8,128)}, u32[]{:S(2)}, u32[]{:S(2)}) async-start(f32[32,136,256]{2,1,0:T(8,128)} %pad_maximum_fusion), calls=%async_computation | async-start | bytes 8912896 | tf_op jit(solution)/shard_map/all_to_all | solution.py:55
  125.1 2.6 %copy-start.15 = (pred[64,64]{1,0:T(32,128)(4,1)S(1)}, pred[64,64]{1,0:T(32,128)(4,1)}, u32[]{:S(2)}) copy-start(pred[64,64]{1,0:T(32,128)(4,1)} %constant.60) | copy-start | bytes 12292
  125.2 2.6 %copy-start.16 = (pred[64,64]{1,0:T(32,128)(4,1)S(1)}, pred[64,64]{1,0:T(32,128)(4,1)}, u32[]{:S(2)}) copy-start(pred[64,64]{1,0:T(32,128)(4,1)} %constant.61) | copy-start | bytes 12292
  138.1 7.1 %copy-start.1 = (bf16[256,2048]{1,0:T(8,128)(2,1)S(1)}, bf16[256,2048]{1,0:T(8,128)(2,1)}, u32[]{:S(2)}) copy-start(bf16[256,2048]{1,0:T(8,128)(2,1)} %param.12) | copy-start | bytes 3145732
  138.1 103.9 %all-to-all-start.1 = ((f32[32,128,256]{2,1,0:T(8,128)}), f32[32,128,256]{2,1,0:T(8,128)}, u32[]{:S(2)}, u32[]{:S(2)}) async-start(f32[32,128,256]{2,1,0:T(8,128)} %bitcast.92), calls=%async_computation.1 | async-start | bytes 8388608 | tf_op jit(solution)/shard_map/all_to_all | solution.py:79
  148.4 2.3 slice-start
  150.0 3.1 %copy-start.14 = (f32[32,256]{1,0:T(8,128)S(1)}, f32[32,256]{1,0:T(8,128)}, u32[]{:S(2)}) copy-start(f32[32,256]{1,0:T(8,128)} %param.14) | copy-start | bytes 98308
  150.0 3.1 %copy-start.11 = (bf16[256,256]{1,0:T(8,128)(2,1)S(1)}, bf16[256,256]{1,0:T(8,128)(2,1)}, u32[]{:S(2)}) copy-start(bf16[256,256]{1,0:T(8,128)(2,1)} %param.16) | copy-start | bytes 393220
  150.0 3.3 %copy-start.5 = (bf16[2,128,32,64]{1,0,3,2:T(2,128)(2,1)S(1)}, bf16[2,128,32,64]{1,0,3,2:T(2,128)(2,1)}, u32[]{:S(2)}) copy-start(bf16[2,128,32,64]{1,0,3,2:T(2,128)(2,1)} %copy-done.4) | copy-start | bytes 3145732
  154.9 3.0 %copy-start.17 = (f32[32]{0:T(128)S(1)}, f32[32]{0:T(128)}, u32[]{:S(2)}) copy-start(f32[32]{0:T(128)} %param.17) | copy-start | bytes 388
  156.5 6.6 %copy-start.18 = (s32[32,1]{0,1:T(1,128)S(1)}, s32[32,1]{0,1:T(1,128)}, u32[]{:S(2)}) copy-start(s32[32,1]{0,1:T(1,128)} %constant.56.clone) | copy-start | bytes 388
  156.5 85.4 %copy-start.3 = (f32[1,128,1,32,64]{1,4,3,2,0:T(8,128)S(1)}, f32[1,128,1,32,64]{1,4,3,2,0:T(8,128)}, u32[]{:S(2)}) copy-start(f32[1,128,1,32,64]{1,4,3,2,0:T(8,128)} %copy.56) | copy-start | bytes 3145732
  156.6 85.4 %slice-start.1 = ((f32[2,128,32]{1,2,0:T(8,128)}), f32[1,128,32]{1,2,0:T(8,128)S(1)}, s32[]{:S(2)}) async-start(f32[2,128,32]{1,2,0:T(8,128)} %copy-done.13), calls=%async_computation.3 | async-start | bytes 32768 | tf_op jit(solution)/shard_map/slice | solution.py:83
  159.5 84.7 %copy-start.2 = (f32[256,2048]{1,0:T(8,128)S(1)}, f32[256,2048]{1,0:T(8,128)}, u32[]{:S(2)}) copy-start(f32[256,2048]{1,0:T(8,128)} %convert_element_type.49) | copy-start | bytes 6291460
  242.0 2.2 copy-start.6
  242.0 2.2 copy-start.8
  244.2 2.4 copy-start.7
  244.2 2.4 copy-start.9

commit v10 on v9

--- a/solution.py
+++ b/solution.py
@@ -47,14 +47,9 @@
     span_states = jnp.einsum(
         "ksgn,ksgqp->gqkpn", b_spans, weighted, preferred_element_type=jnp.float32
     ).reshape(head_count, rows, state_size)
-    tail = jnp.zeros((extra, state_size), jnp.float32)
-    tail = tail.at[:halves, :head_count].set(jnp.transpose(totals))
-    payload = jnp.concatenate(
-        [span_states, jnp.broadcast_to(tail[None], (head_count, extra, state_size))], axis=1
-    )
-    got = lax.all_to_all(payload, "ctx", 0, 0, tiled=True)
-    got_states = got[:, :rows].reshape(devices, per_chunk, halves, head_width, state_size)
-    all_decay = got[:, rows:rows + halves, :head_count]
+    decay_out = jnp.broadcast_to(jnp.transpose(totals)[None], (devices, halves, head_count))
+    got, all_decay = lax.all_to_all((span_states, decay_out), "ctx", 0, 0, tiled=True)
+    got_states = got.reshape(devices, per_chunk, halves, head_width, state_size)
     me = lax.axis_index("ctx")
     mine = lax.dynamic_slice_in_dim(all_decay, me * per_chunk, per_chunk, axis=2)
 
@@ -68,7 +63,7 @@
     if per_chunk == 1:
         solved = jnp.einsum(
             "uv,vpn->upn", others.reshape(devices * halves, devices * halves),
-            got[:, :rows].reshape(devices * halves, head_width, state_size),
+            got.reshape(devices * halves, head_width, state_size),
             precision=lax.Precision.HIGHEST, preferred_element_type=jnp.float32,
         ).reshape(devices, rows, state_size)
     else:

time: 249 us -> 248 us (level)
  starting transfers between devices: 18.8 us -> 23.6 us
  waiting for transfers between devices: 181 us -> 177 us
  other arithmetic: 8.58 us -> 5.16 us
  matrix products: 11.6 us -> 14.1 us
    all_to_all x1 -> x2, starting transfers between devices: 11.7 us -> 18.2 us  [on_device(): lax.all_to_all((span_states, decay_out), 'ctx', 0, 0, tiled=True)]
    all_to_all x1 -> x2, waiting for transfers between devices: 102 us -> 98.7 us  [on_device(): lax.all_to_all((span_states, decay_out), 'ctx', 0, 0, tiled=True)]
    slice x1 -> x0, local copies, waits for them, and re-layouts: 2.56 us -> none  [on_device(): got[:, :rows].reshape(devices * halves, head_width, state_size)]
    concatenate x1 -> x0, other arithmetic: 2.55 us -> none  [on_device(): jnp.concatenate([span_states, jnp.broadcast_to(tail[None], (head_count, e...]
  transfers between devices with their start and end apart: 2 -> 3, of which waited for: 2 -> 3; matrix products, arithmetic and copies ran while one was open for 7% -> 10% of each run, Pallas kernels for 0% -> 0%
where the time goes in v10:
time: 248 us
  waiting for transfers between devices  177 us (71%)
  local copies, waits for them, and re-layouts  27.4 us (11%)
  starting transfers between devices  23.6 us (10%)
  matrix products  14.1 us (6%)
  other arithmetic  5.16 us (2%)
    all_to_all x2, waiting for transfers between devices, on_device(): lax.all_to_all((span_states, decay_out), 'ctx', 0, 0, tiled=True)  98.7 us
    all_to_all x1, waiting for transfers between devices, on_device(): back = lax.all_to_all(solved, 'ctx', 0, 0, tiled=True)  78.7 us
    all_to_all x2, starting transfers between devices, on_device(): lax.all_to_all((span_states, decay_out), 'ctx', 0, 0, tiled=True)  18.2 us
    dot_general x1, matrix products, on_device(): jnp.einsum('uv,vpn->upn', others.reshape(devices * halves, devices * halv...  8.39 us
    all_to_all x1, starting transfers between devices, on_device(): back = lax.all_to_all(solved, 'ctx', 0, 0, tiled=True)  5.39 us
    broadcast_in_dim x4, local copies, waits for them, and re-layouts, on_device(): jnp.repeat(jnp.transpose(jnp.exp(cumulative), (1, 2, 0)), head_width, axi...  4.97 us
  transfers between devices with their start and end apart: 3, of which 3 were waited for; matrix products, arithmetic and copies ran while one was open for 10% of the time, Pallas kernels for 0%

profile of v10, /device:TPU:8, one launch (start us, length us, event | category | flops | bytes accessed | tf_op | source)
XLA Modules:
  0.0 248.0 jit_solution(12631484168671577387)
XLA Ops:
  0.0 0.0 copy-start
  0.0 0.8 copy-done
  0.8 0.6 reduce_window_sum.13
  1.3 0.2 slice_reduce_fusion
  1.5 0.6 broadcast_in_dim.70
  2.1 11.3 %all-to-all-start = ((f32[32,2,32]{2,1,0:T(2,128)}), f32[32,2,32]{2,1,0:T(2,128)S(1)}, u32[]{:S(2)}, u32[]{:S(2)}) async-start(f32[32,2,32]{2,1,0:T(2,128)} %broadcast_in_dim.70), calls=%async_computation | async-start | bytes 65536 | tf_op jit(solution)/shard_map/all_to_all | solution.py:51
  13.4 0.8 reshape.174
  14.2 0.1 fusion.30
  14.3 0.0 copy-start.13
  14.4 1.5 copy.57
  15.9 0.3 reshape.171
  16.1 0.0 copy-start.4
  16.2 1.1 multiply_convert_fusion.2
  17.2 0.0 copy-done.10
  17.2 0.7 convolution_bitcast_fusion.2
  17.9 2.2 copy.62
  20.2 0.0 copy-done.4
  20.2 3.2 %all-to-all-done = f32[32,2,32]{2,1,0:T(2,128)S(1)} async-done(((f32[32,2,32]{2,1,0:T(2,128)}), f32[32,2,32]{2,1,0:T(2,128)S(1)}, u32[]{:S(2)}, u32[]{:S(2)}) %all-to-all-start) | async-done | bytes 8224 | tf_op jit(solution)/shard_map/all_to_all | solution.py:51
  23.4 6.9 %all-to-all-start.1 = ((f32[32,128,256]{2,1,0:T(8,128)}), f32[32,128,256]{2,1,0:T(8,128)}, u32[]{:S(2)}, u32[]{:S(2)}) async-start(f32[32,128,256]{2,1,0:T(8,128)} %bitcast.93), calls=%async_computation.1 | async-start | bytes 8388608 | tf_op jit(solution)/shard_map/all_to_all | solution.py:51
  30.3 0.2 dynamic-slice_reduce_fusion
  30.5 0.1 broadcast_in_dim.71
  30.6 0.0 copy-done.12
  30.6 0.6 select_reduce_fusion
  31.2 95.5 %all-to-all-done.1 = f32[32,128,256]{2,1,0:T(8,128)} async-done(((f32[32,128,256]{2,1,0:T(8,128)}), f32[32,128,256]{2,1,0:T(8,128)}, u32[]{:S(2)}, u32[]{:S(2)}) %all-to-all-start.1) | async-done | bytes 4194336 | tf_op jit(solution)/shard_map/all_to_all | solution.py:51
  126.7 0.0 copy-done.15
  126.7 0.0 copy-done.16
  126.7 8.4 %fusion = f32[64,64,256]{2,0,1:T(8,128)S(1)} fusion(f32[64,64,256]{2,1,0:T(8,128)} %bitcast.16, pred[64,64]{1,0:T(32,128)(4,1)S(1)} %copy-done.16, pred[64,64]{1,0:T(32,128)(4,1)S(1)} %copy-done.15, f32[64,64]{1,0:T(8,128)S(1)} %select_reduce_fusion), kind=kOutput, calls=%fused_computation | convolution fusion | flops 805314560 | bytes 8413184 | tf_op jit(solution)/shard_map/uv,vpn->upn/dot_general | solution.py:64
  135.1 4.4 %copy.64 = f32[64,64,256]{2,1,0:T(8,128)} copy(f32[64,64,256]{2,0,1:T(8,128)S(1)} %fusion) | data formatting | bytes 8388608 | tf_op jit(solution)/shard_map/uv,vpn->upn/dot_general | solution.py:64
  139.5 5.4 %all-to-all-start.2 = ((f32[32,128,256]{2,1,0:T(8,128)}), f32[32,128,256]{2,1,0:T(8,128)}, u32[]{:S(2)}, u32[]{:S(2)}) async-start(f32[32,128,256]{2,1,0:T(8,128)} %bitcast.92), calls=%async_computation.2 | async-start | bytes 8388608 | tf_op jit(solution)/shard_map/all_to_all | solution.py:74
  144.9 0.0 copy-done.13
  145.0 0.0 copy-done.1
  145.0 3.2 %reshape.196 = f32[2,128,1,32,64]{4,3,1,0,2:T(8,128)} reshape(bf16[256,2048]{1,0:T(8,128)(2,1)S(1)} %copy-done.1) | data formatting | bytes 3145728 | tf_op jit(solution)/shard_map/convert_element_type | solution.py:46
  148.2 1.6 convert_element_type.49
  149.8 0.8 slice-done
  150.5 2.3 copy.76
  152.9 0.0 copy-done.14
  152.9 0.0 copy-done.11
  152.9 0.2 fusion.39
  153.1 0.0 copy-done.5
  153.1 1.6 fusion.18
  154.7 0.3 fusion.38
  155.0 1.3 copy.71
  156.3 0.0 copy-start.18
  156.3 0.0 copy-start.3
  156.4 0.0 slice-start.1
  156.4 0.1 broadcast_in_dim.81
  156.4 1.3 copy.70
  157.7 0.0 copy-done.17
  157.7 0.1 broadcast_in_dim.77
  157.8 0.1 mul.97
  157.9 1.4 copy.66
  159.3 1.1 broadcast_in_dim.75
  160.3 2.6 %copy.65 = f32[128,2048]{1,0:T(8,128)} copy(f32[128,2048]{0,1:T(8,128)} %bitcast.96) | data formatting | bytes 2097152 | tf_op jit(solution)/shard_map/broadcast_in_dim | solution.py:97
  162.9 0.0 copy-done.18
  163.0 0.1 copy.75
  163.0 0.1 select_reduce_fusion.1
  163.2 78.7 %all-to-all-done.2 = f32[32,128,256]{2,1,0:T(8,128)} async-done(((f32[32,128,256]{2,1,0:T(8,128)}), f32[32,128,256]{2,1,0:T(8,128)}, u32[]{:S(2)}, u32[]{:S(2)}) %all-to-all-start.2) | async-done | bytes 4194336 | tf_op jit(solution)/shard_map/all_to_all | solution.py:74
  241.8 0.0 copy-done.3
  241.8 0.0 slice-done.1
  241.9 2.2 fusion.11
  244.1 0.5 fusion.8
  244.6 1.8 slice.102
  246.4 0.5 fusion.9
  246.9 1.1 pad_maximum_fusion
  (29 shorter events, 0.2 us)
Async XLA Ops:
  0.0 0.8 copy-start
  0.0 17.2 %copy-start.10 = (bf16[256,256]{1,0:T(8,128)(2,1)S(1)}, bf16[256,256]{1,0:T(8,128)(2,1)}, u32[]{:S(2)}) copy-start(bf16[256,256]{1,0:T(8,128)(2,1)} %param.13) | copy-start | bytes 393220
  2.1 21.2 %all-to-all-start = ((f32[32,2,32]{2,1,0:T(2,128)}), f32[32,2,32]{2,1,0:T(2,128)S(1)}, u32[]{:S(2)}, u32[]{:S(2)}) async-start(f32[32,2,32]{2,1,0:T(2,128)} %broadcast_in_dim.70), calls=%async_computation | async-start | bytes 65536 | tf_op jit(solution)/shard_map/all_to_all | solution.py:51
  14.3 130.6 %copy-start.13 = (f32[2,128,32]{1,2,0:T(8,128)}, f32[2,128,32]{1,2,0:T(8,128)S(1)}, u32[]{:S(2)}) copy-start(f32[2,128,32]{1,2,0:T(8,128)S(1)} %fusion.30) | copy-start | bytes 98308
  16.1 4.0 %copy-start.4 = (bf16[2,128,32,64]{1,0,3,2:T(2,128)(2,1)}, bf16[2,128,32,64]{1,0,3,2:T(2,128)(2,1)S(1)}, u32[]{:S(2)}) copy-start(bf16[2,128,32,64]{1,0,3,2:T(2,128)(2,1)S(1)} %reshape.171) | copy-start | bytes 3145732
  23.4 7.2 %copy-start.12 = (pred[1,64,64,64]{3,2,1,0:T(32,128)(4,1)S(1)}, pred[1,64,64,64]{3,2,1,0:T(32,128)(4,1)}, u32[]{:S(2)}) copy-start(pred[1,64,64,64]{3,2,1,0:T(32,128)(4,1)} %constant.25.clone) | copy-start | bytes 786436
  23.4 103.4 %copy-start.15 = (pred[64,64]{1,0:T(32,128)(4,1)S(1)}, pred[64,64]{1,0:T(32,128)(4,1)}, u32[]{:S(2)}) copy-start(pred[64,64]{1,0:T(32,128)(4,1)} %constant.30) | copy-start | bytes 12292
  23.4 103.4 %copy-start.16 = (pred[64,64]{1,0:T(32,128)(4,1)S(1)}, pred[64,64]{1,0:T(32,128)(4,1)}, u32[]{:S(2)}) copy-start(pred[64,64]{1,0:T(32,128)(4,1)} %constant.31) | copy-start | bytes 12292
  23.4 103.4 %all-to-all-start.1 = ((f32[32,128,256]{2,1,0:T(8,128)}), f32[32,128,256]{2,1,0:T(8,128)}, u32[]{:S(2)}, u32[]{:S(2)}) async-start(f32[32,128,256]{2,1,0:T(8,128)} %bitcast.93), calls=%async_computation.1 | async-start | bytes 8388608 | tf_op jit(solution)/shard_map/all_to_all | solution.py:51
  139.5 5.4 %copy-start.1 = (bf16[256,2048]{1,0:T(8,128)(2,1)S(1)}, bf16[256,2048]{1,0:T(8,128)(2,1)}, u32[]{:S(2)}) copy-start(bf16[256,2048]{1,0:T(8,128)(2,1)} %param.10) | copy-start | bytes 3145732
  139.5 102.3 %all-to-all-start.2 = ((f32[32,128,256]{2,1,0:T(8,128)}), f32[32,128,256]{2,1,0:T(8,128)}, u32[]{:S(2)}, u32[]{:S(2)}) async-start(f32[32,128,256]{2,1,0:T(8,128)} %bitcast.92), calls=%async_computation.2 | async-start | bytes 8388608 | tf_op jit(solution)/shard_map/all_to_all | solution.py:74
  148.2 2.3 slice-start
  149.8 3.1 %copy-start.14 = (f32[32,256]{1,0:T(8,128)S(1)}, f32[32,256]{1,0:T(8,128)}, u32[]{:S(2)}) copy-start(f32[32,256]{1,0:T(8,128)} %param.12) | copy-start | bytes 98308
  149.8 3.1 %copy-start.11 = (bf16[256,256]{1,0:T(8,128)(2,1)S(1)}, bf16[256,256]{1,0:T(8,128)(2,1)}, u32[]{:S(2)}) copy-start(bf16[256,256]{1,0:T(8,128)(2,1)} %param.14) | copy-start | bytes 393220
  149.8 3.3 %copy-start.5 = (bf16[2,128,32,64]{1,0,3,2:T(2,128)(2,1)S(1)}, bf16[2,128,32,64]{1,0,3,2:T(2,128)(2,1)}, u32[]{:S(2)}) copy-start(bf16[2,128,32,64]{1,0,3,2:T(2,128)(2,1)} %copy-done.4) | copy-start | bytes 3145732
  154.7 3.0 %copy-start.17 = (f32[32]{0:T(128)S(1)}, f32[32]{0:T(128)}, u32[]{:S(2)}) copy-start(f32[32]{0:T(128)} %param.15) | copy-start | bytes 388
  156.3 6.6 %copy-start.18 = (s32[32,1]{0,1:T(1,128)S(1)}, s32[32,1]{0,1:T(1,128)}, u32[]{:S(2)}) copy-start(s32[32,1]{0,1:T(1,128)} %constant.28.clone) | copy-start | bytes 388
  156.3 85.5 %copy-start.3 = (f32[1,128,1,32,64]{1,4,3,2,0:T(8,128)S(1)}, f32[1,128,1,32,64]{1,4,3,2,0:T(8,128)}, u32[]{:S(2)}) copy-start(f32[1,128,1,32,64]{1,4,3,2,0:T(8,128)} %copy.76) | copy-start | bytes 3145732
  156.4 85.5 %slice-start.1 = ((f32[2,128,32]{1,2,0:T(8,128)}), f32[1,128,32]{1,2,0:T(8,128)S(1)}, s32[]{:S(2)}) async-start(f32[2,128,32]{1,2,0:T(8,128)} %copy-done.13), calls=%async_computation.4 | async-start | bytes 32768 | tf_op jit(solution)/shard_map/slice | solution.py:78
  159.3 84.8 %copy-start.2 = (f32[256,2048]{1,0:T(8,128)S(1)}, f32[256,2048]{1,0:T(8,128)}, u32[]{:S(2)}) copy-start(f32[256,2048]{1,0:T(8,128)} %convert_element_type.49) | copy-start | bytes 6291460
  241.9 2.2 copy-start.6
  241.9 2.2 copy-start.8
  244.0 2.4 copy-start.7
  244.0 2.4 copy-start.9

commit v11 on v10

--- a/solution.py
+++ b/solution.py
@@ -77,11 +77,11 @@
     own_front = jnp.einsum(
         "sgn,sgqp->gqpn", b_spans[0], weighted[0], preferred_element_type=jnp.float32
     ).reshape(head_count, head_width, state_size)
-    state_halves = [
-        back[:, :head_width].astype(jnp.bfloat16).reshape(head_count * head_width, state_size),
-        (back[:, head_width:rows] + gain[:, None, None] * own_front)
-        .astype(jnp.bfloat16).reshape(head_count * head_width, state_size),
-    ]
+    own_gain = jnp.stack([jnp.zeros_like(gain), gain], axis=1)[:, :, None, None]
+    entering = back.reshape(head_count, halves, head_width, state_size) + own_gain * own_front[:, None]
+    state_bf = jnp.transpose(entering, (1, 0, 2, 3)).astype(jnp.bfloat16).reshape(
+        halves, head_count * head_width, state_size
+    )
 
     scores = jnp.einsum("ktgn,ksgn->gkts", c_spans, b_spans, preferred_element_type=jnp.float32)
     causal = jnp.arange(SPAN)[:, None] >= jnp.arange(SPAN)[None, :]
@@ -97,22 +97,18 @@
     decay_in = jnp.repeat(jnp.transpose(jnp.exp(cumulative), (1, 2, 0)), head_width, axis=2)
     skip = jnp.repeat(skip_gain, head_width)[None, :]
     inputs = features.reshape(halves, SPAN, head_count * head_width).astype(jnp.float32)
-    per_group_width = per_group * head_width
-    outs = []
-    for k in range(halves):
-        state_part = jnp.concatenate(
-            [
-                jnp.dot(
-                    c_spans[k, :, g],
-                    state_halves[k][g * per_group_width:(g + 1) * per_group_width].T,
-                    preferred_element_type=jnp.float32,
-                )
-                for g in range(group_count)
-            ],
-            axis=1,
+    if group_count == 1:
+        state_part = jnp.einsum(
+            "ktn,kmn->ktm", c_spans[:, :, 0], state_bf, preferred_element_type=jnp.float32
         )
-        outs.append(diagonal_part[k] + state_part * decay_in[k] + skip * inputs[k])
-    return jnp.concatenate(outs, axis=0).astype(jnp.bfloat16)
+    else:
+        state_part = jnp.einsum(
+            "ktgn,kgmn->ktgm", c_spans,
+            state_bf.reshape(halves, group_count, per_group * head_width, state_size),
+            preferred_element_type=jnp.float32,
+        ).reshape(halves, SPAN, head_count * head_width)
+    output_rows = diagonal_part + state_part * decay_in + skip[None] * inputs
+    return output_rows.reshape(tok_rows, head_count * head_width).astype(jnp.bfloat16)
 
 
 def solution(mesh):

time: 248 us -> 249 us (level)
  local copies, waits for them, and re-layouts: 27.4 us -> 23.7 us
    broadcast_in_dim x4 -> x1, local copies, waits for them, and re-layouts: 4.97 us -> 0.14 us  [on_device(): jnp.repeat(jnp.transpose(jnp.exp(cumulative), (1, 2, 0)), head_width, axi...]
    reshape x0 -> x2, local copies, waits for them, and re-layouts: none -> 3.7 us  [the longest x1 1.86 us: on_device(): diagonal_part = jnp.einsum('gqkts,ksgqp->ktgqp', weights, grouped_inputs,...]
    squeeze x2 -> x0, local copies, waits for them, and re-layouts: 2.72 us -> none  [on_device(): outs.append(diagonal_part[k] + state_part * decay_in[k] + skip * inputs[k])]
  transfers between devices with their start and end apart: 3 -> 3, of which waited for: 3 -> 3; matrix products, arithmetic and copies ran while one was open for 10% -> 9% of each run, Pallas kernels for 0% -> 0%
where the time goes in v11:
time: 249 us
  waiting for transfers between devices  179 us (72%)
  local copies, waits for them, and re-layouts  23.7 us (10%)
  starting transfers between devices  23.7 us (10%)
  matrix products  15.2 us (6%)
  other arithmetic  6.88 us (3%)
    all_to_all x2, waiting for transfers between devices, on_device(): lax.all_to_all((span_states, decay_out), 'ctx', 0, 0, tiled=True)  98.7 us
    all_to_all x1, waiting for transfers between devices, on_device(): back = lax.all_to_all(solved, 'ctx', 0, 0, tiled=True)  80.5 us
    all_to_all x2, starting transfers between devices, on_device(): lax.all_to_all((span_states, decay_out), 'ctx', 0, 0, tiled=True)  18.3 us
    dot_general x1, matrix products, on_device(): jnp.einsum('uv,vpn->upn', others.reshape(devices * halves, devices * halv...  8.39 us
    all_to_all x1, starting transfers between devices, on_device(): back = lax.all_to_all(solved, 'ctx', 0, 0, tiled=True)  5.38 us
  transfers between devices with their start and end apart: 3, of which 3 were waited for; matrix products, arithmetic and copies ran while one was open for 9% of the time, Pallas kernels for 0%

profile of v11, /device:TPU:8, one launch (start us, length us, event | category | flops | bytes accessed | tf_op | source)
XLA Modules:
  0.0 248.9 jit_solution(8711991772730559232)
XLA Ops:
  0.0 0.0 copy-start
  0.0 0.8 copy_bitcast_fusion.1
  0.8 0.6 reduce_window_sum.13
  1.4 0.2 slice_reduce_fusion
  1.5 0.6 broadcast_in_dim.64
  2.2 11.3 %all-to-all-start = ((f32[32,2,32]{2,1,0:T(2,128)}), f32[32,2,32]{2,1,0:T(2,128)S(1)}, u32[]{:S(2)}, u32[]{:S(2)}) async-start(f32[32,2,32]{2,1,0:T(2,128)} %broadcast_in_dim.64), calls=%async_computation | async-start | bytes 65536 | tf_op jit(solution)/shard_map/all_to_all | solution.py:51
  13.5 0.8 reshape.168
  14.3 0.1 fusion.24
  14.4 0.0 copy-start.8
  14.4 1.5 copy.70
  15.9 0.0 copy-start.6
  15.9 0.3 reshape.164
  16.2 0.0 copy-start.5
  16.2 1.1 multiply_convert_fusion.2
  17.3 0.0 copy-done.6
  17.3 0.7 convolution_bitcast_fusion.1
  18.0 0.0 copy-done.5
  18.0 2.2 copy.75
  20.2 3.1 %all-to-all-done = f32[32,2,32]{2,1,0:T(2,128)S(1)} async-done(((f32[32,2,32]{2,1,0:T(2,128)}), f32[32,2,32]{2,1,0:T(2,128)S(1)}, u32[]{:S(2)}, u32[]{:S(2)}) %all-to-all-start) | async-done | bytes 8224 | tf_op jit(solution)/shard_map/all_to_all | solution.py:51
  23.4 7.0 %all-to-all-start.1 = ((f32[32,128,256]{2,1,0:T(8,128)}), f32[32,128,256]{2,1,0:T(8,128)}, u32[]{:S(2)}, u32[]{:S(2)}) async-start(f32[32,128,256]{2,1,0:T(8,128)} %bitcast.85), calls=%async_computation.1 | async-start | bytes 8388608 | tf_op jit(solution)/shard_map/all_to_all | solution.py:51
  30.3 0.2 dynamic-slice_reduce_fusion
  30.5 0.1 broadcast_in_dim.65
  30.6 0.0 copy-done.7
  30.6 0.6 select_reduce_fusion
  31.2 95.6 %all-to-all-done.1 = f32[32,128,256]{2,1,0:T(8,128)} async-done(((f32[32,128,256]{2,1,0:T(8,128)}), f32[32,128,256]{2,1,0:T(8,128)}, u32[]{:S(2)}, u32[]{:S(2)}) %all-to-all-start.1) | async-done | bytes 4194336 | tf_op jit(solution)/shard_map/all_to_all | solution.py:51
  126.8 0.0 copy-done.10
  126.8 0.0 copy-done.11
  126.8 8.4 %fusion = f32[64,64,256]{2,0,1:T(8,128)S(1)} fusion(f32[64,64,256]{2,1,0:T(8,128)} %bitcast.16, pred[64,64]{1,0:T(32,128)(4,1)S(1)} %copy-done.11, pred[64,64]{1,0:T(32,128)(4,1)S(1)} %copy-done.10, f32[64,64]{1,0:T(8,128)S(1)} %select_reduce_fusion), kind=kOutput, calls=%fused_computation | convolution fusion | flops 805314560 | bytes 8413184 | tf_op jit(solution)/shard_map/uv,vpn->upn/dot_general | solution.py:64
  135.2 4.4 %copy.77 = f32[64,64,256]{2,1,0:T(8,128)} copy(f32[64,64,256]{2,0,1:T(8,128)S(1)} %fusion) | data formatting | bytes 8388608 | tf_op jit(solution)/shard_map/uv,vpn->upn/dot_general | solution.py:64
  139.6 5.4 %all-to-all-start.2 = ((f32[32,128,256]{2,1,0:T(8,128)}), f32[32,128,256]{2,1,0:T(8,128)}, u32[]{:S(2)}, u32[]{:S(2)}) async-start(f32[32,128,256]{2,1,0:T(8,128)} %bitcast.84), calls=%async_computation.2 | async-start | bytes 8388608 | tf_op jit(solution)/shard_map/all_to_all | solution.py:74
  145.0 0.0 copy-done.8
  145.0 0.0 copy-done.1
  145.0 3.2 %reshape.192 = f32[2,128,1,32,64]{4,3,1,0,2:T(8,128)} reshape(bf16[256,2048]{1,0:T(8,128)(2,1)S(1)} %copy-done.1) | data formatting | bytes 3145728 | tf_op jit(solution)/shard_map/convert_element_type | solution.py:46
  148.3 1.6 convert_element_type.67
  149.9 1.6 slice-done
  151.4 1.3 copy.90
  152.8 0.0 copy-done.9
  152.8 0.0 copy-done
  152.8 0.2 fusion.32
  153.0 3.6 %fusion.6 = f32[2,32,128,64]{2,3,1,0:T(8,128)S(1)} fusion(f32[32,2,128]{2,0,1:T(8,128)S(1)} %copy_bitcast_fusion, f32[32,2,128]{2,0,1:T(8,128)S(1)} %reduce_window_sum.13, f32[2,128,128]{2,1,0:T(8,128)S(1)} %fusion.32, pred[128,128]{1,0:T(8,128)(4,1)S(1)} %iota_compare_fusion, bf16[2,128,32,64]{1,0,3,2:T(2,128)(2,1)} %copy-done.5), kind=kOutput, calls=%fused_computation.10 | convolution fusion | flops 139460608 | bytes 3358720 | tf_op jit(solution)/shard_map/gqkts,ksgqp->ktgqp/dot_general | solution.py:94
  156.6 1.9 copy.84
  158.5 0.1 broadcast_in_dim.72
  158.6 0.0 copy-start.12
  158.6 0.0 copy-start.13
  158.6 0.0 slice-start.1
  158.6 1.8 copy.83
  160.5 0.0 copy-done.12
  160.5 0.1 broadcast_in_dim.73
  160.6 0.1 mul.98
  160.6 0.0 copy-done.13
  160.6 0.0 slice-done.1
  160.6 0.4 fusion.17
  161.1 0.1 copy.88
  161.2 0.1 select_reduce_fusion.1
  161.3 0.1 copy.89
  161.4 0.1 stack.4.clone
  161.5 80.5 %all-to-all-done.2 = f32[32,128,256]{2,1,0:T(8,128)} async-done(((f32[32,128,256]{2,1,0:T(8,128)}), f32[32,128,256]{2,1,0:T(8,128)}, u32[]{:S(2)}, u32[]{:S(2)}) %all-to-all-start.2) | async-done | bytes 4194336 | tf_op jit(solution)/shard_map/all_to_all | solution.py:74
  242.0 2.8 %fusion.7 = bf16[2,32,64,256]{3,2,0,1:T(8,128)(2,1)S(1)} fusion(f32[32,2,64,256]{3,2,1,0:T(8,128)} %bitcast.18, f32[32,64,256]{2,1,0:T(8,128)S(1)} %fusion.17, f32[32,2]{1,0:T(8,128)S(1)} %stack.4.clone), kind=kLoop, calls=%fused_computation.11 | loop fusion | flops 3145728 | bytes 8388864 | tf_op jit(solution)/shard_map/convert_element_type | solution.py:82
  244.8 0.0 copy-start.2
  244.8 0.0 copy-start.3
  244.8 0.2 copy.82
  245.1 1.3 copy-done.2
  246.4 0.6 copy-done.3
  247.0 1.9 fusion.5
  (15 shorter events, 0.1 us)
Async XLA Ops:
  0.0 152.8 %copy-start = (bf16[256,256]{1,0:T(8,128)(2,1)S(1)}, bf16[256,256]{1,0:T(8,128)(2,1)}, u32[]{:S(2)}) copy-start(bf16[256,256]{1,0:T(8,128)(2,1)} %param.14) | copy-start | bytes 393220
  2.2 21.2 %all-to-all-start = ((f32[32,2,32]{2,1,0:T(2,128)}), f32[32,2,32]{2,1,0:T(2,128)S(1)}, u32[]{:S(2)}, u32[]{:S(2)}) async-start(f32[32,2,32]{2,1,0:T(2,128)} %broadcast_in_dim.64), calls=%async_computation | async-start | bytes 65536 | tf_op jit(solution)/shard_map/all_to_all | solution.py:51
  14.4 130.7 %copy-start.8 = (f32[2,128,32]{1,2,0:T(8,128)}, f32[2,128,32]{1,2,0:T(8,128)S(1)}, u32[]{:S(2)}) copy-start(f32[2,128,32]{1,2,0:T(8,128)S(1)} %fusion.24) | copy-start | bytes 98308
  15.9 1.4 copy-start.6
  16.2 1.8 copy-start.5
  23.3 7.3 %copy-start.7 = (pred[1,64,64,64]{3,2,1,0:T(32,128)(4,1)S(1)}, pred[1,64,64,64]{3,2,1,0:T(32,128)(4,1)}, u32[]{:S(2)}) copy-start(pred[1,64,64,64]{3,2,1,0:T(32,128)(4,1)} %constant.26.clone) | copy-start | bytes 786436
  23.4 103.5 %copy-start.10 = (pred[64,64]{1,0:T(32,128)(4,1)S(1)}, pred[64,64]{1,0:T(32,128)(4,1)}, u32[]{:S(2)}) copy-start(pred[64,64]{1,0:T(32,128)(4,1)} %constant.33) | copy-start | bytes 12292
  23.4 103.5 %copy-start.11 = (pred[64,64]{1,0:T(32,128)(4,1)S(1)}, pred[64,64]{1,0:T(32,128)(4,1)}, u32[]{:S(2)}) copy-start(pred[64,64]{1,0:T(32,128)(4,1)} %constant.34) | copy-start | bytes 12292
  23.4 103.5 %all-to-all-start.1 = ((f32[32,128,256]{2,1,0:T(8,128)}), f32[32,128,256]{2,1,0:T(8,128)}, u32[]{:S(2)}, u32[]{:S(2)}) async-start(f32[32,128,256]{2,1,0:T(8,128)} %bitcast.85), calls=%async_computation.1 | async-start | bytes 8388608 | tf_op jit(solution)/shard_map/all_to_all | solution.py:51
  139.6 5.4 %copy-start.1 = (bf16[256,2048]{1,0:T(8,128)(2,1)S(1)}, bf16[256,2048]{1,0:T(8,128)(2,1)}, u32[]{:S(2)}) copy-start(bf16[256,2048]{1,0:T(8,128)(2,1)} %param.10) | copy-start | bytes 3145732
  139.6 102.3 %all-to-all-start.2 = ((f32[32,128,256]{2,1,0:T(8,128)}), f32[32,128,256]{2,1,0:T(8,128)}, u32[]{:S(2)}, u32[]{:S(2)}) async-start(f32[32,128,256]{2,1,0:T(8,128)} %bitcast.84), calls=%async_computation.2 | async-start | bytes 8388608 | tf_op jit(solution)/shard_map/all_to_all | solution.py:74
  149.9 1.6 slice-start
  151.4 1.3 copy-start.9
  158.6 1.9 copy-start.12
  158.6 2.0 copy-start.13
  158.6 2.0 slice-start.1
  242.0 3.1 %copy-start.4 = (f32[2,128,2048]{2,1,0:T(8,128)S(1)}, f32[2,128,2048]{2,1,0:T(8,128)}, u32[]{:S(2)}) copy-start(f32[2,128,2048]{2,1,0:T(8,128)} %copy.83) | copy-start | bytes 6291460
  244.8 1.6 copy-start.2
  244.8 2.2 copy-start.3
